TPU v7x, 256 devices: a whole 4x4x8 slice. The times are simulated.
256 devices in a mesh: dp: 16 (over y_lo, x, core), tensor: 16 (over y_hi, z).
Axes of the slice: x: 4, y: 4 (y_hi: 2, y_lo: 2; y = y_hi * 2 + y_lo), z: 8, core: 2. Of those that a mesh axis runs over, the one named last changes fastest.
Arguments:
- tokens: bfloat16 [12288, 8192], P(('dp', 'tensor')), may hold values from -6 to 6
- q_weight: bfloat16 [8192, 8192], P(None, 'tensor'), may hold values from -0.0625 to 0.0625
- pool_down: bfloat16 [128, 64, 8192], P('dp', None, 'tensor'), may hold values from -0.0625 to 0.0625
- pool_up: bfloat16 [128, 64, 8192], P('dp', None, 'tensor'), may hold values from -0.75 to 0.75
- block_units: int32 [16, 8], replicated, may hold values from 1 to 24, 48 in all within a row
- adapter_ids: int32 [16, 8], replicated, may hold values from 0 to 127, as said below
- location: int32 [128], replicated, may hold values from 0 to 127, as said below
Outputs:
- queries: bfloat16 [12288, 8192], P('dp', 'tensor')
Inputs may be any that keep to these rules, and one draw needn't show every extreme that they name: `adapter_ids`: the 8 adapters of one group lie in pool rows of 8 different dp shards (row location[a] lies on shard location[a] // 8). A permutation: adapter a is held in pool row location[a]. `block_units`: each group's blocks sum to 48; the largest is exactly 24.
All inputs are finite; a program needn't handle non-finite values.
Results may differ from a plain program's by a relative error of at most 0.0029.
Values may be sent and summed in bfloat16 or wider, within the bound.
No kernel may reach another device: no remote copies, remote signals or barrier semaphores. Data moves between devices by JAX's collectives and lax.ppermute only.
A program may use at most 128 MiB of HBM per device.

v0:
```python
import jax
import jax.numpy as jnp
from jax import lax
from jax.sharding import PartitionSpec as P

adapter_scale = 0.5


def tenant_mask(pool_unit_row, group_rows, tenants):
    block_ends = 16 * jnp.cumsum(pool_unit_row)
    positions = jnp.arange(group_rows, dtype=jnp.int32)
    tenant_index = jnp.sum((positions[:, None] >= block_ends[None, :]).astype(jnp.int32), axis=1)
    return tenant_index[:, None] == jnp.arange(tenants, dtype=jnp.int32)[None, :]


def select_rows(one_hot, table):
    picked = jnp.einsum(
        "ks,srd->krd", one_hot.astype(jnp.bfloat16), table, preferred_element_type=jnp.float32
    )
    return picked.astype(jnp.bfloat16)


def on_device(tokens, q_weight, pool_down, pool_up, block_units, adapter_ids, location):
    my_group = lax.axis_index("dp")
    tenants = adapter_ids.shape[1]
    rank_size = pool_down.shape[1]
    local_width = pool_down.shape[2]
    columns = q_weight.shape[1]
    pool_total = location.shape[0]
    id_hits = adapter_ids[:, :, None] == jnp.arange(pool_total, dtype=jnp.int32)[None, None, :]
    slot_ids = jnp.sum(jnp.where(id_hits, location[None, None, :], 0), axis=2)
    my_slots = lax.dynamic_index_in_dim(slot_ids, my_group, 0, keepdims=False)
    whole_down, whole_up = (
        lax.all_gather(pool_down, "dp", axis=0, tiled=True),
        lax.all_gather(pool_up, "dp", axis=0, tiled=True),
    )
    pick_rows = my_slots[:, None] == jnp.arange(pool_total, dtype=jnp.int32)[None, :]
    panels_down = select_rows(pick_rows, whole_down)
    panels_up = select_rows(pick_rows, whole_up)
    down_flat = panels_down.reshape(tenants * rank_size, local_width)
    up_flat = panels_up.reshape(tenants * rank_size, columns)
    width_start = lax.axis_index("tensor") * local_width
    row_block = lax.all_gather(tokens, "tensor", axis=0, tiled=True)
    base_projection = jnp.dot(row_block, q_weight, preferred_element_type=jnp.float32)
    local_cols = lax.dynamic_slice_in_dim(row_block, width_start, local_width, 1)
    wide_part = lax.dot_general(
        local_cols, down_flat, (((1,), (1,)), ((), ())), preferred_element_type=jnp.float32
    )
    combined = jnp.concatenate([base_projection, wide_part], axis=1)
    group_rows = combined.shape[0]
    base_projection = combined[:, :columns]
    wide_part = combined[:, columns:].reshape(group_rows, tenants, rank_size)
    pool_unit_row = lax.dynamic_index_in_dim(block_units, my_group, 0, keepdims=False)
    tenant_masks = tenant_mask(pool_unit_row, group_rows, tenants)
    partial_low = jnp.sum(
        jnp.where(tenant_masks[:, :, None], wide_part, jnp.zeros((), jnp.float32)), axis=1
    )
    packed = partial_low.reshape(group_rows * rank_size // 128, 128)
    low_rank = lax.psum(packed, "tensor").astype(jnp.bfloat16)
    low_rank = low_rank.reshape(group_rows, rank_size)
    low_wide = jnp.where(
        tenant_masks[:, :, None], low_rank[:, None, :], jnp.zeros((), jnp.bfloat16)
    )
    adapter_contribution = jnp.dot(
        low_wide.reshape(group_rows, tenants * rank_size),
        up_flat,
        preferred_element_type=jnp.float32,
    )
    return (base_projection + adapter_scale * adapter_contribution).astype(jnp.bfloat16)


def solution(mesh):
    placed = (
        P(("dp", "tensor"), None),
        P(None, "tensor"),
        P("dp", None, "tensor"),
        P("dp", None, "tensor"),
        P(),
        P(),
        P(),
    )
    return jax.shard_map(
        on_device, mesh=mesh, in_specs=placed, out_specs=P("dp", "tensor"), check_vma=False
    )
```

profile of v0, /device:TPU:2, one launch (start us, length us, event | category | flops | bytes accessed | tf_op | source)
XLA Modules:
  0.0 403.1 jit_solution(1845596998475962294)
XLA Ops:
  6.5 0.0 copy-start
  6.5 0.7 all-gather.6.cloned.1.call-update
  7.3 0.0 all-gather.8.cloned.1.call-start
  7.3 0.7 all-gather.8.cloned.1.call-update
  8.0 0.0 all-gather.4.cloned.1.call-start
  8.1 0.7 all-gather.4.cloned.1.call-update
  8.7 0.8 copy.18
  9.5 0.2 dynamic-slice_reduce_fusion
  9.7 0.2 reduce-window.8
  9.9 1.1 select_reduce_fusion.1
  11.0 0.1 convert_reduce_fusion
  11.1 55.6 %all-gather.6.cloned.1.call-done = bf16[128,64,512]{2,1,0:T(8,128)(2,1)} async-done(((bf16[8,64,512]{2,1,0:T(8,128)(2,1)}), bf16[128,64,512]{2,1,0:T(8,128)(2,1)}) %all-gather.6.cloned.1.call-update) | async-done | bytes 8388624 | tf_op jit(solution)/shard_map/all_gather | solution.py:34
  66.7 12.2 %fusion.6 = bf16[8,64,512]{2,0,1:T(8,128)(2,1)S(1)} fusion(bf16[128,64,512]{2,1,0:T(8,128)(2,1)} %all-gather.6.cloned.1.call-done, s32[8]{0:T(128)S(1)} %fusion.27), kind=kOutput, calls=%fused_computation.8 | convolution fusion | flops 67372032 | bytes 8912928 | tf_op jit(solution)/shard_map/ks,srd->krd/dot_general | solution.py:17
  78.8 45.2 %all-gather.8.cloned.1.call-done = bf16[128,64,512]{2,1,0:T(8,128)(2,1)} async-done(((bf16[8,64,512]{2,1,0:T(8,128)(2,1)}), bf16[128,64,512]{2,1,0:T(8,128)(2,1)}) %all-gather.8.cloned.1.call-update) | async-done | bytes 8388624 | tf_op jit(solution)/shard_map/all_gather | solution.py:35
  124.0 12.3 %fusion.9 = bf16[8,64,512]{2,0,1:T(8,128)(2,1)S(1)} fusion(bf16[128,64,512]{2,1,0:T(8,128)(2,1)} %all-gather.8.cloned.1.call-done, s32[8]{0:T(128)S(1)} %fusion.27), kind=kOutput, calls=%fused_computation.9 | convolution fusion | flops 67372032 | bytes 8912928 | tf_op jit(solution)/shard_map/ks,srd->krd/dot_general | solution.py:17
  136.4 169.6 %all-gather.4.cloned.1.call-done = bf16[768,8192]{1,0:T(8,128)(2,1)} async-done(((bf16[48,8192]{1,0:T(8,128)(2,1)}), bf16[768,8192]{1,0:T(8,128)(2,1)}) %all-gather.4.cloned.1.call-update) | async-done | bytes 12582928 | tf_op jit(solution)/shard_map/all_gather | solution.py:43
  306.0 1.8 select_reduce_fusion
  307.8 0.2 copy.21
  308.0 0.1 reshape.63
  308.1 74.8 %all-reduce.1 = bf16[384,128]{1,0:T(8,128)(2,1)S(1)} all-reduce(f32[384,128]{1,0:T(8,128)S(1)} %reshape.63), channel_id=1, replica_groups=mesh['dp'=16,'tensor'=16] {'tensor'}, use_global_device_ids=true, to_apply=%region_4.5 | all-reduce | flops 49152 | bytes 294912 | tf_op jit(solution)/shard_map/psum | solution.py:59
  382.9 0.1 broadcast_in_dim.59
  383.0 0.1 copy.22
  383.1 0.6 fusion.13
  383.8 12.8 %fusion.5 = bf16[768,512]{1,0:T(8,128)(2,1)} fusion(f32[768,512,1]{1,0,2:T(8,128)S(1)} %fusion.13, bf16[768,8192]{1,0:T(8,128)(2,1)} %all-gather.4.cloned.1.call-done, bf16[8192,512]{1,0:T(8,128)(2,1)} %param.8), kind=kOutput, calls=%fused_computation.6 | convolution fusion | flops 6443630592 | bytes 23330816 | tf_op jit(solution)/shard_map/dot_general | solution.py:44
  (5 shorter events, 0.0 us)
Async XLA Ops:
  6.5 3.0 copy-start
  6.5 60.1 %all-gather.6.cloned.1.call-start = ((), (), s32[]{:S(2)}) async-start(), calls=%async_computation.1 | async-start | bytes 8912896 | tf_op jit(solution)/shard_map/all_gather | solution.py:34
  7.3 116.8 %all-gather.8.cloned.1.call-start = ((), (), s32[]{:S(2)}) async-start(), calls=%async_computation.2 | async-start | bytes 8912896 | tf_op jit(solution)/shard_map/all_gather | solution.py:35
  8.0 298.0 %all-gather.4.cloned.1.call-start = ((), (), s32[]{:S(2)}) async-start(), calls=%async_computation | async-start | bytes 13369344 | tf_op jit(solution)/shard_map/all_gather | solution.py:43
Sparse Core Ops, SparseCore 0:
  9.2 57.4 all-gather.5
  68.5 55.4 all-gather.7
  126.6 179.3 all-gather.3
where the time goes:
time: 403 us
  waiting for transfers between devices  272 us (67%)
  blocking collectives  74.8 us (19%)
  matrix products  39.7 us (10%)
  between operations  13.2 us (3%)
    all_gather x1, waiting for transfers between devices, on_device(): row_block = lax.all_gather(tokens, 'tensor', axis=0, tiled=True)  170 us
    psum x1, blocking collectives, on_device(): low_rank = lax.psum(packed, 'tensor').astype(jnp.bfloat16)  74.8 us
    all_gather x1, waiting for transfers between devices, on_device(): lax.all_gather(pool_down, 'dp', axis=0, tiled=True)  55.6 us
    all_gather x1, waiting for transfers between devices, on_device(): lax.all_gather(pool_up, 'dp', axis=0, tiled=True)  45.2 us
    dot_general x2, matrix products, select_rows(): jnp.einsum('ks,srd->krd', one_hot.astype(jnp.bfloat16), table, preferred_...  24.5 us
    dot_general x1, matrix products, on_device(): jnp.dot(row_block, q_weight, preferred_element_type=jnp.float32)  12.8 us
  transfers between devices with their start and end apart: 3, of which 3 were waited for; matrix products, arithmetic and copies ran while one was open for 7% of the time, Pallas kernels for 0%

commit v1 on v0

v1 whole, which is shorter than its diff:
```python
import jax
import jax.numpy as jnp
from jax import lax
from jax.sharding import PartitionSpec as P

adapter_scale = 0.5


def tenant_mask(pool_unit_row, group_rows, tenants):
    block_ends = 16 * jnp.cumsum(pool_unit_row)
    positions = jnp.arange(group_rows, dtype=jnp.int32)
    tenant_index = jnp.sum((positions[:, None] >= block_ends[None, :]).astype(jnp.int32), axis=1)
    return tenant_index[:, None] == jnp.arange(tenants, dtype=jnp.int32)[None, :]


def on_device(tokens, q_weight, pool_down, pool_up, block_units, adapter_ids, location):
    my_group = lax.axis_index("dp")
    groups = adapter_ids.shape[0]
    tenants = adapter_ids.shape[1]
    pool_dev = pool_down.shape[0]
    rank_size = pool_down.shape[1]
    local_width = pool_down.shape[2]
    columns = q_weight.shape[1]

    slot_ids = jnp.take(location, adapter_ids, axis=0)
    slot_shard = slot_ids // pool_dev
    slot_row = slot_ids % pool_dev

    from_me = slot_shard == my_group
    send_row = jnp.sum(jnp.where(from_me, slot_row, 0), axis=1)
    both = jnp.concatenate([pool_down, pool_up], axis=1)
    send = jnp.take(both, send_row, axis=0)
    recv = lax.all_to_all(send, "dp", 0, 0, tiled=True)
    my_src = lax.dynamic_index_in_dim(slot_shard, my_group, 0, keepdims=False)
    panels = jnp.take(recv, my_src, axis=0)
    down_flat = panels[:, :rank_size, :].reshape(tenants * rank_size, local_width)
    up_flat = panels[:, rank_size:, :].reshape(tenants * rank_size, columns)

    width_start = lax.axis_index("tensor") * local_width
    row_block = lax.all_gather(tokens, "tensor", axis=0, tiled=True)
    base_projection = jnp.dot(row_block, q_weight, preferred_element_type=jnp.float32)
    local_cols = lax.dynamic_slice_in_dim(row_block, width_start, local_width, 1)
    wide_part = lax.dot_general(
        local_cols, down_flat, (((1,), (1,)), ((), ())), preferred_element_type=jnp.float32
    )
    group_rows = wide_part.shape[0]
    wide_part = wide_part.reshape(group_rows, tenants, rank_size)
    pool_unit_row = lax.dynamic_index_in_dim(block_units, my_group, 0, keepdims=False)
    tenant_masks = tenant_mask(pool_unit_row, group_rows, tenants)
    partial_low = jnp.sum(
        jnp.where(tenant_masks[:, :, None], wide_part, jnp.zeros((), jnp.float32)), axis=1
    )
    low_part = lax.psum_scatter(partial_low, "tensor", scatter_dimension=0, tiled=True)
    low_rank = lax.all_gather(low_part, "tensor", axis=0, tiled=True).astype(jnp.bfloat16)
    low_wide = jnp.where(
        tenant_masks[:, :, None], low_rank[:, None, :], jnp.zeros((), jnp.bfloat16)
    )
    adapter_contribution = jnp.dot(
        low_wide.reshape(group_rows, tenants * rank_size),
        up_flat,
        preferred_element_type=jnp.float32,
    )
    return (base_projection + adapter_scale * adapter_contribution).astype(jnp.bfloat16)


def solution(mesh):
    placed = (
        P(("dp", "tensor"), None),
        P(None, "tensor"),
        P("dp", None, "tensor"),
        P("dp", None, "tensor"),
        P(),
        P(),
        P(),
    )
    return jax.shard_map(
        on_device, mesh=mesh, in_specs=placed, out_specs=P("dp", "tensor"), check_vma=False
    )
```

time: 403 us -> 472 us (1.17)
  waiting for transfers between devices: 272 us -> 390 us
  blocking collectives: 74.8 us -> 40.6 us
  matrix products: 39.7 us -> 15.1 us
  starting transfers between devices: 0.08 us -> 5.9 us
    reduce_scatter x0 -> x1, waiting for transfers between devices: none -> 201 us  [on_device(): lax.psum_scatter(partial_low, 'tensor', scatter_dimension=0, tiled=True)]
    all_gather x2 -> x0, waiting for transfers between devices: 101 us -> none  [the longest x1 55.6 us: on_device(): lax.all_gather(pool_down, 'dp', axis=0, tiled=True)]
    psum x1 -> x0, blocking collectives: 74.8 us -> none  [on_device(): low_rank = lax.psum(packed, 'tensor').astype(jnp.bfloat16)]
    all_gather x0 -> x1, blocking collectives: none -> 40.6 us  [on_device(): lax.all_gather(low_part, 'tensor', axis=0, tiled=True).astype(jnp.bfloat16)]
    all_to_all x0 -> x1, waiting for transfers between devices: none -> 28 us  [on_device(): recv = lax.all_to_all(send, 'dp', 0, 0, tiled=True)]
    dot_general x2 -> x0, matrix products: 24.5 us -> none  [select_rows(): jnp.einsum('ks,srd->krd', one_hot.astype(jnp.bfloat16), table, preferred_...]
    all_gather x1, waiting for transfers between devices: 170 us -> 160 us  [on_device(): row_block = lax.all_gather(tokens, 'tensor', axis=0, tiled=True)]
    all_to_all x0 -> x1, starting transfers between devices: none -> 5.86 us  [on_device(): recv = lax.all_to_all(send, 'dp', 0, 0, tiled=True)]
  transfers between devices with their start and end apart: 3 -> 3, of which waited for: 3 -> 3; matrix products, arithmetic and copies ran while one was open for 7% -> 1% of each run, Pallas kernels for 0% -> 0%
where the time goes in v1:
time: 472 us
  waiting for transfers between devices  390 us (83%)
  blocking collectives  40.6 us (9%)
  matrix products  15.1 us (3%)
  between operations  13.6 us (3%)
  starting transfers between devices  5.9 us (1%)
    reduce_scatter x1, waiting for transfers between devices, on_device(): lax.psum_scatter(partial_low, 'tensor', scatter_dimension=0, tiled=True)  201 us
    all_gather x1, waiting for transfers between devices, on_device(): row_block = lax.all_gather(tokens, 'tensor', axis=0, tiled=True)  160 us
    all_gather x1, blocking collectives, on_device(): lax.all_gather(low_part, 'tensor', axis=0, tiled=True).astype(jnp.bfloat16)  40.6 us
    all_to_all x1, waiting for transfers between devices, on_device(): recv = lax.all_to_all(send, 'dp', 0, 0, tiled=True)  28 us
    dot_general x1, matrix products, on_device(): jnp.dot(row_block, q_weight, preferred_element_type=jnp.float32)  12.8 us
  transfers between devices with their start and end apart: 3, of which 3 were waited for; matrix products, arithmetic and copies ran while one was open for 1% of the time, Pallas kernels for 0%

profile of v1, /device:TPU:2, one launch (start us, length us, event | category | flops | bytes accessed | tf_op | source)
XLA Modules:
  0.0 472.1 jit_solution(14032850056442191799)
XLA Ops:
  6.5 0.7 all-gather.2.cloned.1.call-update
  7.3 0.8 copy.24
  8.0 0.1 reshape.115
  8.2 1.2 gather_fusion
  9.4 0.1 reshape.114
  9.5 0.1 add_select_fusion.1
  9.7 0.1 pad_maximum_fusion
  9.7 0.7 gather_fusion.1
  10.4 1.6 broadcast_select_fusion
  12.1 5.9 %all-to-all-start = ((bf16[16,128,512]{2,1,0:T(8,128)(2,1)}), bf16[16,128,512]{2,1,0:T(8,128)(2,1)S(1)}, u32[]{:S(2)}, u32[]{:S(2)}) async-start(bf16[16,128,512]{2,1,0:T(8,128)(2,1)} %broadcast_select_fusion), calls=%async_computation | async-start | bytes 4194304 | tf_op jit(solution)/shard_map/all_to_all | solution.py:33
  18.0 0.2 dynamic-slice_reduce_fusion
  18.2 0.2 reduce-window.8
  18.4 0.1 convert_reduce_fusion
  18.5 28.0 %all-to-all-done = bf16[16,128,512]{2,1,0:T(8,128)(2,1)S(1)} async-done(((bf16[16,128,512]{2,1,0:T(8,128)(2,1)}), bf16[16,128,512]{2,1,0:T(8,128)(2,1)S(1)}, u32[]{:S(2)}, u32[]{:S(2)}) %all-to-all-start) | async-done | bytes 2097184 | tf_op jit(solution)/shard_map/all_to_all | solution.py:33
  46.5 0.6 gather_fusion.2
  47.1 0.2 broadcast_select_fusion.1
  47.3 160.2 %all-gather.2.cloned.1.call-done = bf16[768,8192]{1,0:T(8,128)(2,1)} async-done(((bf16[48,8192]{1,0:T(8,128)(2,1)}), bf16[768,8192]{1,0:T(8,128)(2,1)}) %all-gather.2.cloned.1.call-update) | async-done | bytes 12582928 | tf_op jit(solution)/shard_map/all_gather | solution.py:40
  207.5 1.8 select_reduce_fusion
  209.3 0.9 copy.29
  210.2 201.0 %reduce-scatter.4.cloned.1.call-done = f32[48,64]{1,0:T(8,128)} async-done(((f32[768,64]{1,0:T(8,128)}), f32[48,64]{1,0:T(8,128)}) %reduce-scatter.4.cloned.1.call-update) | async-done | bytes 12304 | tf_op jit(solution)/shard_map/reduce_scatter | solution.py:53
  411.2 40.6 %all_gather.7 = f32[768,64]{1,0:T(8,128)S(1)} all-gather(f32[48,64]{1,0:T(8,128)} %reduce-scatter.4.cloned.1.call-done), channel_id=1, replica_groups=mesh['dp'=16,'tensor'=16] {'tensor'}, dimensions={0}, use_global_device_ids=true | all-gather | bytes 208896 | tf_op jit(solution)/shard_map/all_gather | solution.py:54
  451.8 0.1 copy.28
  451.9 0.6 fusion.3
  452.5 12.8 %fusion.1 = bf16[768,512]{1,0:T(8,128)(2,1)} fusion(f32[768,512,1]{1,0,2:T(8,128)S(1)} %fusion.3, bf16[768,8192]{1,0:T(8,128)(2,1)} %all-gather.2.cloned.1.call-done, bf16[8192,512]{1,0:T(8,128)(2,1)} %param.8), kind=kOutput, calls=%fused_computation.6 | convolution fusion | flops 6443630592 | bytes 23330816 | tf_op jit(solution)/shard_map/dot_general | solution.py:41
  (21 shorter events, 0.1 us)
Async XLA Ops:
  6.5 11.4 %copy-start = (s32[16,8]{0,1:T(8,128)S(1)}, s32[16,8]{0,1:T(8,128)}, u32[]{:S(2)}) copy-start(s32[16,8]{0,1:T(8,128)} %param.11) | copy-start | bytes 1540
  6.5 1.6 copy-start.1
  6.5 201.0 %all-gather.2.cloned.1.call-start = ((), (), s32[]{:S(2)}) async-start(), calls=%async_computation.2 | async-start | bytes 13369344 | tf_op jit(solution)/shard_map/all_gather | solution.py:40
  8.1 1.5 copy-start.2
  8.2 1.5 copy-start.3
  12.1 34.4 %all-to-all-start = ((bf16[16,128,512]{2,1,0:T(8,128)(2,1)}), bf16[16,128,512]{2,1,0:T(8,128)(2,1)S(1)}, u32[]{:S(2)}, u32[]{:S(2)}) async-start(bf16[16,128,512]{2,1,0:T(8,128)(2,1)} %broadcast_select_fusion), calls=%async_computation | async-start | bytes 4194304 | tf_op jit(solution)/shard_map/all_to_all | solution.py:33
  17.9 393.3 %reduce-scatter.4.cloned.1.call-start = ((), (), s32[]{:S(2)}) async-start(), calls=%async_computation.3 | async-start | bytes 417792 | tf_op jit(solution)/shard_map/reduce_scatter | solution.py:53
Sparse Core Ops, SparseCore 0:
  9.9 197.5 all-gather.1
  211.3 199.8 reduce-scatter.3

commit v2 on v1

--- a/solution.py
+++ b/solution.py
@@ -11,6 +11,15 @@
     positions = jnp.arange(group_rows, dtype=jnp.int32)
     tenant_index = jnp.sum((positions[:, None] >= block_ends[None, :]).astype(jnp.int32), axis=1)
     return tenant_index[:, None] == jnp.arange(tenants, dtype=jnp.int32)[None, :]
+
+
+def tensor_sum(value, members):
+    step = 1
+    while step < members:
+        pairs = [(i, i ^ step) for i in range(members)]
+        value = value + lax.ppermute(value, "tensor", pairs)
+        step *= 2
+    return value
 
 
 def on_device(tokens, q_weight, pool_down, pool_up, block_units, adapter_ids, location):
@@ -50,8 +59,7 @@
     partial_low = jnp.sum(
         jnp.where(tenant_masks[:, :, None], wide_part, jnp.zeros((), jnp.float32)), axis=1
     )
-    low_part = lax.psum_scatter(partial_low, "tensor", scatter_dimension=0, tiled=True)
-    low_rank = lax.all_gather(low_part, "tensor", axis=0, tiled=True).astype(jnp.bfloat16)
+    low_rank = tensor_sum(partial_low, lax.axis_size("tensor")).astype(jnp.bfloat16)
     low_wide = jnp.where(
         tenant_masks[:, :, None], low_rank[:, None, :], jnp.zeros((), jnp.bfloat16)
     )

time: 472 us -> 261 us (0.55)
  waiting for transfers between devices: 390 us -> 214 us
  blocking collectives: 40.6 us -> 0 us
  starting transfers between devices: 5.9 us -> 11.6 us
    reduce_scatter x1 -> x0, waiting for transfers between devices: 201 us -> none  [on_device(): lax.psum_scatter(partial_low, 'tensor', scatter_dimension=0, tiled=True)]
    all_gather x1 -> x0, blocking collectives: 40.6 us -> none  [on_device(): lax.all_gather(low_part, 'tensor', axis=0, tiled=True).astype(jnp.bfloat16)]
    ppermute x0 -> x4, waiting for transfers between devices: none -> 25 us  [tensor_sum(): value = value + lax.ppermute(value, 'tensor', pairs)]
    ppermute x0 -> x4, starting transfers between devices: none -> 5.78 us  [tensor_sum(): value = value + lax.ppermute(value, 'tensor', pairs)]
  transfers between devices with their start and end apart: 3 -> 6, of which waited for: 3 -> 5; matrix products, arithmetic and copies ran while one was open for 1% -> 7% of each run, Pallas kernels for 0% -> 0%
where the time goes in v2:
time: 261 us; the launch traced here: 260 us
  waiting for transfers between devices  214 us (82%)
  matrix products  14.9 us (6%)
  between operations  13.6 us (5%)
  starting transfers between devices  11.6 us (4%)
  local copies, waits for them, and re-layouts  3.65 us (1%)
    all_gather x1, waiting for transfers between devices, on_device(): row_block = lax.all_gather(tokens, 'tensor', axis=0, tiled=True)  160 us
    all_to_all x1, waiting for transfers between devices, on_device(): recv = lax.all_to_all(send, 'dp', 0, 0, tiled=True)  28.1 us
    ppermute x4, waiting for transfers between devices, tensor_sum(): value = value + lax.ppermute(value, 'tensor', pairs)  25 us
    dot_general x1, matrix products, on_device(): jnp.dot(row_block, q_weight, preferred_element_type=jnp.float32)  11.7 us
    all_to_all x1, starting transfers between devices, on_device(): recv = lax.all_to_all(send, 'dp', 0, 0, tiled=True)  5.86 us
    ppermute x4, starting transfers between devices, tensor_sum(): value = value + lax.ppermute(value, 'tensor', pairs)  5.78 us
  transfers between devices with their start and end apart: 6, of which 5 were waited for; matrix products, arithmetic and copies ran while one was open for 7% of the time, Pallas kernels for 0%

profile of v2, /device:TPU:2, one launch (start us, length us, event | category | flops | bytes accessed | tf_op | source)
XLA Modules:
  0.0 260.2 jit_solution(11681030077185463062)
XLA Ops:
  6.5 0.7 all-gather.2.cloned.1.call-update
  7.3 0.8 copy.14
  8.0 0.1 reshape.115
  8.2 1.2 gather_fusion
  9.5 0.1 add_select_fusion.1
  9.7 0.7 gather_fusion.1
  10.4 1.6 broadcast_select_fusion
  12.1 5.9 %all-to-all-start = ((bf16[16,128,512]{2,1,0:T(8,128)(2,1)}), bf16[16,128,512]{2,1,0:T(8,128)(2,1)S(1)}, u32[]{:S(2)}, u32[]{:S(2)}) async-start(bf16[16,128,512]{2,1,0:T(8,128)(2,1)} %broadcast_select_fusion), calls=%async_computation | async-start | bytes 4194304 | tf_op jit(solution)/shard_map/all_to_all | solution.py:42
  17.9 0.2 dynamic-slice_reduce_fusion
  18.1 0.2 reduce-window.8
  18.5 28.1 %all-to-all-done = bf16[16,128,512]{2,1,0:T(8,128)(2,1)S(1)} async-done(((bf16[16,128,512]{2,1,0:T(8,128)(2,1)}), bf16[16,128,512]{2,1,0:T(8,128)(2,1)S(1)}, u32[]{:S(2)}, u32[]{:S(2)}) %all-to-all-start) | async-done | bytes 2097184 | tf_op jit(solution)/shard_map/all_to_all | solution.py:42
  46.5 0.6 gather_fusion.2
  47.1 0.2 broadcast_select_fusion.1
  47.3 160.2 %all-gather.2.cloned.1.call-done = bf16[768,8192]{1,0:T(8,128)(2,1)} async-done(((bf16[48,8192]{1,0:T(8,128)(2,1)}), bf16[768,8192]{1,0:T(8,128)(2,1)}) %all-gather.2.cloned.1.call-update) | async-done | bytes 12582928 | tf_op jit(solution)/shard_map/all_gather | solution.py:49
  207.5 1.8 select_reduce_fusion
  209.3 0.1 collective-permute-start
  209.4 5.9 %collective-permute-done = f32[768,64]{0,1:T(8,128)S(1)} collective-permute-done((f32[768,64]{0,1:T(8,128)S(1)}, f32[768,64]{0,1:T(8,128)S(1)}, u32[]{:S(2)}, u32[]{:S(2)}) %collective-permute-start) | collective-permute-done | bytes 196640 | tf_op jit(solution)/shard_map/ppermute | solution.py:20
  215.3 1.9 collective-permute-start.1
  217.2 8.4 %collective-permute-done.1 = f32[768,64]{0,1:T(8,128)S(1)} collective-permute-done((f32[768,64]{0,1:T(8,128)S(1)}, f32[768,64]{0,1:T(8,128)S(1)}, u32[]{:S(2)}, u32[]{:S(2)}) %collective-permute-start.1) | collective-permute-done | bytes 196640 | tf_op jit(solution)/shard_map/ppermute | solution.py:20
  225.6 3.2 %collective-permute-start.2 = (f32[768,64]{0,1:T(8,128)S(1)}, f32[768,64]{0,1:T(8,128)S(1)}, u32[]{:S(2)}, u32[]{:S(2)}) collective-permute-start(f32[768,64]{0,1:T(8,128)S(1)} %add.78), channel_id=1, source_target_pairs={{0,4},{1,5},{2,6},{3,7},{4,0},{5,1},{6,2},{7,3},{8,12},{9,13},{10,... | collective-permute-start | bytes 589832 | tf_op jit(solution)/shard_map/ppermute | solution.py:20
  228.7 10.7 %collective-permute-done.2 = f32[768,64]{0,1:T(8,128)S(1)} collective-permute-done((f32[768,64]{0,1:T(8,128)S(1)}, f32[768,64]{0,1:T(8,128)S(1)}, u32[]{:S(2)}, u32[]{:S(2)}) %collective-permute-start.2) | collective-permute-done | bytes 196640 | tf_op jit(solution)/shard_map/ppermute | solution.py:20
  239.5 0.6 collective-permute-start.3
  240.1 11.7 %fusion.18 = f32[768,512]{1,0:T(8,128)S(1)} fusion(bf16[768,8192]{1,0:T(8,128)(2,1)} %all-gather.2.cloned.1.call-done, bf16[8192,512]{1,0:T(8,128)(2,1)} %param.8), kind=kOutput, calls=%fused_computation.50 | convolution fusion | flops 6442450944 | bytes 22544384 | tf_op jit(solution)/shard_map/dot_general | solution.py:50
  251.8 1.5 fusion.1
  (27 shorter events, 0.4 us)
Async XLA Ops:
  6.5 11.4 %copy-start = (s32[16,8]{0,1:T(8,128)S(1)}, s32[16,8]{0,1:T(8,128)}, u32[]{:S(2)}) copy-start(s32[16,8]{0,1:T(8,128)} %param.11) | copy-start | bytes 1540
  6.5 1.6 copy-start.1
  6.5 201.0 %all-gather.2.cloned.1.call-start = ((), (), s32[]{:S(2)}) async-start(), calls=%async_computation.1 | async-start | bytes 13369344 | tf_op jit(solution)/shard_map/all_gather | solution.py:49
  8.1 1.5 copy-start.2
  8.2 1.5 copy-start.3
  12.1 34.4 %all-to-all-start = ((bf16[16,128,512]{2,1,0:T(8,128)(2,1)}), bf16[16,128,512]{2,1,0:T(8,128)(2,1)S(1)}, u32[]{:S(2)}, u32[]{:S(2)}) async-start(bf16[16,128,512]{2,1,0:T(8,128)(2,1)} %broadcast_select_fusion), calls=%async_computation | async-start | bytes 4194304 | tf_op jit(solution)/shard_map/all_to_all | solution.py:42
  209.3 6.0 %collective-permute-start = (f32[768,64]{0,1:T(8,128)S(1)}, f32[768,64]{0,1:T(8,128)S(1)}, u32[]{:S(2)}, u32[]{:S(2)}) collective-permute-start(f32[768,64]{0,1:T(8,128)S(1)} %select_reduce_fusion), channel_id=1, source_target_pairs={{0,1},{1,0},{2,3},{3,2},{4,5},{5,4},{6,7},{7,6},{8,9},{9,8},{10,11... | collective-permute-start | bytes 589832 | tf_op jit(solution)/shard_map/ppermute | solution.py:20
  215.3 10.3 %collective-permute-start.1 = (f32[768,64]{0,1:T(8,128)S(1)}, f32[768,64]{0,1:T(8,128)S(1)}, u32[]{:S(2)}, u32[]{:S(2)}) collective-permute-start(f32[768,64]{0,1:T(8,128)S(1)} %add.77), channel_id=1, source_target_pairs={{0,2},{1,3},{2,0},{3,1},{4,6},{5,7},{6,4},{7,5},{8,10},{9,11},{10,... | collective-permute-start | bytes 589832 | tf_op jit(solution)/shard_map/ppermute | solution.py:20
  225.6 13.9 %collective-permute-start.2 = (f32[768,64]{0,1:T(8,128)S(1)}, f32[768,64]{0,1:T(8,128)S(1)}, u32[]{:S(2)}, u32[]{:S(2)}) collective-permute-start(f32[768,64]{0,1:T(8,128)S(1)} %add.78), channel_id=1, source_target_pairs={{0,4},{1,5},{2,6},{3,7},{4,0},{5,1},{6,2},{7,3},{8,12},{9,13},{10,... | collective-permute-start | bytes 589832 | tf_op jit(solution)/shard_map/ppermute | solution.py:20
  239.5 12.3 %collective-permute-start.3 = (f32[768,64]{0,1:T(8,128)S(1)}, f32[768,64]{0,1:T(8,128)S(1)}, u32[]{:S(2)}, u32[]{:S(2)}) collective-permute-start(f32[768,64]{0,1:T(8,128)S(1)} %add.79), channel_id=1, source_target_pairs={{0,8},{1,9},{2,10},{3,11},{4,12},{5,13},{6,14},{7,15},{8,0},{9,1},... | collective-permute-start | bytes 589832 | tf_op jit(solution)/shard_map/ppermute | solution.py:20
Sparse Core Ops, SparseCore 0:
  9.9 197.5 all-gather.1

commit v3 on v2

--- a/solution.py
+++ b/solution.py
@@ -45,21 +45,73 @@
     down_flat = panels[:, :rank_size, :].reshape(tenants * rank_size, local_width)
     up_flat = panels[:, rank_size:, :].reshape(tenants * rank_size, columns)
 
-    width_start = lax.axis_index("tensor") * local_width
-    row_block = lax.all_gather(tokens, "tensor", axis=0, tiled=True)
-    base_projection = jnp.dot(row_block, q_weight, preferred_element_type=jnp.float32)
-    local_cols = lax.dynamic_slice_in_dim(row_block, width_start, local_width, 1)
-    wide_part = lax.dot_general(
-        local_cols, down_flat, (((1,), (1,)), ((), ())), preferred_element_type=jnp.float32
-    )
-    group_rows = wide_part.shape[0]
-    wide_part = wide_part.reshape(group_rows, tenants, rank_size)
+    tensor_at = lax.axis_index("tensor")
+    members = lax.axis_size("tensor")
+    ring = members // 2
+    half = tensor_at // ring
+    ring_at = tensor_at % ring
+    width_start = tensor_at * local_width
+    shard_rows = tokens.shape[0]
+    group_rows = shard_rows * members
     pool_unit_row = lax.dynamic_index_in_dim(block_units, my_group, 0, keepdims=False)
-    tenant_masks = tenant_mask(pool_unit_row, group_rows, tenants)
-    partial_low = jnp.sum(
-        jnp.where(tenant_masks[:, :, None], wide_part, jnp.zeros((), jnp.float32)), axis=1
-    )
-    low_rank = tensor_sum(partial_low, lax.axis_size("tensor")).astype(jnp.bfloat16)
+    block_ends = 16 * jnp.cumsum(pool_unit_row)
+
+    swap = [(i, i ^ ring) for i in range(members)]
+    from_right = [(i, (i // ring) * ring + (i % ring - 1) % ring) for i in range(members)]
+    from_left = [(i, (i // ring) * ring + (i % ring + 1) % ring) for i in range(members)]
+
+    def ring_pieces(own):
+        pieces = [own] + [None] * (ring - 1)
+        right, left = own, own
+        for step in range(1, ring // 2):
+            right = lax.ppermute(right, "tensor", from_right)
+            left = lax.ppermute(left, "tensor", from_left)
+            pieces[step], pieces[ring - step] = right, left
+        cut = shard_rows // 2
+        far_right = lax.ppermute(right[:cut], "tensor", from_right)
+        far_left = lax.ppermute(left[cut:], "tensor", from_left)
+        pieces[ring // 2] = jnp.concatenate([far_right, far_left], axis=0)
+        return pieces
+
+    partner = lax.ppermute(tokens, "tensor", swap)
+    own_pieces = ring_pieces(tokens)
+    partner_pieces = ring_pieces(partner)
+
+    tenant_ids = jnp.arange(tenants, dtype=jnp.int32)
+
+    def piece_work(piece, piece_half, step):
+        first_row = (piece_half * ring + (ring_at + step) % ring) * shard_rows
+        positions = first_row + jnp.arange(shard_rows, dtype=jnp.int32)
+        tenant_index = jnp.sum((positions[:, None] >= block_ends[None, :]).astype(jnp.int32), axis=1)
+        masks = tenant_index[:, None] == tenant_ids[None, :]
+        base = jnp.dot(piece, q_weight, preferred_element_type=jnp.float32)
+        cols = lax.dynamic_slice_in_dim(piece, width_start, local_width, 1)
+        wide = lax.dot_general(
+            cols, down_flat, (((1,), (1,)), ((), ())), preferred_element_type=jnp.float32
+        ).reshape(shard_rows, tenants, rank_size)
+        low = jnp.sum(jnp.where(masks[:, :, None], wide, jnp.zeros((), jnp.float32)), axis=1)
+        return base, low
+
+    own_work = [piece_work(p, half, k) for k, p in enumerate(own_pieces)]
+    partner_work = [piece_work(p, 1 - half, k) for k, p in enumerate(partner_pieces)]
+
+    def to_group_order(own_list, partner_list):
+        def roll(stacked):
+            doubled = jnp.concatenate([stacked, stacked], axis=0)
+            return lax.dynamic_slice_in_dim(doubled, (ring - ring_at) % ring, ring, 0)
+        own_abs = roll(jnp.stack(own_list))
+        partner_abs = roll(jnp.stack(partner_list))
+        ordered = jnp.where(
+            half == 0, jnp.stack([own_abs, partner_abs]), jnp.stack([partner_abs, own_abs])
+        )
+        return ordered.reshape((group_rows,) + own_list[0].shape[1:])
+
+    base_projection = to_group_order([w[0] for w in own_work], [w[0] for w in partner_work])
+    partial_low = to_group_order([w[1] for w in own_work], [w[1] for w in partner_work])
+    positions = jnp.arange(group_rows, dtype=jnp.int32)
+    tenant_index = jnp.sum((positions[:, None] >= block_ends[None, :]).astype(jnp.int32), axis=1)
+    tenant_masks = tenant_index[:, None] == tenant_ids[None, :]
+    low_rank = tensor_sum(partial_low, members).astype(jnp.bfloat16)
     low_wide = jnp.where(
         tenant_masks[:, :, None], low_rank[:, None, :], jnp.zeros((), jnp.bfloat16)
     )

time: 261 us -> 215 us (0.82)
  waiting for transfers between devices: 214 us -> 68.4 us
  matrix products: 14.9 us -> 78.3 us
  starting transfers between devices: 11.6 us -> 43.6 us
  local copies, waits for them, and re-layouts: 3.65 us -> 18 us
  between operations: 13.6 us -> 1.08 us
    all_gather x1 -> x0, waiting for transfers between devices: 160 us -> none  [on_device(): row_block = lax.all_gather(tokens, 'tensor', axis=0, tiled=True)]
    dot_general x2 -> x32, matrix products: 13.4 us -> 76.8 us  [the longest x16 61.9 us: piece_work(): base = jnp.dot(piece, q_weight, preferred_element_type=jnp.float32)]
    ppermute x0 -> x17, waiting for transfers between devices: none -> 51.5 us  [the longest x6 26.3 us: ring_pieces(): right = lax.ppermute(right, 'tensor', from_right)]
    ppermute x0 -> x17, starting transfers between devices: none -> 32.7 us  [the longest x6 22.5 us: ring_pieces(): right = lax.ppermute(right, 'tensor', from_right)]
    all_to_all x1, waiting for transfers between devices: 28.1 us -> 0.01 us  [on_device(): recv = lax.all_to_all(send, 'dp', 0, 0, tiled=True)]
    unnamed x9 -> x73, local copies, waits for them, and re-layouts: 0.78 us -> 9.96 us
    ppermute x4, waiting for transfers between devices: 25 us -> 16.9 us  [tensor_sum(): value = value + lax.ppermute(value, 'tensor', pairs)]
  transfers between devices with their start and end apart: 6 -> 22, of which waited for: 5 -> 8; matrix products, arithmetic and copies ran while one was open for 7% -> 46% of each run, Pallas kernels for 0% -> 0%
where the time goes in v3:
time: 215 us; the launch traced here: 213 us
  matrix products  78.3 us (36%)
  waiting for transfers between devices  68.4 us (32%)
  starting transfers between devices  43.6 us (20%)
  local copies, waits for them, and re-layouts  18 us (8%)
  other arithmetic  4.14 us (2%)
    dot_general x16, matrix products, piece_work(): base = jnp.dot(piece, q_weight, preferred_element_type=jnp.float32)  61.9 us
    ppermute x6, waiting for transfers between devices, ring_pieces(): right = lax.ppermute(right, 'tensor', from_right)  26.3 us
    ppermute x6, starting transfers between devices, ring_pieces(): right = lax.ppermute(right, 'tensor', from_right)  22.5 us
    ppermute x1, waiting for transfers between devices, on_device(): partner = lax.ppermute(tokens, 'tensor', swap)  19.1 us
    ppermute x4, waiting for transfers between devices, tensor_sum(): value = value + lax.ppermute(value, 'tensor', pairs)  16.9 us
    dot_general x16, matrix products, piece_work(): lax.dot_general(cols, down_flat, (((1,), (1,)), ((), ())), preferred_elem...  14.9 us
    unnamed x73, local copies, waits for them, and re-layouts  9.96 us
    ppermute x2, starting transfers between devices, ring_pieces(): far_right = lax.ppermute(right[:cut], 'tensor', from_right)  6.57 us
  transfers between devices with their start and end apart: 22, of which 8 were waited for; matrix products, arithmetic and copies ran while one was open for 46% of the time, Pallas kernels for 0%

profile of v3, /device:TPU:2, one launch (start us, length us, event | category | flops | bytes accessed | tf_op | source)
XLA Modules:
  0.0 213.4 jit_solution(13713505870494934191)
XLA Ops:
  0.0 5.9 %collective-permute-start = (bf16[48,8192]{1,0:T(8,128)(2,1)}, bf16[48,8192]{1,0:T(8,128)(2,1)}, u32[]{:S(2)}, u32[]{:S(2)}) collective-permute-start(bf16[48,8192]{1,0:T(8,128)(2,1)} %param.7), channel_id=1, source_target_pairs={{0,7},{1,0},{2,1},{3,2},{4,3},{5,4},{6,5},{7,6},{8,15},{9,8},{10,9... | collective-permute-start | bytes 2359304 | tf_op jit(solution)/shard_map/ppermute | solution.py:67
  13.9 5.1 %all-to-all-start = ((bf16[16,128,512]{2,1,0:T(8,128)(2,1)}), bf16[16,128,512]{2,1,0:T(8,128)(2,1)S(1)}, u32[]{:S(2)}, u32[]{:S(2)}) async-start(bf16[16,128,512]{2,1,0:T(8,128)(2,1)} %broadcast_select_fusion), calls=%async_computation | async-start | bytes 4194304 | tf_op jit(solution)/shard_map/all_to_all | solution.py:42
  20.1 5.7 %constant_dynamic-update-slice_fusion.17 = (f32[16,48,512]{2,1,0:T(8,128)}, f32[1,48,512]{2,1,0:T(8,128)S(1)}) fusion(bf16[48,8192]{1,0:T(8,128)(2,1)S(1)} %copy-done.2, bf16[8192,512]{1,0:T(8,128)(2,1)} %param.8), kind=kOutput, calls=%fused_computation.86 | convolution fusion | flops 402653184 | bytes 9371648 | tf_op jit(solution)/shard_map/dot_general | solution.py:87
  25.8 19.1 %collective-permute-done.8 = bf16[48,8192]{1,0:T(8,128)(2,1)} collective-permute-done((bf16[48,8192]{1,0:T(8,128)(2,1)}, bf16[48,8192]{1,0:T(8,128)(2,1)}, u32[]{:S(2)}, u32[]{:S(2)}) %collective-permute-start.8) | collective-permute-done | bytes 786464 | tf_op jit(solution)/shard_map/ppermute | solution.py:76
  51.4 5.8 %constant_dynamic-update-slice_fusion.35 = (f32[16,48,512]{2,1,0:T(8,128)}, f32[1,48,512]{2,1,0:T(8,128)S(1)}) fusion(bf16[48,8192]{1,0:T(8,128)(2,1)} %collective-permute-done.8, bf16[8192,512]{1,0:T(8,128)(2,1)} %param.8), kind=kOutput, calls=%fused_computation.104 | convolution fusion | flops 402653184 | bytes 9371648 | tf_op jit(solution)/shard_map/dot_general | solution.py:87
  57.2 3.3 %constant_dynamic-update-slice_fusion.16 = (f32[16,48,512]{2,1,0:T(8,128)}, f32[1,48,512]{2,1,0:T(8,128)S(1)}) fusion(f32[16,48,512]{2,1,0:T(8,128)} %get-tuple-element.39, bf16[48,8192]{1,0:T(8,128)(2,1)} %collective-permute-done, bf16[8192,512]{1,0:T(8,128)(2,1)S(1)} %bitcast.191), kind=kOutput, calls=%fused_computation.85 | convolution fusion | flops 402653184 | bytes 9371648 | tf_op jit(solution)/shard_map/dot_general | solution.py:87
  60.6 18.9 %collective-permute-done.1 = bf16[48,8192]{1,0:T(8,128)(2,1)} collective-permute-done((bf16[48,8192]{1,0:T(8,128)(2,1)}, bf16[48,8192]{1,0:T(8,128)(2,1)}, u32[]{:S(2)}, u32[]{:S(2)}) %collective-permute-start.1) | collective-permute-done | bytes 786464 | tf_op jit(solution)/shard_map/ppermute | solution.py:67
  86.0 3.3 %constant_dynamic-update-slice_fusion.34 = (f32[16,48,512]{2,1,0:T(8,128)}, f32[1,48,512]{2,1,0:T(8,128)S(1)}) fusion(f32[16,48,512]{2,1,0:T(8,128)} %get-tuple-element.23, bf16[48,8192]{1,0:T(8,128)(2,1)} %collective-permute-done.9, bf16[8192,512]{1,0:T(8,128)(2,1)S(1)} %bitcast.191), kind=kOutput, calls=%fused_computation.103 | convolution fusion | flops 402653184 | bytes 9371648 | tf_op jit(solution)/shard_map/dot_general | solution.py:87
  89.3 3.3 %constant_dynamic-update-slice_fusion.15 = (f32[16,48,512]{2,1,0:T(8,128)}, f32[1,48,512]{2,1,0:T(8,128)S(1)}) fusion(f32[16,48,512]{2,1,0:T(8,128)} %get-tuple-element.41, bf16[48,8192]{1,0:T(8,128)(2,1)} %collective-permute-done.1, bf16[8192,512]{1,0:T(8,128)(2,1)S(1)} %bitcast.191), kind=kOutput, calls=%fused_computation.84 | convolution fusion | flops 402653184 | bytes 9371648 | tf_op jit(solution)/shard_map/dot_general | solution.py:87
  106.2 3.3 %collective-permute-start.3 = (bf16[24,8192]{1,0:T(8,128)(2,1)S(1)}, bf16[24,8192]{1,0:T(8,128)(2,1)S(1)}, u32[]{:S(2)}, u32[]{:S(2)}) collective-permute-start(bf16[24,8192]{1,0:T(8,128)(2,1)S(1)} %slice.30), channel_id=1, source_target_pairs={{0,7},{1,0},{2,1},{3,2},{4,3},{5,4},{6,5},{7,6},{8,15},{9,8},{10,9... | collective-permute-start | bytes 1179656 | tf_op jit(solution)/shard_map/ppermute | solution.py:71
  109.6 7.4 %collective-permute-done.10 = bf16[48,8192]{1,0:T(8,128)(2,1)} collective-permute-done((bf16[48,8192]{1,0:T(8,128)(2,1)}, bf16[48,8192]{1,0:T(8,128)(2,1)}, u32[]{:S(2)}, u32[]{:S(2)}) %collective-permute-start.10) | collective-permute-done | bytes 786464 | tf_op jit(solution)/shard_map/ppermute | solution.py:67
  117.0 3.7 %collective-permute-start.11 = (bf16[48,8192]{1,0:T(8,128)(2,1)}, bf16[48,8192]{1,0:T(8,128)(2,1)S(1)}, u32[]{:S(2)}, u32[]{:S(2)}) collective-permute-start(bf16[48,8192]{1,0:T(8,128)(2,1)} %collective-permute-done.10), channel_id=1, source_target_pairs={{0,7},{1,0},{2,1},{3,2},{4,3},{5,4},{6,5},{7,6},{8,15},{9,8},{10,9... | collective-permute-start | bytes 2359304 | tf_op jit(solution)/shard_map/ppermute | solution.py:67
  123.5 5.9 %constant_dynamic-update-slice_fusion.33 = (f32[16,48,512]{2,1,0:T(8,128)}, f32[1,48,512]{2,1,0:T(8,128)S(1)}) fusion(f32[16,48,512]{2,1,0:T(8,128)} %get-tuple-element.25, bf16[48,8192]{1,0:T(8,128)(2,1)} %collective-permute-done.10, bf16[8192,512]{1,0:T(8,128)(2,1)} %param.8), kind=kOutput, calls=%fused_computation.102 | convolution fusion | flops 402653184 | bytes 9371648 | tf_op jit(solution)/shard_map/dot_general | solution.py:87
  129.5 3.3 %constant_dynamic-update-slice_fusion.14 = (f32[16,48,512]{2,1,0:T(8,128)}, f32[1,48,512]{2,1,0:T(8,128)S(1)}) fusion(f32[16,48,512]{2,1,0:T(8,128)} %get-tuple-element.43, bf16[48,8192]{1,0:T(8,128)(2,1)} %collective-permute-done.2, bf16[8192,512]{1,0:T(8,128)(2,1)S(1)} %bitcast.193), kind=kOutput, calls=%fused_computation.83 | convolution fusion | flops 402653184 | bytes 9371648 | tf_op jit(solution)/shard_map/dot_general | solution.py:87
  139.3 3.3 %constant_dynamic-update-slice_fusion.11 = (f32[16,48,512]{2,1,0:T(8,128)}, f32[1,48,512]{2,1,0:T(8,128)S(1)}) fusion(f32[16,48,512]{2,1,0:T(8,128)} %get-tuple-element.49, bf16[48,8192]{1,0:T(8,128)(2,1)} %collective-permute-done.5, bf16[8192,512]{1,0:T(8,128)(2,1)S(1)} %bitcast.193), kind=kOutput, calls=%fused_computation.80 | convolution fusion | flops 402653184 | bytes 9371648 | tf_op jit(solution)/shard_map/dot_general | solution.py:87
  142.6 3.3 %constant_dynamic-update-slice_fusion.10 = (f32[16,48,512]{2,1,0:T(8,128)}, f32[1,48,512]{2,1,0:T(8,128)S(1)}) fusion(f32[16,48,512]{2,1,0:T(8,128)} %get-tuple-element.51, bf16[48,8192]{1,0:T(8,128)(2,1)} %collective-permute-done.4, bf16[8192,512]{1,0:T(8,128)(2,1)S(1)} %bitcast.193), kind=kOutput, calls=%fused_computation.79 | convolution fusion | flops 402653184 | bytes 9371648 | tf_op jit(solution)/shard_map/dot_general | solution.py:87
  151.1 3.3 %collective-permute-start.12 = (bf16[24,8192]{1,0:T(8,128)(2,1)S(1)}, bf16[24,8192]{1,0:T(8,128)(2,1)S(1)}, u32[]{:S(2)}, u32[]{:S(2)}) collective-permute-start(bf16[24,8192]{1,0:T(8,128)(2,1)S(1)} %slice.32), channel_id=1, source_target_pairs={{0,7},{1,0},{2,1},{3,2},{4,3},{5,4},{6,5},{7,6},{8,15},{9,8},{10,9... | collective-permute-start | bytes 1179656 | tf_op jit(solution)/shard_map/ppermute | solution.py:71
  159.7 3.8 %collective-permute-done.16 = bf16[24,8192]{1,0:T(8,128)(2,1)S(1)} collective-permute-done((bf16[24,8192]{1,0:T(8,128)(2,1)S(1)}, bf16[24,8192]{1,0:T(8,128)(2,1)S(1)}, u32[]{:S(2)}, u32[]{:S(2)}) %collective-permute-start.16) | collective-permute-done | bytes 393248 | tf_op jit(solution)/shard_map/ppermute | solution.py:72
  164.6 5.7 %constant_dynamic-update-slice_fusion.31 = (f32[16,48,512]{2,1,0:T(8,128)}, f32[1,48,512]{2,1,0:T(8,128)S(1)}) fusion(f32[16,48,512]{2,1,0:T(8,128)} %get-tuple-element.29, bf16[48,8192]{1,0:T(8,128)(2,1)S(1)} %constant_dynamic-update-slice_fusion.18, bf16[8192,512]{1,0:T(8,128)(2,1)} %param.8), kind=kOutput, calls=%fused_computation.100 | convolution fusion | flops 402653184 | bytes 9371648 | tf_op jit(solution)/shard_map/dot_general | solution.py:87
  170.3 5.7 %constant_dynamic-update-slice_fusion.30 = (f32[16,48,512]{2,1,0:T(8,128)}, f32[1,48,512]{2,1,0:T(8,128)S(1)}) fusion(f32[16,48,512]{2,1,0:T(8,128)} %get-tuple-element.31, bf16[48,8192]{1,0:T(8,128)(2,1)S(1)} %collective-permute-done.15, bf16[8192,512]{1,0:T(8,128)(2,1)} %param.8), kind=kOutput, calls=%fused_computation.99 | convolution fusion | flops 402653184 | bytes 9371648 | tf_op jit(solution)/shard_map/dot_general | solution.py:87
  176.0 3.3 %constant_dynamic-update-slice_fusion.29 = (f32[16,48,512]{2,1,0:T(8,128)}, f32[1,48,512]{2,1,0:T(8,128)S(1)}) fusion(f32[16,48,512]{2,1,0:T(8,128)} %get-tuple-element.33, bf16[48,8192]{1,0:T(8,128)(2,1)} %collective-permute-done.14, bf16[8192,512]{1,0:T(8,128)(2,1)S(1)} %bitcast.195), kind=kOutput, calls=%fused_computation.98 | convolution fusion | flops 402653184 | bytes 9371648 | tf_op jit(solution)/shard_map/dot_general | solution.py:87
  179.3 3.3 %constant_dynamic-update-slice_fusion.28 = (f32[16,48,512]{2,1,0:T(8,128)}, f32[1,48,512]{2,1,0:T(8,128)S(1)}) fusion(f32[16,48,512]{2,1,0:T(8,128)} %get-tuple-element.35, bf16[48,8192]{1,0:T(8,128)(2,1)} %collective-permute-done.13, bf16[8192,512]{1,0:T(8,128)(2,1)S(1)} %bitcast.195), kind=kOutput, calls=%fused_computation.97 | convolution fusion | flops 402653184 | bytes 9371648 | tf_op jit(solution)/shard_map/dot_general | solution.py:87
  186.6 7.4 %collective-permute-done.18 = f32[768,64]{0,1:T(8,128)S(1)} collective-permute-done((f32[768,64]{0,1:T(8,128)S(1)}, f32[768,64]{0,1:T(8,128)S(1)}, u32[]{:S(2)}, u32[]{:S(2)}) %collective-permute-start.18) | collective-permute-done | bytes 196640 | tf_op jit(solution)/shard_map/ppermute | solution.py:20
  197.4 7.2 %collective-permute-done.19 = f32[768,64]{0,1:T(8,128)S(1)} collective-permute-done((f32[768,64]{0,1:T(8,128)S(1)}, f32[768,64]{0,1:T(8,128)S(1)}, u32[]{:S(2)}, u32[]{:S(2)}) %collective-permute-start.19) | collective-permute-done | bytes 196640 | tf_op jit(solution)/shard_map/ppermute | solution.py:20
  (203 shorter events, 71.9 us)
Async XLA Ops:
  0.0 48.2 %collective-permute-start = (bf16[48,8192]{1,0:T(8,128)(2,1)}, bf16[48,8192]{1,0:T(8,128)(2,1)}, u32[]{:S(2)}, u32[]{:S(2)}) collective-permute-start(bf16[48,8192]{1,0:T(8,128)(2,1)} %param.7), channel_id=1, source_target_pairs={{0,7},{1,0},{2,1},{3,2},{4,3},{5,4},{6,5},{7,6},{8,15},{9,8},{10,9... | collective-permute-start | bytes 2359304 | tf_op jit(solution)/shard_map/ppermute | solution.py:67
  5.9 45.5 %collective-permute-start.4 = (bf16[48,8192]{1,0:T(8,128)(2,1)}, bf16[48,8192]{1,0:T(8,128)(2,1)}, u32[]{:S(2)}, u32[]{:S(2)}) collective-permute-start(bf16[48,8192]{1,0:T(8,128)(2,1)} %param.7), channel_id=1, source_target_pairs={{0,1},{1,2},{2,3},{3,4},{4,5},{5,6},{6,7},{7,0},{8,9},{9,10},{10,1... | collective-permute-start | bytes 2359304 | tf_op jit(solution)/shard_map/ppermute | solution.py:68
  5.9 39.1 %collective-permute-start.8 = (bf16[48,8192]{1,0:T(8,128)(2,1)}, bf16[48,8192]{1,0:T(8,128)(2,1)}, u32[]{:S(2)}, u32[]{:S(2)}) collective-permute-start(bf16[48,8192]{1,0:T(8,128)(2,1)} %param.7), channel_id=1, source_target_pairs={{0,8},{1,9},{2,10},{3,11},{4,12},{5,13},{6,14},{7,15},{8,0},{9,1},... | collective-permute-start | bytes 2359304 | tf_op jit(solution)/shard_map/ppermute | solution.py:76
  13.9 78.8 %all-to-all-start = ((bf16[16,128,512]{2,1,0:T(8,128)(2,1)}), bf16[16,128,512]{2,1,0:T(8,128)(2,1)S(1)}, u32[]{:S(2)}, u32[]{:S(2)}) async-start(bf16[16,128,512]{2,1,0:T(8,128)(2,1)} %broadcast_select_fusion), calls=%async_computation | async-start | bytes 4194304 | tf_op jit(solution)/shard_map/all_to_all | solution.py:42
  20.1 37.1 %slice-start = ((s8[8388608]{0:T(1024)(128)(4,1)}), s8[4194304]{0:T(1024)(128)(4,1)S(1)}, s32[]{:S(2)}) async-start(s8[8388608]{0:T(1024)(128)(4,1)} %bitcast.190), calls=%async_computation.1 | async-start | bytes 8388608
  44.9 37.8 %collective-permute-start.9 = (bf16[48,8192]{1,0:T(8,128)(2,1)}, bf16[48,8192]{1,0:T(8,128)(2,1)}, u32[]{:S(2)}, u32[]{:S(2)}) collective-permute-start(bf16[48,8192]{1,0:T(8,128)(2,1)} %collective-permute-done.8), channel_id=1, source_target_pairs={{0,7},{1,0},{2,1},{3,2},{4,3},{5,4},{6,5},{7,6},{8,15},{9,8},{10,9... | collective-permute-start | bytes 2359304 | tf_op jit(solution)/shard_map/ppermute | solution.py:67
  48.2 37.8 %collective-permute-start.13 = (bf16[48,8192]{1,0:T(8,128)(2,1)}, bf16[48,8192]{1,0:T(8,128)(2,1)}, u32[]{:S(2)}, u32[]{:S(2)}) collective-permute-start(bf16[48,8192]{1,0:T(8,128)(2,1)} %collective-permute-done.8), channel_id=1, source_target_pairs={{0,1},{1,2},{2,3},{3,4},{4,5},{5,6},{6,7},{7,0},{8,9},{9,10},{10,1... | collective-permute-start | bytes 2359304 | tf_op jit(solution)/shard_map/ppermute | solution.py:68
  48.2 31.3 %collective-permute-start.1 = (bf16[48,8192]{1,0:T(8,128)(2,1)}, bf16[48,8192]{1,0:T(8,128)(2,1)}, u32[]{:S(2)}, u32[]{:S(2)}) collective-permute-start(bf16[48,8192]{1,0:T(8,128)(2,1)} %collective-permute-done), channel_id=1, source_target_pairs={{0,7},{1,0},{2,1},{3,2},{4,3},{5,4},{6,5},{7,6},{8,15},{9,8},{10,9... | collective-permute-start | bytes 2359304 | tf_op jit(solution)/shard_map/ppermute | solution.py:67
  51.4 31.3 %collective-permute-start.5 = (bf16[48,8192]{1,0:T(8,128)(2,1)}, bf16[48,8192]{1,0:T(8,128)(2,1)}, u32[]{:S(2)}, u32[]{:S(2)}) collective-permute-start(bf16[48,8192]{1,0:T(8,128)(2,1)} %collective-permute-done.4), channel_id=1, source_target_pairs={{0,1},{1,2},{2,3},{3,4},{4,5},{5,6},{6,7},{7,0},{8,9},{9,10},{10,1... | collective-permute-start | bytes 2359304 | tf_op jit(solution)/shard_map/ppermute | solution.py:68
  79.5 25.7 %collective-permute-start.2 = (bf16[48,8192]{1,0:T(8,128)(2,1)}, bf16[48,8192]{1,0:T(8,128)(2,1)}, u32[]{:S(2)}, u32[]{:S(2)}) collective-permute-start(bf16[48,8192]{1,0:T(8,128)(2,1)} %collective-permute-done.1), channel_id=1, source_target_pairs={{0,7},{1,0},{2,1},{3,2},{4,3},{5,4},{6,5},{7,6},{8,15},{9,8},{10,9... | collective-permute-start | bytes 2359304 | tf_op jit(solution)/shard_map/ppermute | solution.py:67
  82.7 26.7 %collective-permute-start.6 = (bf16[48,8192]{1,0:T(8,128)(2,1)}, bf16[48,8192]{1,0:T(8,128)(2,1)S(1)}, u32[]{:S(2)}, u32[]{:S(2)}) collective-permute-start(bf16[48,8192]{1,0:T(8,128)(2,1)} %collective-permute-done.5), channel_id=1, source_target_pairs={{0,1},{1,2},{2,3},{3,4},{4,5},{5,6},{6,7},{7,0},{8,9},{9,10},{10,1... | collective-permute-start | bytes 2359304 | tf_op jit(solution)/shard_map/ppermute | solution.py:68
  82.7 34.3 %collective-permute-start.10 = (bf16[48,8192]{1,0:T(8,128)(2,1)}, bf16[48,8192]{1,0:T(8,128)(2,1)}, u32[]{:S(2)}, u32[]{:S(2)}) collective-permute-start(bf16[48,8192]{1,0:T(8,128)(2,1)} %collective-permute-done.9), channel_id=1, source_target_pairs={{0,7},{1,0},{2,1},{3,2},{4,3},{5,4},{6,5},{7,6},{8,15},{9,8},{10,9... | collective-permute-start | bytes 2359304 | tf_op jit(solution)/shard_map/ppermute | solution.py:67
  86.0 37.2 %collective-permute-start.14 = (bf16[48,8192]{1,0:T(8,128)(2,1)}, bf16[48,8192]{1,0:T(8,128)(2,1)}, u32[]{:S(2)}, u32[]{:S(2)}) collective-permute-start(bf16[48,8192]{1,0:T(8,128)(2,1)} %collective-permute-done.13), channel_id=1, source_target_pairs={{0,1},{1,2},{2,3},{3,4},{4,5},{5,6},{6,7},{7,0},{8,9},{9,10},{10,1... | collective-permute-start | bytes 2359304 | tf_op jit(solution)/shard_map/ppermute | solution.py:68
  95.6 67.9 %copy-start.3 = (bf16[8,128,512]{2,1,0:T(8,128)(2,1)}, bf16[8,128,512]{2,1,0:T(8,128)(2,1)S(1)}, u32[]{:S(2)}) copy-start(bf16[8,128,512]{2,1,0:T(8,128)(2,1)S(1)} %broadcast_select_fusion.1) | copy-start | bytes 3145732
  106.2 28.2 %collective-permute-start.3 = (bf16[24,8192]{1,0:T(8,128)(2,1)S(1)}, bf16[24,8192]{1,0:T(8,128)(2,1)S(1)}, u32[]{:S(2)}, u32[]{:S(2)}) collective-permute-start(bf16[24,8192]{1,0:T(8,128)(2,1)S(1)} %slice.30), channel_id=1, source_target_pairs={{0,7},{1,0},{2,1},{3,2},{4,3},{5,4},{6,5},{7,6},{8,15},{9,8},{10,9... | collective-permute-start | bytes 1179656 | tf_op jit(solution)/shard_map/ppermute | solution.py:71
  109.5 24.9 %collective-permute-start.7 = (bf16[24,8192]{1,0:T(8,128)(2,1)S(1)}, bf16[24,8192]{1,0:T(8,128)(2,1)S(1)}, u32[]{:S(2)}, u32[]{:S(2)}) collective-permute-start(bf16[24,8192]{1,0:T(8,128)(2,1)S(1)} %slice.31), channel_id=1, source_target_pairs={{0,1},{1,2},{2,3},{3,4},{4,5},{5,6},{6,7},{7,0},{8,9},{9,10},{10,1... | collective-permute-start | bytes 1179656 | tf_op jit(solution)/shard_map/ppermute | solution.py:72
  117.0 34.0 %collective-permute-start.11 = (bf16[48,8192]{1,0:T(8,128)(2,1)}, bf16[48,8192]{1,0:T(8,128)(2,1)S(1)}, u32[]{:S(2)}, u32[]{:S(2)}) collective-permute-start(bf16[48,8192]{1,0:T(8,128)(2,1)} %collective-permute-done.10), channel_id=1, source_target_pairs={{0,7},{1,0},{2,1},{3,2},{4,3},{5,4},{6,5},{7,6},{8,15},{9,8},{10,9... | collective-permute-start | bytes 2359304 | tf_op jit(solution)/shard_map/ppermute | solution.py:67
  123.2 31.1 %collective-permute-start.15 = (bf16[48,8192]{1,0:T(8,128)(2,1)}, bf16[48,8192]{1,0:T(8,128)(2,1)S(1)}, u32[]{:S(2)}, u32[]{:S(2)}) collective-permute-start(bf16[48,8192]{1,0:T(8,128)(2,1)} %collective-permute-done.14), channel_id=1, source_target_pairs={{0,1},{1,2},{2,3},{3,4},{4,5},{5,6},{6,7},{7,0},{8,9},{9,10},{10,1... | collective-permute-start | bytes 2359304 | tf_op jit(solution)/shard_map/ppermute | solution.py:68
  151.1 8.6 %collective-permute-start.12 = (bf16[24,8192]{1,0:T(8,128)(2,1)S(1)}, bf16[24,8192]{1,0:T(8,128)(2,1)S(1)}, u32[]{:S(2)}, u32[]{:S(2)}) collective-permute-start(bf16[24,8192]{1,0:T(8,128)(2,1)S(1)} %slice.32), channel_id=1, source_target_pairs={{0,7},{1,0},{2,1},{3,2},{4,3},{5,4},{6,5},{7,6},{8,15},{9,8},{10,9... | collective-permute-start | bytes 1179656 | tf_op jit(solution)/shard_map/ppermute | solution.py:71
  154.4 9.1 %collective-permute-start.16 = (bf16[24,8192]{1,0:T(8,128)(2,1)S(1)}, bf16[24,8192]{1,0:T(8,128)(2,1)S(1)}, u32[]{:S(2)}, u32[]{:S(2)}) collective-permute-start(bf16[24,8192]{1,0:T(8,128)(2,1)S(1)} %slice.33), channel_id=1, source_target_pairs={{0,1},{1,2},{2,3},{3,4},{4,5},{5,6},{6,7},{7,0},{8,9},{9,10},{10,1... | collective-permute-start | bytes 1179656 | tf_op jit(solution)/shard_map/ppermute | solution.py:72
  164.3 21.0 %collective-permute-start.17 = (f32[768,64]{0,1:T(8,128)S(1)}, f32[768,64]{0,1:T(8,128)S(1)}, u32[]{:S(2)}, u32[]{:S(2)}) collective-permute-start(f32[768,64]{0,1:T(8,128)S(1)} %copy.25), channel_id=1, source_target_pairs={{0,1},{1,0},{2,3},{3,2},{4,5},{5,4},{6,7},{7,6},{8,9},{9,8},{10,11... | collective-permute-start | bytes 589832 | tf_op jit(solution)/shard_map/ppermute | solution.py:20
  185.2 8.8 %collective-permute-start.18 = (f32[768,64]{0,1:T(8,128)S(1)}, f32[768,64]{0,1:T(8,128)S(1)}, u32[]{:S(2)}, u32[]{:S(2)}) collective-permute-start(f32[768,64]{0,1:T(8,128)S(1)} %add.443), channel_id=1, source_target_pairs={{0,2},{1,3},{2,0},{3,1},{4,6},{5,7},{6,4},{7,5},{8,10},{9,11},{10,... | collective-permute-start | bytes 589832 | tf_op jit(solution)/shard_map/ppermute | solution.py:20
  194.0 10.6 %collective-permute-start.19 = (f32[768,64]{0,1:T(8,128)S(1)}, f32[768,64]{0,1:T(8,128)S(1)}, u32[]{:S(2)}, u32[]{:S(2)}) collective-permute-start(f32[768,64]{0,1:T(8,128)S(1)} %add.444), channel_id=1, source_target_pairs={{0,4},{1,5},{2,6},{3,7},{4,0},{5,1},{6,2},{7,3},{8,12},{9,13},{10,... | collective-permute-start | bytes 589832 | tf_op jit(solution)/shard_map/ppermute | solution.py:20
  204.6 7.3 %collective-permute-start.20 = (f32[768,64]{0,1:T(8,128)S(1)}, f32[768,64]{0,1:T(8,128)S(1)}, u32[]{:S(2)}, u32[]{:S(2)}) collective-permute-start(f32[768,64]{0,1:T(8,128)S(1)} %add.445), channel_id=1, source_target_pairs={{0,8},{1,9},{2,10},{3,11},{4,12},{5,13},{6,14},{7,15},{8,0},{9,1},... | collective-permute-start | bytes 589832 | tf_op jit(solution)/shard_map/ppermute | solution.py:20
  (11 other events, 104.2 us)

commit v4 on v3

--- a/solution.py
+++ b/solution.py
@@ -79,21 +79,21 @@
 
     tenant_ids = jnp.arange(tenants, dtype=jnp.int32)
 
-    def piece_work(piece, piece_half, step):
-        first_row = (piece_half * ring + (ring_at + step) % ring) * shard_rows
-        positions = first_row + jnp.arange(shard_rows, dtype=jnp.int32)
-        tenant_index = jnp.sum((positions[:, None] >= block_ends[None, :]).astype(jnp.int32), axis=1)
-        masks = tenant_index[:, None] == tenant_ids[None, :]
-        base = jnp.dot(piece, q_weight, preferred_element_type=jnp.float32)
-        cols = lax.dynamic_slice_in_dim(piece, width_start, local_width, 1)
-        wide = lax.dot_general(
-            cols, down_flat, (((1,), (1,)), ((), ())), preferred_element_type=jnp.float32
-        ).reshape(shard_rows, tenants, rank_size)
-        low = jnp.sum(jnp.where(masks[:, :, None], wide, jnp.zeros((), jnp.float32)), axis=1)
-        return base, low
-
-    own_work = [piece_work(p, half, k) for k, p in enumerate(own_pieces)]
-    partner_work = [piece_work(p, 1 - half, k) for k, p in enumerate(partner_pieces)]
+    arrivals = [
+        [("own", 0)],
+        [("own", 1), ("own", ring - 1), ("partner", 0)],
+    ]
+    for step in range(2, ring // 2):
+        arrivals.append([("own", step), ("own", ring - step), ("partner", step - 1), ("partner", ring - step + 1)])
+    arrivals.append([("own", ring // 2), ("partner", ring // 2 - 1), ("partner", ring // 2 + 1)])
+    arrivals.append([("partner", ring // 2)])
+    pieces = {"own": own_pieces, "partner": partner_pieces}
+    base_of = {"own": [None] * ring, "partner": [None] * ring}
+    for batch in arrivals:
+        stacked = jnp.concatenate([pieces[side][k] for side, k in batch], axis=0)
+        product = jnp.dot(stacked, q_weight, preferred_element_type=jnp.float32)
+        for i, (side, k) in enumerate(batch):
+            base_of[side][k] = product[i * shard_rows:(i + 1) * shard_rows]
 
     def to_group_order(own_list, partner_list):
         def roll(stacked):
@@ -106,11 +106,18 @@
         )
         return ordered.reshape((group_rows,) + own_list[0].shape[1:])
 
-    base_projection = to_group_order([w[0] for w in own_work], [w[0] for w in partner_work])
-    partial_low = to_group_order([w[1] for w in own_work], [w[1] for w in partner_work])
+    base_projection = to_group_order(base_of["own"], base_of["partner"])
+
+    local_cols = lax.all_to_all(tokens, "tensor", 1, 0, tiled=True)
+    wide_part = lax.dot_general(
+        local_cols, down_flat, (((1,), (1,)), ((), ())), preferred_element_type=jnp.float32
+    ).reshape(group_rows, tenants, rank_size)
     positions = jnp.arange(group_rows, dtype=jnp.int32)
     tenant_index = jnp.sum((positions[:, None] >= block_ends[None, :]).astype(jnp.int32), axis=1)
     tenant_masks = tenant_index[:, None] == tenant_ids[None, :]
+    partial_low = jnp.sum(
+        jnp.where(tenant_masks[:, :, None], wide_part, jnp.zeros((), jnp.float32)), axis=1
+    )
     low_rank = tensor_sum(partial_low, members).astype(jnp.bfloat16)
     low_wide = jnp.where(
         tenant_masks[:, :, None], low_rank[:, None, :], jnp.zeros((), jnp.bfloat16)

time: 215 us -> 210 us (0.977)
  matrix products: 78.3 us -> 27.2 us
  waiting for transfers between devices: 68.4 us -> 102 us
  starting transfers between devices: 43.6 us -> 68.8 us
  local copies, waits for them, and re-layouts: 18 us -> 7.82 us
    dot_general x32 -> x7, matrix products: 76.8 us -> 25.7 us  [the longest x6 23.9 us: on_device(): product = jnp.dot(stacked, q_weight, preferred_element_type=jnp.float32)]
    ppermute x6, waiting for transfers between devices: 0.02 us -> 31.5 us  [ring_pieces(): left = lax.ppermute(left, 'tensor', from_left)]
    ppermute x4, waiting for transfers between devices: 16.9 us -> 46.1 us  [tensor_sum(): value = value + lax.ppermute(value, 'tensor', pairs)]
    ppermute x6, waiting for transfers between devices: 26.3 us -> 0.02 us  [ring_pieces(): right = lax.ppermute(right, 'tensor', from_right)]
    ppermute x1, waiting for transfers between devices: 19.1 us -> 3.45 us  [on_device(): partner = lax.ppermute(tokens, 'tensor', swap)]
    all_to_all x1, waiting for transfers between devices: 0.01 us -> 12.7 us  [on_device(): recv = lax.all_to_all(send, 'dp', 0, 0, tiled=True)]
    all_to_all x0 -> x1, starting transfers between devices: none -> 11 us  [on_device(): local_cols = lax.all_to_all(tokens, 'tensor', 1, 0, tiled=True)]
    unnamed x73 -> x38, local copies, waits for them, and re-layouts: 9.96 us -> 1.69 us
  transfers between devices with their start and end apart: 22 -> 23, of which waited for: 8 -> 9; matrix products, arithmetic and copies ran while one was open for 46% -> 14% of each run, Pallas kernels for 0% -> 0%
where the time goes in v4:
time: 210 us
  waiting for transfers between devices  102 us (49%)
  starting transfers between devices  68.8 us (33%)
  matrix products  27.2 us (13%)
  local copies, waits for them, and re-layouts  7.82 us (4%)
  other arithmetic  3.83 us (2%)
    ppermute x4, waiting for transfers between devices, tensor_sum(): value = value + lax.ppermute(value, 'tensor', pairs)  46.1 us
    ppermute x6, waiting for transfers between devices, ring_pieces(): left = lax.ppermute(left, 'tensor', from_left)  31.5 us
    dot_general x6, matrix products, on_device(): product = jnp.dot(stacked, q_weight, preferred_element_type=jnp.float32)  23.9 us
    ppermute x6, starting transfers between devices, ring_pieces(): right = lax.ppermute(right, 'tensor', from_right)  21.7 us
    all_to_all x1, waiting for transfers between devices, on_device(): recv = lax.all_to_all(send, 'dp', 0, 0, tiled=True)  12.7 us
    ppermute x4, starting transfers between devices, tensor_sum(): value = value + lax.ppermute(value, 'tensor', pairs)  12 us
    all_to_all x1, starting transfers between devices, on_device(): local_cols = lax.all_to_all(tokens, 'tensor', 1, 0, tiled=True)  11 us
    ppermute x2, starting transfers between devices, ring_pieces(): far_left = lax.ppermute(left[cut:], 'tensor', from_left)  7.62 us
  transfers between devices with their start and end apart: 23, of which 9 were waited for; matrix products, arithmetic and copies ran while one was open for 14% of the time, Pallas kernels for 0%

profile of v4, /device:TPU:2, one launch (start us, length us, event | category | flops | bytes accessed | tf_op | source)
XLA Modules:
  0.0 209.7 jit_solution(11743922650001378935)
XLA Ops:
  4.8 6.0 %all-to-all-start = ((bf16[16,128,512]{2,1,0:T(8,128)(2,1)}), bf16[16,128,512]{2,1,0:T(8,128)(2,1)S(1)}, u32[]{:S(2)}, u32[]{:S(2)}) async-start(bf16[16,128,512]{2,1,0:T(8,128)(2,1)} %broadcast_select_fusion), calls=%async_computation | async-start | bytes 4194304 | tf_op jit(solution)/shard_map/all_to_all | solution.py:42
  15.7 3.9 %collective-permute-start = (bf16[48,8192]{1,0:T(8,128)(2,1)S(1)}, bf16[48,8192]{1,0:T(8,128)(2,1)}, u32[]{:S(2)}, u32[]{:S(2)}) collective-permute-start(bf16[48,8192]{1,0:T(8,128)(2,1)S(1)} %copy-done.2), channel_id=1, source_target_pairs={{0,7},{1,0},{2,1},{3,2},{4,3},{5,4},{6,5},{7,6},{8,15},{9,8},{10,9... | collective-permute-start | bytes 2359304 | tf_op jit(solution)/shard_map/ppermute | solution.py:67
  21.1 5.6 %constant_dynamic-update-slice_fusion.1 = (f32[16,48,512]{2,1,0:T(8,128)}, f32[1,48,512]{2,1,0:T(8,128)S(1)}) fusion(bf16[48,8192]{1,0:T(8,128)(2,1)S(1)} %copy-done.2, bf16[8192,512]{1,0:T(8,128)(2,1)} %param.8), kind=kOutput, calls=%fused_computation.98 | convolution fusion | flops 402653184 | bytes 9371648 | tf_op jit(solution)/shard_map/dot_general | solution.py:94
  26.6 12.7 %all-to-all-done = bf16[16,128,512]{2,1,0:T(8,128)(2,1)S(1)} async-done(((bf16[16,128,512]{2,1,0:T(8,128)(2,1)}), bf16[16,128,512]{2,1,0:T(8,128)(2,1)S(1)}, u32[]{:S(2)}, u32[]{:S(2)}) %all-to-all-start) | async-done | bytes 2097184 | tf_op jit(solution)/shard_map/all_to_all | solution.py:42
  39.3 11.0 %all-to-all-start.1 = ((bf16[48,16,512]{2,0,1:T(8,128)(2,1)}), bf16[48,16,512]{2,0,1:T(8,128)(2,1)}, u32[]{:S(2)}, u32[]{:S(2)}) async-start(bf16[48,16,512]{2,0,1:T(8,128)(2,1)} %bitcast.137), calls=%async_computation.1 | async-start | bytes 1572864 | tf_op jit(solution)/shard_map/all_to_all | solution.py:111
  50.8 3.5 %collective-permute-done.2 = bf16[48,8192]{1,0:T(8,128)(2,1)} collective-permute-done((bf16[48,8192]{1,0:T(8,128)(2,1)S(1)}, bf16[48,8192]{1,0:T(8,128)(2,1)}, u32[]{:S(2)}, u32[]{:S(2)}) %collective-permute-start.2) | collective-permute-done | bytes 786464 | tf_op jit(solution)/shard_map/ppermute | solution.py:76
  56.6 4.9 %collective-permute-start.5 = (bf16[48,8192]{1,0:T(8,128)(2,1)}, bf16[48,8192]{1,0:T(8,128)(2,1)}, u32[]{:S(2)}, u32[]{:S(2)}) collective-permute-start(bf16[48,8192]{1,0:T(8,128)(2,1)} %collective-permute-done.2), channel_id=1, source_target_pairs={{0,7},{1,0},{2,1},{3,2},{4,3},{5,4},{6,5},{7,6},{8,15},{9,8},{10,9... | collective-permute-start | bytes 2359304 | tf_op jit(solution)/shard_map/ppermute | solution.py:67
  61.5 3.2 %collective-permute-start.3 = (bf16[48,8192]{1,0:T(8,128)(2,1)}, bf16[48,8192]{1,0:T(8,128)(2,1)}, u32[]{:S(2)}, u32[]{:S(2)}) collective-permute-start(bf16[48,8192]{1,0:T(8,128)(2,1)} %collective-permute-done), channel_id=1, source_target_pairs={{0,7},{1,0},{2,1},{3,2},{4,3},{5,4},{6,5},{7,6},{8,15},{9,8},{10,9... | collective-permute-start | bytes 2359304 | tf_op jit(solution)/shard_map/ppermute | solution.py:67
  64.7 5.5 %fusion.16 = f32[144,512]{1,0:T(8,128)S(1)} fusion(bf16[8192,512]{1,0:T(8,128)(2,1)} %param.8, bf16[48,8192]{1,0:T(8,128)(2,1)} %collective-permute-done.2, bf16[48,8192]{1,0:T(8,128)(2,1)} %collective-permute-done.1, bf16[48,8192]{1,0:T(8,128)(2,1)} %collective-permute-done), kind=kOutput, calls=%fused_computation.19 | convolution fusion | flops 1215037440 | bytes 11042816 | tf_op jit(solution)/shard_map/dot_general | solution.py:94
  70.8 17.8 %collective-permute-done.6 = bf16[48,8192]{1,0:T(8,128)(2,1)} collective-permute-done((bf16[48,8192]{1,0:T(8,128)(2,1)}, bf16[48,8192]{1,0:T(8,128)(2,1)}, u32[]{:S(2)}, u32[]{:S(2)}) %collective-permute-start.6) | collective-permute-done | bytes 786464 | tf_op jit(solution)/shard_map/ppermute | solution.py:68
  88.7 3.2 %collective-permute-start.9 = (bf16[48,8192]{1,0:T(8,128)(2,1)}, bf16[48,8192]{1,0:T(8,128)(2,1)}, u32[]{:S(2)}, u32[]{:S(2)}) collective-permute-start(bf16[48,8192]{1,0:T(8,128)(2,1)} %collective-permute-done.5), channel_id=1, source_target_pairs={{0,7},{1,0},{2,1},{3,2},{4,3},{5,4},{6,5},{7,6},{8,15},{9,8},{10,9... | collective-permute-start | bytes 2359304 | tf_op jit(solution)/shard_map/ppermute | solution.py:67
  91.9 13.6 %collective-permute-done.4 = bf16[48,8192]{1,0:T(8,128)(2,1)} collective-permute-done((bf16[48,8192]{1,0:T(8,128)(2,1)}, bf16[48,8192]{1,0:T(8,128)(2,1)}, u32[]{:S(2)}, u32[]{:S(2)}) %collective-permute-start.4) | collective-permute-done | bytes 786464 | tf_op jit(solution)/shard_map/ppermute | solution.py:68
  105.5 3.2 %collective-permute-start.7 = (bf16[48,8192]{1,0:T(8,128)(2,1)}, bf16[48,8192]{1,0:T(8,128)(2,1)}, u32[]{:S(2)}, u32[]{:S(2)}) collective-permute-start(bf16[48,8192]{1,0:T(8,128)(2,1)} %collective-permute-done.3), channel_id=1, source_target_pairs={{0,7},{1,0},{2,1},{3,2},{4,3},{5,4},{6,5},{7,6},{8,15},{9,8},{10,9... | collective-permute-start | bytes 2359304 | tf_op jit(solution)/shard_map/ppermute | solution.py:67
  112.2 6.3 %fusion = f32[192,512]{1,0:T(8,128)S(1)} fusion(bf16[8192,512]{1,0:T(8,128)(2,1)} %param.8, bf16[48,8192]{1,0:T(8,128)(2,1)} %collective-permute-done.6, bf16[48,8192]{1,0:T(8,128)(2,1)} %collective-permute-done.5, bf16[48,8192]{1,0:T(8,128)(2,1)} %collective-permute-done.4, bf16[48,8192]{1,0:T(8,128)(2,1)} %collective-permute-done.3), kind=kOutput, calls=%fused_computation.3 | convolution fusion | flops 1623195648 | bytes 11927552 | tf_op jit(solution)/shard_map/dot_general | solution.py:94
  118.6 22.6 %collective-permute-done.17 = f32[768,64]{0,1:T(8,128)S(1)} collective-permute-done((f32[768,64]{0,1:T(8,128)S(1)}, f32[768,64]{0,1:T(8,128)S(1)}, u32[]{:S(2)}, u32[]{:S(2)}) %collective-permute-start.17) | collective-permute-done | bytes 196640 | tf_op jit(solution)/shard_map/ppermute | solution.py:20
  146.1 3.1 %collective-permute-start.11 = (bf16[24,8192]{1,0:T(8,128)(2,1)S(1)}, bf16[24,8192]{1,0:T(8,128)(2,1)S(1)}, u32[]{:S(2)}, u32[]{:S(2)}) collective-permute-start(bf16[24,8192]{1,0:T(8,128)(2,1)S(1)} %slice.89), channel_id=1, source_target_pairs={{0,7},{1,0},{2,1},{3,2},{4,3},{5,4},{6,5},{7,6},{8,15},{9,8},{10,9... | collective-permute-start | bytes 1179656 | tf_op jit(solution)/shard_map/ppermute | solution.py:71
  149.2 3.2 %collective-permute-start.13 = (bf16[48,8192]{1,0:T(8,128)(2,1)}, bf16[48,8192]{1,0:T(8,128)(2,1)S(1)}, u32[]{:S(2)}, u32[]{:S(2)}) collective-permute-start(bf16[48,8192]{1,0:T(8,128)(2,1)} %collective-permute-done.9), channel_id=1, source_target_pairs={{0,7},{1,0},{2,1},{3,2},{4,3},{5,4},{6,5},{7,6},{8,15},{9,8},{10,9... | collective-permute-start | bytes 2359304 | tf_op jit(solution)/shard_map/ppermute | solution.py:67
  152.5 5.9 %collective-permute-start.19 = (f32[768,64]{0,1:T(8,128)S(1)}, f32[768,64]{0,1:T(8,128)S(1)}, u32[]{:S(2)}, u32[]{:S(2)}) collective-permute-start(f32[768,64]{0,1:T(8,128)S(1)} %add.90), channel_id=1, source_target_pairs={{0,4},{1,5},{2,6},{3,7},{4,0},{5,1},{6,2},{7,3},{8,12},{9,13},{10,... | collective-permute-start | bytes 589832 | tf_op jit(solution)/shard_map/ppermute | solution.py:20
  158.3 3.6 %fusion.8 = f32[192,512]{1,0:T(8,128)S(1)} fusion(bf16[8192,512]{1,0:T(8,128)(2,1)S(1)} %bitcast.134, bf16[48,8192]{1,0:T(8,128)(2,1)} %collective-permute-done.10, bf16[48,8192]{1,0:T(8,128)(2,1)} %collective-permute-done.9, bf16[48,8192]{1,0:T(8,128)(2,1)} %collective-permute-done.8, bf16[48,8192]{1,0:T(8,128)(2,1)} %collective-permute-done.7), kind=kOutput, calls=%fused_computation.11 | convolution fusion | flops 1623195648 | bytes 11927552 | tf_op jit(solution)/shard_map/dot_general | solution.py:94
  162.0 19.5 %collective-permute-done.19 = f32[768,64]{0,1:T(8,128)S(1)} collective-permute-done((f32[768,64]{0,1:T(8,128)S(1)}, f32[768,64]{0,1:T(8,128)S(1)}, u32[]{:S(2)}, u32[]{:S(2)}) %collective-permute-start.19) | collective-permute-done | bytes 196640 | tf_op jit(solution)/shard_map/ppermute | solution.py:20
  181.5 3.5 %collective-permute-start.20 = (f32[768,64]{0,1:T(8,128)S(1)}, f32[768,64]{0,1:T(8,128)S(1)}, u32[]{:S(2)}, u32[]{:S(2)}) collective-permute-start(f32[768,64]{0,1:T(8,128)S(1)} %add.91), channel_id=1, source_target_pairs={{0,8},{1,9},{2,10},{3,11},{4,12},{5,13},{6,14},{7,15},{8,0},{9,1},... | collective-permute-start | bytes 589832 | tf_op jit(solution)/shard_map/ppermute | solution.py:20
  185.1 4.0 %collective-permute-done.20 = f32[768,64]{0,1:T(8,128)S(1)} collective-permute-done((f32[768,64]{0,1:T(8,128)S(1)}, f32[768,64]{0,1:T(8,128)S(1)}, u32[]{:S(2)}, u32[]{:S(2)}) %collective-permute-start.20) | collective-permute-done | bytes 196640 | tf_op jit(solution)/shard_map/ppermute | solution.py:20
  190.7 7.4 %collective-permute-start.16 = (bf16[24,8192]{1,0:T(8,128)(2,1)S(1)}, bf16[24,8192]{1,0:T(8,128)(2,1)S(1)}, u32[]{:S(2)}, u32[]{:S(2)}) collective-permute-start(bf16[24,8192]{1,0:T(8,128)(2,1)S(1)} %slice.100), channel_id=1, source_target_pairs={{0,1},{1,2},{2,3},{3,4},{4,5},{5,6},{6,7},{7,0},{8,9},{9,10},{10,1... | collective-permute-start | bytes 1179656 | tf_op jit(solution)/shard_map/ppermute | solution.py:72
  198.2 5.5 %collective-permute-done.16 = bf16[24,8192]{1,0:T(8,128)(2,1)S(1)} collective-permute-done((bf16[24,8192]{1,0:T(8,128)(2,1)S(1)}, bf16[24,8192]{1,0:T(8,128)(2,1)S(1)}, u32[]{:S(2)}, u32[]{:S(2)}) %collective-permute-start.16) | collective-permute-done | bytes 393248 | tf_op jit(solution)/shard_map/ppermute | solution.py:72
  (106 shorter events, 30.4 us)
Async XLA Ops:
  4.8 34.5 %all-to-all-start = ((bf16[16,128,512]{2,1,0:T(8,128)(2,1)}), bf16[16,128,512]{2,1,0:T(8,128)(2,1)S(1)}, u32[]{:S(2)}, u32[]{:S(2)}) async-start(bf16[16,128,512]{2,1,0:T(8,128)(2,1)} %broadcast_select_fusion), calls=%async_computation | async-start | bytes 4194304 | tf_op jit(solution)/shard_map/all_to_all | solution.py:42
  10.8 43.5 %collective-permute-start.2 = (bf16[48,8192]{1,0:T(8,128)(2,1)S(1)}, bf16[48,8192]{1,0:T(8,128)(2,1)}, u32[]{:S(2)}, u32[]{:S(2)}) collective-permute-start(bf16[48,8192]{1,0:T(8,128)(2,1)S(1)} %copy-done.2), channel_id=1, source_target_pairs={{0,8},{1,9},{2,10},{3,11},{4,12},{5,13},{6,14},{7,15},{8,0},{9,1},... | collective-permute-start | bytes 2359304 | tf_op jit(solution)/shard_map/ppermute | solution.py:76
  13.8 47.7 %collective-permute-start.1 = (bf16[48,8192]{1,0:T(8,128)(2,1)S(1)}, bf16[48,8192]{1,0:T(8,128)(2,1)}, u32[]{:S(2)}, u32[]{:S(2)}) collective-permute-start(bf16[48,8192]{1,0:T(8,128)(2,1)S(1)} %copy-done.2), channel_id=1, source_target_pairs={{0,1},{1,2},{2,3},{3,4},{4,5},{5,6},{6,7},{7,0},{8,9},{9,10},{10,1... | collective-permute-start | bytes 2359304 | tf_op jit(solution)/shard_map/ppermute | solution.py:68
  15.7 45.8 %collective-permute-start = (bf16[48,8192]{1,0:T(8,128)(2,1)S(1)}, bf16[48,8192]{1,0:T(8,128)(2,1)}, u32[]{:S(2)}, u32[]{:S(2)}) collective-permute-start(bf16[48,8192]{1,0:T(8,128)(2,1)S(1)} %copy-done.2), channel_id=1, source_target_pairs={{0,7},{1,0},{2,1},{3,2},{4,3},{5,4},{6,5},{7,6},{8,15},{9,8},{10,9... | collective-permute-start | bytes 2359304 | tf_op jit(solution)/shard_map/ppermute | solution.py:67
  39.3 70.9 %all-to-all-start.1 = ((bf16[48,16,512]{2,0,1:T(8,128)(2,1)}), bf16[48,16,512]{2,0,1:T(8,128)(2,1)}, u32[]{:S(2)}, u32[]{:S(2)}) async-start(bf16[48,16,512]{2,0,1:T(8,128)(2,1)} %bitcast.137), calls=%async_computation.1 | async-start | bytes 1572864 | tf_op jit(solution)/shard_map/all_to_all | solution.py:111
  54.3 34.4 %collective-permute-start.6 = (bf16[48,8192]{1,0:T(8,128)(2,1)}, bf16[48,8192]{1,0:T(8,128)(2,1)}, u32[]{:S(2)}, u32[]{:S(2)}) collective-permute-start(bf16[48,8192]{1,0:T(8,128)(2,1)} %collective-permute-done.2), channel_id=1, source_target_pairs={{0,1},{1,2},{2,3},{3,4},{4,5},{5,6},{6,7},{7,0},{8,9},{9,10},{10,1... | collective-permute-start | bytes 2359304 | tf_op jit(solution)/shard_map/ppermute | solution.py:68
  56.6 32.1 %collective-permute-start.5 = (bf16[48,8192]{1,0:T(8,128)(2,1)}, bf16[48,8192]{1,0:T(8,128)(2,1)}, u32[]{:S(2)}, u32[]{:S(2)}) collective-permute-start(bf16[48,8192]{1,0:T(8,128)(2,1)} %collective-permute-done.2), channel_id=1, source_target_pairs={{0,7},{1,0},{2,1},{3,2},{4,3},{5,4},{6,5},{7,6},{8,15},{9,8},{10,9... | collective-permute-start | bytes 2359304 | tf_op jit(solution)/shard_map/ppermute | solution.py:67
  61.5 44.1 %collective-permute-start.4 = (bf16[48,8192]{1,0:T(8,128)(2,1)}, bf16[48,8192]{1,0:T(8,128)(2,1)}, u32[]{:S(2)}, u32[]{:S(2)}) collective-permute-start(bf16[48,8192]{1,0:T(8,128)(2,1)} %collective-permute-done.1), channel_id=1, source_target_pairs={{0,1},{1,2},{2,3},{3,4},{4,5},{5,6},{6,7},{7,0},{8,9},{9,10},{10,1... | collective-permute-start | bytes 2359304 | tf_op jit(solution)/shard_map/ppermute | solution.py:68
  61.5 44.1 %collective-permute-start.3 = (bf16[48,8192]{1,0:T(8,128)(2,1)}, bf16[48,8192]{1,0:T(8,128)(2,1)}, u32[]{:S(2)}, u32[]{:S(2)}) collective-permute-start(bf16[48,8192]{1,0:T(8,128)(2,1)} %collective-permute-done), channel_id=1, source_target_pairs={{0,7},{1,0},{2,1},{3,2},{4,3},{5,4},{6,5},{7,6},{8,15},{9,8},{10,9... | collective-permute-start | bytes 2359304 | tf_op jit(solution)/shard_map/ppermute | solution.py:67
  88.7 60.5 %collective-permute-start.10 = (bf16[48,8192]{1,0:T(8,128)(2,1)}, bf16[48,8192]{1,0:T(8,128)(2,1)}, u32[]{:S(2)}, u32[]{:S(2)}) collective-permute-start(bf16[48,8192]{1,0:T(8,128)(2,1)} %collective-permute-done.6), channel_id=1, source_target_pairs={{0,1},{1,2},{2,3},{3,4},{4,5},{5,6},{6,7},{7,0},{8,9},{9,10},{10,1... | collective-permute-start | bytes 2359304 | tf_op jit(solution)/shard_map/ppermute | solution.py:68
  88.7 60.5 %collective-permute-start.9 = (bf16[48,8192]{1,0:T(8,128)(2,1)}, bf16[48,8192]{1,0:T(8,128)(2,1)}, u32[]{:S(2)}, u32[]{:S(2)}) collective-permute-start(bf16[48,8192]{1,0:T(8,128)(2,1)} %collective-permute-done.5), channel_id=1, source_target_pairs={{0,7},{1,0},{2,1},{3,2},{4,3},{5,4},{6,5},{7,6},{8,15},{9,8},{10,9... | collective-permute-start | bytes 2359304 | tf_op jit(solution)/shard_map/ppermute | solution.py:67
  105.5 38.2 %collective-permute-start.8 = (bf16[48,8192]{1,0:T(8,128)(2,1)}, bf16[48,8192]{1,0:T(8,128)(2,1)}, u32[]{:S(2)}, u32[]{:S(2)}) collective-permute-start(bf16[48,8192]{1,0:T(8,128)(2,1)} %collective-permute-done.4), channel_id=1, source_target_pairs={{0,1},{1,2},{2,3},{3,4},{4,5},{5,6},{6,7},{7,0},{8,9},{9,10},{10,1... | collective-permute-start | bytes 2359304 | tf_op jit(solution)/shard_map/ppermute | solution.py:68
  105.5 39.5 %collective-permute-start.7 = (bf16[48,8192]{1,0:T(8,128)(2,1)}, bf16[48,8192]{1,0:T(8,128)(2,1)}, u32[]{:S(2)}, u32[]{:S(2)}) collective-permute-start(bf16[48,8192]{1,0:T(8,128)(2,1)} %collective-permute-done.3), channel_id=1, source_target_pairs={{0,7},{1,0},{2,1},{3,2},{4,3},{5,4},{6,5},{7,6},{8,15},{9,8},{10,9... | collective-permute-start | bytes 2359304 | tf_op jit(solution)/shard_map/ppermute | solution.py:67
  112.0 46.4 %slice-start = ((s8[8388608]{0:T(1024)(128)(4,1)}), s8[4194304]{0:T(1024)(128)(4,1)S(1)}, s32[]{:S(2)}) async-start(s8[8388608]{0:T(1024)(128)(4,1)} %bitcast.133), calls=%async_computation.2 | async-start | bytes 8388608
  112.1 29.0 %collective-permute-start.17 = (f32[768,64]{0,1:T(8,128)S(1)}, f32[768,64]{0,1:T(8,128)S(1)}, u32[]{:S(2)}, u32[]{:S(2)}) collective-permute-start(f32[768,64]{0,1:T(8,128)S(1)} %select_reduce_fusion), channel_id=1, source_target_pairs={{0,1},{1,0},{2,3},{3,2},{4,5},{5,4},{6,7},{7,6},{8,9},{9,8},{10,11... | collective-permute-start | bytes 589832 | tf_op jit(solution)/shard_map/ppermute | solution.py:20
  141.2 11.3 %collective-permute-start.18 = (f32[768,64]{0,1:T(8,128)S(1)}, f32[768,64]{0,1:T(8,128)S(1)}, u32[]{:S(2)}, u32[]{:S(2)}) collective-permute-start(f32[768,64]{0,1:T(8,128)S(1)} %add.89), channel_id=1, source_target_pairs={{0,2},{1,3},{2,0},{3,1},{4,6},{5,7},{6,4},{7,5},{8,10},{9,11},{10,... | collective-permute-start | bytes 589832 | tf_op jit(solution)/shard_map/ppermute | solution.py:20
  144.8 44.4 %collective-permute-start.12 = (bf16[24,8192]{1,0:T(8,128)(2,1)S(1)}, bf16[24,8192]{1,0:T(8,128)(2,1)S(1)}, u32[]{:S(2)}, u32[]{:S(2)}) collective-permute-start(bf16[24,8192]{1,0:T(8,128)(2,1)S(1)} %slice.90), channel_id=1, source_target_pairs={{0,1},{1,2},{2,3},{3,4},{4,5},{5,6},{6,7},{7,0},{8,9},{9,10},{10,1... | collective-permute-start | bytes 1179656 | tf_op jit(solution)/shard_map/ppermute | solution.py:72
  146.1 43.1 %collective-permute-start.11 = (bf16[24,8192]{1,0:T(8,128)(2,1)S(1)}, bf16[24,8192]{1,0:T(8,128)(2,1)S(1)}, u32[]{:S(2)}, u32[]{:S(2)}) collective-permute-start(bf16[24,8192]{1,0:T(8,128)(2,1)S(1)} %slice.89), channel_id=1, source_target_pairs={{0,7},{1,0},{2,1},{3,2},{4,3},{5,4},{6,5},{7,6},{8,15},{9,8},{10,9... | collective-permute-start | bytes 1179656 | tf_op jit(solution)/shard_map/ppermute | solution.py:71
  149.2 40.0 %collective-permute-start.14 = (bf16[48,8192]{1,0:T(8,128)(2,1)}, bf16[48,8192]{1,0:T(8,128)(2,1)S(1)}, u32[]{:S(2)}, u32[]{:S(2)}) collective-permute-start(bf16[48,8192]{1,0:T(8,128)(2,1)} %collective-permute-done.10), channel_id=1, source_target_pairs={{0,1},{1,2},{2,3},{3,4},{4,5},{5,6},{6,7},{7,0},{8,9},{9,10},{10,1... | collective-permute-start | bytes 2359304 | tf_op jit(solution)/shard_map/ppermute | solution.py:68
  149.2 40.0 %collective-permute-start.13 = (bf16[48,8192]{1,0:T(8,128)(2,1)}, bf16[48,8192]{1,0:T(8,128)(2,1)S(1)}, u32[]{:S(2)}, u32[]{:S(2)}) collective-permute-start(bf16[48,8192]{1,0:T(8,128)(2,1)} %collective-permute-done.9), channel_id=1, source_target_pairs={{0,7},{1,0},{2,1},{3,2},{4,3},{5,4},{6,5},{7,6},{8,15},{9,8},{10,9... | collective-permute-start | bytes 2359304 | tf_op jit(solution)/shard_map/ppermute | solution.py:67
  152.5 29.0 %collective-permute-start.19 = (f32[768,64]{0,1:T(8,128)S(1)}, f32[768,64]{0,1:T(8,128)S(1)}, u32[]{:S(2)}, u32[]{:S(2)}) collective-permute-start(f32[768,64]{0,1:T(8,128)S(1)} %add.90), channel_id=1, source_target_pairs={{0,4},{1,5},{2,6},{3,7},{4,0},{5,1},{6,2},{7,3},{8,12},{9,13},{10,... | collective-permute-start | bytes 589832 | tf_op jit(solution)/shard_map/ppermute | solution.py:20
  181.5 7.6 %collective-permute-start.20 = (f32[768,64]{0,1:T(8,128)S(1)}, f32[768,64]{0,1:T(8,128)S(1)}, u32[]{:S(2)}, u32[]{:S(2)}) collective-permute-start(f32[768,64]{0,1:T(8,128)S(1)} %add.91), channel_id=1, source_target_pairs={{0,8},{1,9},{2,10},{3,11},{4,12},{5,13},{6,14},{7,15},{8,0},{9,1},... | collective-permute-start | bytes 589832 | tf_op jit(solution)/shard_map/ppermute | solution.py:20
  190.7 13.1 %collective-permute-start.16 = (bf16[24,8192]{1,0:T(8,128)(2,1)S(1)}, bf16[24,8192]{1,0:T(8,128)(2,1)S(1)}, u32[]{:S(2)}, u32[]{:S(2)}) collective-permute-start(bf16[24,8192]{1,0:T(8,128)(2,1)S(1)} %slice.100), channel_id=1, source_target_pairs={{0,1},{1,2},{2,3},{3,4},{4,5},{5,6},{6,7},{7,0},{8,9},{9,10},{10,1... | collective-permute-start | bytes 1179656 | tf_op jit(solution)/shard_map/ppermute | solution.py:72
  198.1 8.0 %collective-permute-start.15 = (bf16[24,8192]{1,0:T(8,128)(2,1)S(1)}, bf16[24,8192]{1,0:T(8,128)(2,1)S(1)}, u32[]{:S(2)}, u32[]{:S(2)}) collective-permute-start(bf16[24,8192]{1,0:T(8,128)(2,1)S(1)} %slice.99), channel_id=1, source_target_pairs={{0,7},{1,0},{2,1},{3,2},{4,3},{5,4},{6,5},{7,6},{8,15},{9,8},{10,9... | collective-permute-start | bytes 1179656 | tf_op jit(solution)/shard_map/ppermute | solution.py:71
  (7 other events, 107.3 us)

commit v5 on v4

--- a/solution.py
+++ b/solution.py
@@ -42,8 +42,6 @@
     recv = lax.all_to_all(send, "dp", 0, 0, tiled=True)
     my_src = lax.dynamic_index_in_dim(slot_shard, my_group, 0, keepdims=False)
     panels = jnp.take(recv, my_src, axis=0)
-    down_flat = panels[:, :rank_size, :].reshape(tenants * rank_size, local_width)
-    up_flat = panels[:, rank_size:, :].reshape(tenants * rank_size, columns)
 
     tensor_at = lax.axis_index("tensor")
     members = lax.axis_size("tensor")
@@ -60,24 +58,78 @@
     from_right = [(i, (i // ring) * ring + (i % ring - 1) % ring) for i in range(members)]
     from_left = [(i, (i // ring) * ring + (i % ring + 1) % ring) for i in range(members)]
 
-    def ring_pieces(own):
-        pieces = [own] + [None] * (ring - 1)
-        right, left = own, own
-        for step in range(1, ring // 2):
-            right = lax.ppermute(right, "tensor", from_right)
-            left = lax.ppermute(left, "tensor", from_left)
-            pieces[step], pieces[ring - step] = right, left
-        cut = shard_rows // 2
-        far_right = lax.ppermute(right[:cut], "tensor", from_right)
-        far_left = lax.ppermute(left[cut:], "tensor", from_left)
-        pieces[ring // 2] = jnp.concatenate([far_right, far_left], axis=0)
-        return pieces
-
-    partner = lax.ppermute(tokens, "tensor", swap)
-    own_pieces = ring_pieces(tokens)
-    partner_pieces = ring_pieces(partner)
+    def hop(value, pairs):
+        return lax.ppermute(value, "tensor", pairs)
 
     tenant_ids = jnp.arange(tenants, dtype=jnp.int32)
+    positions = jnp.arange(group_rows, dtype=jnp.int32)
+    tenant_index = jnp.sum((positions[:, None] >= block_ends[None, :]).astype(jnp.int32), axis=1)
+    tenant_masks = tenant_index[:, None] == tenant_ids[None, :]
+
+    local_cols = lax.all_to_all(tokens, "tensor", 1, 0, tiled=True)
+
+    def partial_of(cols):
+        wide = lax.dot_general(
+            cols, down_flat, (((1,), (1,)), ((), ())), preferred_element_type=jnp.float32
+        ).reshape(group_rows, tenants, rank_size)
+        return jnp.sum(jnp.where(tenant_masks[:, :, None], wide, jnp.zeros((), jnp.float32)), axis=1)
+
+    sum_steps = [ring]
+    step = ring // 2
+    while step >= 1:
+        sum_steps.append(step)
+        step //= 2
+
+    def sum_step(value, mask):
+        return value + hop(value, [(i, i ^ mask) for i in range(members)])
+
+    own_pieces = [tokens] + [None] * (ring - 1)
+    partner_pieces = [None] * ring
+    cut = shard_rows // 2
+    partner = hop(tokens, swap)
+    own_right = hop(tokens, from_right)
+    own_left = hop(tokens, from_left)
+    partner, own_right, own_left = lax.optimization_barrier((partner, own_right, own_left))
+    own_pieces[1], own_pieces[ring - 1] = own_right, own_left
+    partner_pieces[0] = partner
+    partner_right, partner_left = partner, partner
+    low_sum = None
+    for step in range(2, ring // 2 + 2):
+        moved = []
+        if step < ring // 2:
+            moved += [hop(own_right, from_right), hop(own_left, from_left)]
+        elif step == ring // 2:
+            moved += [hop(own_right[:cut], from_right), hop(own_left[cut:], from_left)]
+        if step - 1 < ring // 2:
+            moved += [hop(partner_right, from_right), hop(partner_left, from_left)]
+        else:
+            moved += [hop(partner_right[:cut], from_right), hop(partner_left[cut:], from_left)]
+        if low_sum is None:
+            extra = (local_cols, panels)
+        else:
+            extra = (sum_step(low_sum, sum_steps.pop(0)),)
+        moved, extra = lax.optimization_barrier((moved, extra))
+        if low_sum is None:
+            local_cols, panels = extra
+            down_flat = panels[:, :rank_size, :].reshape(tenants * rank_size, local_width)
+            up_flat = panels[:, rank_size:, :].reshape(tenants * rank_size, columns)
+            low_sum = partial_of(local_cols)
+        else:
+            low_sum = extra[0]
+        if step < ring // 2:
+            own_right, own_left = moved[0], moved[1]
+            own_pieces[step], own_pieces[ring - step] = own_right, own_left
+            moved = moved[2:]
+        elif step == ring // 2:
+            own_pieces[step] = jnp.concatenate(moved[:2], axis=0)
+            moved = moved[2:]
+        if step - 1 < ring // 2:
+            partner_right, partner_left = moved
+            partner_pieces[step - 1], partner_pieces[ring - step + 1] = partner_right, partner_left
+        else:
+            partner_pieces[ring // 2] = jnp.concatenate(moved, axis=0)
+    for mask in sum_steps:
+        low_sum = sum_step(low_sum, mask)
 
     arrivals = [
         [("own", 0)],
@@ -107,18 +159,7 @@
         return ordered.reshape((group_rows,) + own_list[0].shape[1:])
 
     base_projection = to_group_order(base_of["own"], base_of["partner"])
-
-    local_cols = lax.all_to_all(tokens, "tensor", 1, 0, tiled=True)
-    wide_part = lax.dot_general(
-        local_cols, down_flat, (((1,), (1,)), ((), ())), preferred_element_type=jnp.float32
-    ).reshape(group_rows, tenants, rank_size)
-    positions = jnp.arange(group_rows, dtype=jnp.int32)
-    tenant_index = jnp.sum((positions[:, None] >= block_ends[None, :]).astype(jnp.int32), axis=1)
-    tenant_masks = tenant_index[:, None] == tenant_ids[None, :]
-    partial_low = jnp.sum(
-        jnp.where(tenant_masks[:, :, None], wide_part, jnp.zeros((), jnp.float32)), axis=1
-    )
-    low_rank = tensor_sum(partial_low, members).astype(jnp.bfloat16)
+    low_rank = low_sum.astype(jnp.bfloat16)
     low_wide = jnp.where(
         tenant_masks[:, :, None], low_rank[:, None, :], jnp.zeros((), jnp.bfloat16)
     )

time: 210 us -> 210 us (level)
  local copies, waits for them, and re-layouts: 7.82 us -> 15.9 us
  starting transfers between devices: 68.8 us -> 63.5 us
    unnamed x38 -> x36, local copies, waits for them, and re-layouts: 1.69 us -> 9.97 us
    ppermute x21, starting transfers between devices: 51.8 us -> 46.6 us  [hop(): return lax.ppermute(value, 'tensor', pairs)]
    ppermute x21, waiting for transfers between devices: 88.9 us -> 84.1 us  [hop(): return lax.ppermute(value, 'tensor', pairs)]
    all_to_all x1, waiting for transfers between devices: 0.01 us -> 3.61 us  [on_device(): local_cols = lax.all_to_all(tokens, 'tensor', 1, 0, tiled=True)]
  transfers between devices with their start and end apart: 23 -> 23, of which waited for: 9 -> 12; matrix products, arithmetic and copies ran while one was open for 14% -> 18% of each run, Pallas kernels for 0% -> 0%
where the time goes in v5:
time: 210 us; the launch traced here: 209 us
  waiting for transfers between devices  100 us (48%)
  starting transfers between devices  63.5 us (30%)
  matrix products  25.3 us (12%)
  local copies, waits for them, and re-layouts  15.9 us (8%)
  other arithmetic  3.82 us (2%)
    ppermute x21, waiting for transfers between devices, hop(): return lax.ppermute(value, 'tensor', pairs)  84.1 us
    ppermute x21, starting transfers between devices, hop(): return lax.ppermute(value, 'tensor', pairs)  46.6 us
    dot_general x6, matrix products, on_device(): product = jnp.dot(stacked, q_weight, preferred_element_type=jnp.float32)  21.9 us
    all_to_all x1, waiting for transfers between devices, on_device(): recv = lax.all_to_all(send, 'dp', 0, 0, tiled=True)  12.7 us
    all_to_all x1, starting transfers between devices, on_device(): local_cols = lax.all_to_all(tokens, 'tensor', 1, 0, tiled=True)  11 us
    unnamed x36, local copies, waits for them, and re-layouts  9.97 us
    all_to_all x1, starting transfers between devices, on_device(): recv = lax.all_to_all(send, 'dp', 0, 0, tiled=True)  5.99 us
  transfers between devices with their start and end apart: 23, of which 12 were waited for; matrix products, arithmetic and copies ran while one was open for 18% of the time, Pallas kernels for 0%

profile of v5, /device:TPU:2, one launch (start us, length us, event | category | flops | bytes accessed | tf_op | source)
XLA Modules:
  0.0 209.4 jit_solution(10074561380853633285)
XLA Ops:
  4.8 6.0 %all-to-all-start.1 = ((bf16[16,128,512]{2,1,0:T(8,128)(2,1)}), bf16[16,128,512]{2,1,0:T(8,128)(2,1)S(1)}, u32[]{:S(2)}, u32[]{:S(2)}) async-start(bf16[16,128,512]{2,1,0:T(8,128)(2,1)} %broadcast_select_fusion), calls=%async_computation.1 | async-start | bytes 4194304 | tf_op jit(solution)/shard_map/all_to_all | solution.py:42
  10.8 5.9 %collective-permute-start.1 = (bf16[48,8192]{1,0:T(8,128)(2,1)S(1)}, bf16[48,8192]{1,0:T(8,128)(2,1)}, u32[]{:S(2)}, u32[]{:S(2)}) collective-permute-start(bf16[48,8192]{1,0:T(8,128)(2,1)S(1)} %copy-done.2), channel_id=1, source_target_pairs={{0,7},{1,0},{2,1},{3,2},{4,3},{5,4},{6,5},{7,6},{8,15},{9,8},{10,9... | collective-permute-start | bytes 2359304 | tf_op jit(solution)/shard_map/ppermute | solution.py:62
  16.7 2.9 %collective-permute-start = (bf16[48,8192]{1,0:T(8,128)(2,1)S(1)}, bf16[48,8192]{1,0:T(8,128)(2,1)}, u32[]{:S(2)}, u32[]{:S(2)}) collective-permute-start(bf16[48,8192]{1,0:T(8,128)(2,1)S(1)} %copy-done.2), channel_id=1, source_target_pairs={{0,8},{1,9},{2,10},{3,11},{4,12},{5,13},{6,14},{7,15},{8,0},{9,1},... | collective-permute-start | bytes 2359304 | tf_op jit(solution)/shard_map/ppermute | solution.py:62
  21.1 5.6 %constant_dynamic-update-slice_fusion.1 = (f32[16,48,512]{2,1,0:T(8,128)}, f32[1,48,512]{2,1,0:T(8,128)S(1)}) fusion(bf16[48,8192]{1,0:T(8,128)(2,1)S(1)} %copy-done.2, bf16[8192,512]{1,0:T(8,128)(2,1)} %param.8), kind=kOutput, calls=%fused_computation.100 | convolution fusion | flops 402653184 | bytes 9371648 | tf_op jit(solution)/shard_map/dot_general | solution.py:146
  26.6 12.7 %all-to-all-done.1 = bf16[16,128,512]{2,1,0:T(8,128)(2,1)S(1)} async-done(((bf16[16,128,512]{2,1,0:T(8,128)(2,1)}), bf16[16,128,512]{2,1,0:T(8,128)(2,1)S(1)}, u32[]{:S(2)}, u32[]{:S(2)}) %all-to-all-start.1) | async-done | bytes 2097184 | tf_op jit(solution)/shard_map/all_to_all | solution.py:42
  39.3 11.0 %all-to-all-start = ((bf16[48,16,512]{2,0,1:T(8,128)(2,1)}), bf16[48,16,512]{2,0,1:T(8,128)(2,1)}, u32[]{:S(2)}, u32[]{:S(2)}) async-start(bf16[48,16,512]{2,0,1:T(8,128)(2,1)} %bitcast.133), calls=%async_computation | async-start | bytes 1572864 | tf_op jit(solution)/shard_map/all_to_all | solution.py:69
  50.9 3.4 %collective-permute-done = bf16[48,8192]{1,0:T(8,128)(2,1)} collective-permute-done((bf16[48,8192]{1,0:T(8,128)(2,1)S(1)}, bf16[48,8192]{1,0:T(8,128)(2,1)}, u32[]{:S(2)}, u32[]{:S(2)}) %collective-permute-start) | collective-permute-done | bytes 786464 | tf_op jit(solution)/shard_map/ppermute | solution.py:62
  54.3 2.4 %collective-permute-start.6 = (bf16[48,8192]{1,0:T(8,128)(2,1)}, bf16[48,8192]{1,0:T(8,128)(2,1)}, u32[]{:S(2)}, u32[]{:S(2)}) collective-permute-start(bf16[48,8192]{1,0:T(8,128)(2,1)} %collective-permute-done), channel_id=1, source_target_pairs={{0,1},{1,2},{2,3},{3,4},{4,5},{5,6},{6,7},{7,0},{8,9},{9,10},{10,1... | collective-permute-start | bytes 2359304 | tf_op jit(solution)/shard_map/ppermute | solution.py:62
  56.6 4.9 %collective-permute-start.5 = (bf16[48,8192]{1,0:T(8,128)(2,1)}, bf16[48,8192]{1,0:T(8,128)(2,1)}, u32[]{:S(2)}, u32[]{:S(2)}) collective-permute-start(bf16[48,8192]{1,0:T(8,128)(2,1)} %collective-permute-done), channel_id=1, source_target_pairs={{0,7},{1,0},{2,1},{3,2},{4,3},{5,4},{6,5},{7,6},{8,15},{9,8},{10,9... | collective-permute-start | bytes 2359304 | tf_op jit(solution)/shard_map/ppermute | solution.py:62
  63.5 5.5 %fusion.16 = f32[144,512]{1,0:T(8,128)S(1)} fusion(bf16[8192,512]{1,0:T(8,128)(2,1)} %param.8, bf16[48,8192]{1,0:T(8,128)(2,1)} %collective-permute-done, bf16[48,8192]{1,0:T(8,128)(2,1)} %collective-permute-done.2, bf16[48,8192]{1,0:T(8,128)(2,1)} %collective-permute-done.1), kind=kOutput, calls=%fused_computation.19 | convolution fusion | flops 1215037440 | bytes 11042816 | tf_op jit(solution)/shard_map/dot_general | solution.py:146
  71.1 3.6 %all-to-all-done = bf16[48,16,512]{2,0,1:T(8,128)(2,1)} async-done(((bf16[48,16,512]{2,0,1:T(8,128)(2,1)}), bf16[48,16,512]{2,0,1:T(8,128)(2,1)}, u32[]{:S(2)}, u32[]{:S(2)}) %all-to-all-start) | async-done | bytes 786464 | tf_op jit(solution)/shard_map/all_to_all | solution.py:69
  74.7 28.6 %collective-permute-done.3 = bf16[48,8192]{1,0:T(8,128)(2,1)} collective-permute-done((bf16[48,8192]{1,0:T(8,128)(2,1)}, bf16[48,8192]{1,0:T(8,128)(2,1)}, u32[]{:S(2)}, u32[]{:S(2)}) %collective-permute-start.3) | collective-permute-done | bytes 786464 | tf_op jit(solution)/shard_map/ppermute | solution.py:62
  106.5 3.1 %collective-permute-start.11 = (f32[768,64]{0,1:T(8,128)S(1)}, f32[768,64]{0,1:T(8,128)S(1)}, u32[]{:S(2)}, u32[]{:S(2)}) collective-permute-start(f32[768,64]{0,1:T(8,128)S(1)} %select_reduce_fusion), channel_id=1, source_target_pairs={{0,8},{1,9},{2,10},{3,11},{4,12},{5,13},{6,14},{7,15},{8,0},{9,1},... | collective-permute-start | bytes 589832 | tf_op jit(solution)/shard_map/ppermute | solution.py:62
  111.6 2.7 %collective-permute-start.9 = (bf16[48,8192]{1,0:T(8,128)(2,1)}, bf16[48,8192]{1,0:T(8,128)(2,1)S(1)}, u32[]{:S(2)}, u32[]{:S(2)}) collective-permute-start(bf16[48,8192]{1,0:T(8,128)(2,1)} %collective-permute-done.5), channel_id=1, source_target_pairs={{0,7},{1,0},{2,1},{3,2},{4,3},{5,4},{6,5},{7,6},{8,15},{9,8},{10,9... | collective-permute-start | bytes 2359304 | tf_op jit(solution)/shard_map/ppermute | solution.py:62
  114.3 6.1 %fusion = f32[192,512]{1,0:T(8,128)S(1)} fusion(bf16[8192,512]{1,0:T(8,128)(2,1)} %param.8, bf16[48,8192]{1,0:T(8,128)(2,1)} %collective-permute-done.6, bf16[48,8192]{1,0:T(8,128)(2,1)} %collective-permute-done.5, bf16[48,8192]{1,0:T(8,128)(2,1)} %collective-permute-done.4, bf16[48,8192]{1,0:T(8,128)(2,1)} %collective-permute-done.3), kind=kOutput, calls=%fused_computation.3 | convolution fusion | flops 1623195648 | bytes 11927552 | tf_op jit(solution)/shard_map/dot_general | solution.py:146
  121.1 9.1 %collective-permute-done.7 = bf16[48,8192]{1,0:T(8,128)(2,1)S(1)} collective-permute-done((bf16[48,8192]{1,0:T(8,128)(2,1)}, bf16[48,8192]{1,0:T(8,128)(2,1)S(1)}, u32[]{:S(2)}, u32[]{:S(2)}) %collective-permute-start.7) | collective-permute-done | bytes 786464 | tf_op jit(solution)/shard_map/ppermute | solution.py:62
  130.2 2.7 %collective-permute-done.8 = bf16[48,8192]{1,0:T(8,128)(2,1)S(1)} collective-permute-done((bf16[48,8192]{1,0:T(8,128)(2,1)}, bf16[48,8192]{1,0:T(8,128)(2,1)S(1)}, u32[]{:S(2)}, u32[]{:S(2)}) %collective-permute-start.8) | collective-permute-done | bytes 786464 | tf_op jit(solution)/shard_map/ppermute | solution.py:62
  132.9 12.0 %collective-permute-done.9 = bf16[48,8192]{1,0:T(8,128)(2,1)S(1)} collective-permute-done((bf16[48,8192]{1,0:T(8,128)(2,1)}, bf16[48,8192]{1,0:T(8,128)(2,1)S(1)}, u32[]{:S(2)}, u32[]{:S(2)}) %collective-permute-start.9) | collective-permute-done | bytes 786464 | tf_op jit(solution)/shard_map/ppermute | solution.py:62
  144.9 2.4 %collective-permute-done.10 = bf16[48,8192]{1,0:T(8,128)(2,1)S(1)} collective-permute-done((bf16[48,8192]{1,0:T(8,128)(2,1)}, bf16[48,8192]{1,0:T(8,128)(2,1)S(1)}, u32[]{:S(2)}, u32[]{:S(2)}) %collective-permute-start.10) | collective-permute-done | bytes 786464 | tf_op jit(solution)/shard_map/ppermute | solution.py:62
  147.5 3.2 %collective-permute-start.12 = (bf16[24,8192]{1,0:T(8,128)(2,1)S(1)}, bf16[24,8192]{1,0:T(8,128)(2,1)S(1)}, u32[]{:S(2)}, u32[]{:S(2)}) collective-permute-start(bf16[24,8192]{1,0:T(8,128)(2,1)S(1)} %slice.64), channel_id=1, source_target_pairs={{0,7},{1,0},{2,1},{3,2},{4,3},{5,4},{6,5},{7,6},{8,15},{9,8},{10,9... | collective-permute-start | bytes 1179656 | tf_op jit(solution)/shard_map/ppermute | solution.py:62
  154.5 4.6 %collective-permute-start.16 = (f32[768,64]{0,1:T(8,128)S(1)}, f32[768,64]{0,1:T(8,128)S(1)}, u32[]{:S(2)}, u32[]{:S(2)}) collective-permute-start(f32[768,64]{0,1:T(8,128)S(1)} %add.86), channel_id=1, source_target_pairs={{0,4},{1,5},{2,6},{3,7},{4,0},{5,1},{6,2},{7,3},{8,12},{9,13},{10,... | collective-permute-start | bytes 589832 | tf_op jit(solution)/shard_map/ppermute | solution.py:62
  159.8 22.4 %collective-permute-done.16 = f32[768,64]{0,1:T(8,128)S(1)} collective-permute-done((f32[768,64]{0,1:T(8,128)S(1)}, f32[768,64]{0,1:T(8,128)S(1)}, u32[]{:S(2)}, u32[]{:S(2)}) %collective-permute-start.16) | collective-permute-done | bytes 196640 | tf_op jit(solution)/shard_map/ppermute | solution.py:62
  183.1 5.5 %collective-permute-start.18 = (bf16[24,8192]{1,0:T(8,128)(2,1)S(1)}, bf16[24,8192]{1,0:T(8,128)(2,1)S(1)}, u32[]{:S(2)}, u32[]{:S(2)}) collective-permute-start(bf16[24,8192]{1,0:T(8,128)(2,1)S(1)} %slice.75), channel_id=1, source_target_pairs={{0,1},{1,2},{2,3},{3,4},{4,5},{5,6},{6,7},{7,0},{8,9},{9,10},{10,1... | collective-permute-start | bytes 1179656 | tf_op jit(solution)/shard_map/ppermute | solution.py:62
  196.7 5.3 %collective-permute-start.20 = (f32[768,64]{0,1:T(8,128)S(1)}, f32[768,64]{0,1:T(8,128)S(1)}, u32[]{:S(2)}, u32[]{:S(2)}) collective-permute-start(f32[768,64]{0,1:T(8,128)S(1)} %add.91), channel_id=1, source_target_pairs={{0,1},{1,0},{2,3},{3,2},{4,5},{5,4},{6,7},{7,6},{8,9},{9,8},{10,11... | collective-permute-start | bytes 589832 | tf_op jit(solution)/shard_map/ppermute | solution.py:62
  (102 shorter events, 37.6 us)
Async XLA Ops:
  4.8 34.5 %all-to-all-start.1 = ((bf16[16,128,512]{2,1,0:T(8,128)(2,1)}), bf16[16,128,512]{2,1,0:T(8,128)(2,1)S(1)}, u32[]{:S(2)}, u32[]{:S(2)}) async-start(bf16[16,128,512]{2,1,0:T(8,128)(2,1)} %broadcast_select_fusion), calls=%async_computation.1 | async-start | bytes 4194304 | tf_op jit(solution)/shard_map/all_to_all | solution.py:42
  10.8 40.1 %collective-permute-start.1 = (bf16[48,8192]{1,0:T(8,128)(2,1)S(1)}, bf16[48,8192]{1,0:T(8,128)(2,1)}, u32[]{:S(2)}, u32[]{:S(2)}) collective-permute-start(bf16[48,8192]{1,0:T(8,128)(2,1)S(1)} %copy-done.2), channel_id=1, source_target_pairs={{0,7},{1,0},{2,1},{3,2},{4,3},{5,4},{6,5},{7,6},{8,15},{9,8},{10,9... | collective-permute-start | bytes 2359304 | tf_op jit(solution)/shard_map/ppermute | solution.py:62
  16.7 37.6 %collective-permute-start = (bf16[48,8192]{1,0:T(8,128)(2,1)S(1)}, bf16[48,8192]{1,0:T(8,128)(2,1)}, u32[]{:S(2)}, u32[]{:S(2)}) collective-permute-start(bf16[48,8192]{1,0:T(8,128)(2,1)S(1)} %copy-done.2), channel_id=1, source_target_pairs={{0,8},{1,9},{2,10},{3,11},{4,12},{5,13},{6,14},{7,15},{8,0},{9,1},... | collective-permute-start | bytes 2359304 | tf_op jit(solution)/shard_map/ppermute | solution.py:62
  19.6 34.7 %collective-permute-start.2 = (bf16[48,8192]{1,0:T(8,128)(2,1)S(1)}, bf16[48,8192]{1,0:T(8,128)(2,1)}, u32[]{:S(2)}, u32[]{:S(2)}) collective-permute-start(bf16[48,8192]{1,0:T(8,128)(2,1)S(1)} %copy-done.2), channel_id=1, source_target_pairs={{0,1},{1,2},{2,3},{3,4},{4,5},{5,6},{6,7},{7,0},{8,9},{9,10},{10,1... | collective-permute-start | bytes 2359304 | tf_op jit(solution)/shard_map/ppermute | solution.py:62
  39.3 35.4 %all-to-all-start = ((bf16[48,16,512]{2,0,1:T(8,128)(2,1)}), bf16[48,16,512]{2,0,1:T(8,128)(2,1)}, u32[]{:S(2)}, u32[]{:S(2)}) async-start(bf16[48,16,512]{2,0,1:T(8,128)(2,1)} %bitcast.133), calls=%async_computation | async-start | bytes 1572864 | tf_op jit(solution)/shard_map/all_to_all | solution.py:69
  54.3 50.3 %collective-permute-start.6 = (bf16[48,8192]{1,0:T(8,128)(2,1)}, bf16[48,8192]{1,0:T(8,128)(2,1)}, u32[]{:S(2)}, u32[]{:S(2)}) collective-permute-start(bf16[48,8192]{1,0:T(8,128)(2,1)} %collective-permute-done), channel_id=1, source_target_pairs={{0,1},{1,2},{2,3},{3,4},{4,5},{5,6},{6,7},{7,0},{8,9},{9,10},{10,1... | collective-permute-start | bytes 2359304 | tf_op jit(solution)/shard_map/ppermute | solution.py:62
  56.6 47.9 %collective-permute-start.5 = (bf16[48,8192]{1,0:T(8,128)(2,1)}, bf16[48,8192]{1,0:T(8,128)(2,1)}, u32[]{:S(2)}, u32[]{:S(2)}) collective-permute-start(bf16[48,8192]{1,0:T(8,128)(2,1)} %collective-permute-done), channel_id=1, source_target_pairs={{0,7},{1,0},{2,1},{3,2},{4,3},{5,4},{6,5},{7,6},{8,15},{9,8},{10,9... | collective-permute-start | bytes 2359304 | tf_op jit(solution)/shard_map/ppermute | solution.py:62
  61.5 41.9 %collective-permute-start.3 = (bf16[48,8192]{1,0:T(8,128)(2,1)}, bf16[48,8192]{1,0:T(8,128)(2,1)}, u32[]{:S(2)}, u32[]{:S(2)}) collective-permute-start(bf16[48,8192]{1,0:T(8,128)(2,1)} %collective-permute-done.1), channel_id=1, source_target_pairs={{0,7},{1,0},{2,1},{3,2},{4,3},{5,4},{6,5},{7,6},{8,15},{9,8},{10,9... | collective-permute-start | bytes 2359304 | tf_op jit(solution)/shard_map/ppermute | solution.py:62
  63.5 41.0 %collective-permute-start.4 = (bf16[48,8192]{1,0:T(8,128)(2,1)}, bf16[48,8192]{1,0:T(8,128)(2,1)}, u32[]{:S(2)}, u32[]{:S(2)}) collective-permute-start(bf16[48,8192]{1,0:T(8,128)(2,1)} %collective-permute-done.2), channel_id=1, source_target_pairs={{0,1},{1,2},{2,3},{3,4},{4,5},{5,6},{6,7},{7,0},{8,9},{9,10},{10,1... | collective-permute-start | bytes 2359304 | tf_op jit(solution)/shard_map/ppermute | solution.py:62
  104.6 48.1 %slice-start = ((s8[8388608]{0:T(1024)(128)(4,1)}), s8[4194304]{0:T(1024)(128)(4,1)S(1)}, s32[]{:S(2)}) async-start(s8[8388608]{0:T(1024)(128)(4,1)} %bitcast.130), calls=%async_computation.2 | async-start | bytes 8388608
  106.5 14.6 %collective-permute-start.11 = (f32[768,64]{0,1:T(8,128)S(1)}, f32[768,64]{0,1:T(8,128)S(1)}, u32[]{:S(2)}, u32[]{:S(2)}) collective-permute-start(f32[768,64]{0,1:T(8,128)S(1)} %select_reduce_fusion), channel_id=1, source_target_pairs={{0,8},{1,9},{2,10},{3,11},{4,12},{5,13},{6,14},{7,15},{8,0},{9,1},... | collective-permute-start | bytes 589832 | tf_op jit(solution)/shard_map/ppermute | solution.py:62
  109.6 20.6 %collective-permute-start.7 = (bf16[48,8192]{1,0:T(8,128)(2,1)}, bf16[48,8192]{1,0:T(8,128)(2,1)S(1)}, u32[]{:S(2)}, u32[]{:S(2)}) collective-permute-start(bf16[48,8192]{1,0:T(8,128)(2,1)} %collective-permute-done.3), channel_id=1, source_target_pairs={{0,7},{1,0},{2,1},{3,2},{4,3},{5,4},{6,5},{7,6},{8,15},{9,8},{10,9... | collective-permute-start | bytes 2359304 | tf_op jit(solution)/shard_map/ppermute | solution.py:62
  111.0 21.8 %collective-permute-start.8 = (bf16[48,8192]{1,0:T(8,128)(2,1)}, bf16[48,8192]{1,0:T(8,128)(2,1)S(1)}, u32[]{:S(2)}, u32[]{:S(2)}) collective-permute-start(bf16[48,8192]{1,0:T(8,128)(2,1)} %collective-permute-done.4), channel_id=1, source_target_pairs={{0,1},{1,2},{2,3},{3,4},{4,5},{5,6},{6,7},{7,0},{8,9},{9,10},{10,1... | collective-permute-start | bytes 2359304 | tf_op jit(solution)/shard_map/ppermute | solution.py:62
  111.6 33.3 %collective-permute-start.9 = (bf16[48,8192]{1,0:T(8,128)(2,1)}, bf16[48,8192]{1,0:T(8,128)(2,1)S(1)}, u32[]{:S(2)}, u32[]{:S(2)}) collective-permute-start(bf16[48,8192]{1,0:T(8,128)(2,1)} %collective-permute-done.5), channel_id=1, source_target_pairs={{0,7},{1,0},{2,1},{3,2},{4,3},{5,4},{6,5},{7,6},{8,15},{9,8},{10,9... | collective-permute-start | bytes 2359304 | tf_op jit(solution)/shard_map/ppermute | solution.py:62
  114.3 33.0 %collective-permute-start.10 = (bf16[48,8192]{1,0:T(8,128)(2,1)}, bf16[48,8192]{1,0:T(8,128)(2,1)S(1)}, u32[]{:S(2)}, u32[]{:S(2)}) collective-permute-start(bf16[48,8192]{1,0:T(8,128)(2,1)} %collective-permute-done.6), channel_id=1, source_target_pairs={{0,1},{1,2},{2,3},{3,4},{4,5},{5,6},{6,7},{7,0},{8,9},{9,10},{10,1... | collective-permute-start | bytes 2359304 | tf_op jit(solution)/shard_map/ppermute | solution.py:62
  147.4 34.8 %collective-permute-start.13 = (bf16[24,8192]{1,0:T(8,128)(2,1)S(1)}, bf16[24,8192]{1,0:T(8,128)(2,1)S(1)}, u32[]{:S(2)}, u32[]{:S(2)}) collective-permute-start(bf16[24,8192]{1,0:T(8,128)(2,1)S(1)} %slice.65), channel_id=1, source_target_pairs={{0,1},{1,2},{2,3},{3,4},{4,5},{5,6},{6,7},{7,0},{8,9},{9,10},{10,1... | collective-permute-start | bytes 1179656 | tf_op jit(solution)/shard_map/ppermute | solution.py:62
  147.5 34.7 %collective-permute-start.12 = (bf16[24,8192]{1,0:T(8,128)(2,1)S(1)}, bf16[24,8192]{1,0:T(8,128)(2,1)S(1)}, u32[]{:S(2)}, u32[]{:S(2)}) collective-permute-start(bf16[24,8192]{1,0:T(8,128)(2,1)S(1)} %slice.64), channel_id=1, source_target_pairs={{0,7},{1,0},{2,1},{3,2},{4,3},{5,4},{6,5},{7,6},{8,15},{9,8},{10,9... | collective-permute-start | bytes 1179656 | tf_op jit(solution)/shard_map/ppermute | solution.py:62
  150.7 31.5 %collective-permute-start.14 = (bf16[48,8192]{1,0:T(8,128)(2,1)S(1)}, bf16[48,8192]{1,0:T(8,128)(2,1)S(1)}, u32[]{:S(2)}, u32[]{:S(2)}) collective-permute-start(bf16[48,8192]{1,0:T(8,128)(2,1)S(1)} %collective-permute-done.9), channel_id=1, source_target_pairs={{0,7},{1,0},{2,1},{3,2},{4,3},{5,4},{6,5},{7,6},{8,15},{9,8},{10,9... | collective-permute-start | bytes 2359304 | tf_op jit(solution)/shard_map/ppermute | solution.py:62
  150.7 32.2 %collective-permute-start.15 = (bf16[48,8192]{1,0:T(8,128)(2,1)S(1)}, bf16[48,8192]{1,0:T(8,128)(2,1)S(1)}, u32[]{:S(2)}, u32[]{:S(2)}) collective-permute-start(bf16[48,8192]{1,0:T(8,128)(2,1)S(1)} %collective-permute-done.10), channel_id=1, source_target_pairs={{0,1},{1,2},{2,3},{3,4},{4,5},{5,6},{6,7},{7,0},{8,9},{9,10},{10,1... | collective-permute-start | bytes 2359304 | tf_op jit(solution)/shard_map/ppermute | solution.py:62
  154.5 27.6 %collective-permute-start.16 = (f32[768,64]{0,1:T(8,128)S(1)}, f32[768,64]{0,1:T(8,128)S(1)}, u32[]{:S(2)}, u32[]{:S(2)}) collective-permute-start(f32[768,64]{0,1:T(8,128)S(1)} %add.86), channel_id=1, source_target_pairs={{0,4},{1,5},{2,6},{3,7},{4,0},{5,1},{6,2},{7,3},{8,12},{9,13},{10,... | collective-permute-start | bytes 589832 | tf_op jit(solution)/shard_map/ppermute | solution.py:62
  183.0 12.2 %collective-permute-start.19 = (f32[768,64]{0,1:T(8,128)S(1)}, f32[768,64]{0,1:T(8,128)S(1)}, u32[]{:S(2)}, u32[]{:S(2)}) collective-permute-start(f32[768,64]{0,1:T(8,128)S(1)} %add.87), channel_id=1, source_target_pairs={{0,2},{1,3},{2,0},{3,1},{4,6},{5,7},{6,4},{7,5},{8,10},{9,11},{10,... | collective-permute-start | bytes 589832 | tf_op jit(solution)/shard_map/ppermute | solution.py:62
  183.1 12.1 %collective-permute-start.18 = (bf16[24,8192]{1,0:T(8,128)(2,1)S(1)}, bf16[24,8192]{1,0:T(8,128)(2,1)S(1)}, u32[]{:S(2)}, u32[]{:S(2)}) collective-permute-start(bf16[24,8192]{1,0:T(8,128)(2,1)S(1)} %slice.75), channel_id=1, source_target_pairs={{0,1},{1,2},{2,3},{3,4},{4,5},{5,6},{6,7},{7,0},{8,9},{9,10},{10,1... | collective-permute-start | bytes 1179656 | tf_op jit(solution)/shard_map/ppermute | solution.py:62
  188.5 8.2 %collective-permute-start.17 = (bf16[24,8192]{1,0:T(8,128)(2,1)S(1)}, bf16[24,8192]{1,0:T(8,128)(2,1)S(1)}, u32[]{:S(2)}, u32[]{:S(2)}) collective-permute-start(bf16[24,8192]{1,0:T(8,128)(2,1)S(1)} %slice.74), channel_id=1, source_target_pairs={{0,7},{1,0},{2,1},{3,2},{4,3},{5,4},{6,5},{7,6},{8,15},{9,8},{10,9... | collective-permute-start | bytes 1179656 | tf_op jit(solution)/shard_map/ppermute | solution.py:62
  196.7 11.1 %collective-permute-start.20 = (f32[768,64]{0,1:T(8,128)S(1)}, f32[768,64]{0,1:T(8,128)S(1)}, u32[]{:S(2)}, u32[]{:S(2)}) collective-permute-start(f32[768,64]{0,1:T(8,128)S(1)} %add.91), channel_id=1, source_target_pairs={{0,1},{1,0},{2,3},{3,2},{4,5},{5,4},{6,7},{7,6},{8,9},{9,8},{10,11... | collective-permute-start | bytes 589832 | tf_op jit(solution)/shard_map/ppermute | solution.py:62
  (6 other events, 75.8 us)

commit v6 on v5

--- a/solution.py
+++ b/solution.py
@@ -66,20 +66,6 @@
     tenant_index = jnp.sum((positions[:, None] >= block_ends[None, :]).astype(jnp.int32), axis=1)
     tenant_masks = tenant_index[:, None] == tenant_ids[None, :]
 
-    local_cols = lax.all_to_all(tokens, "tensor", 1, 0, tiled=True)
-
-    def partial_of(cols):
-        wide = lax.dot_general(
-            cols, down_flat, (((1,), (1,)), ((), ())), preferred_element_type=jnp.float32
-        ).reshape(group_rows, tenants, rank_size)
-        return jnp.sum(jnp.where(tenant_masks[:, :, None], wide, jnp.zeros((), jnp.float32)), axis=1)
-
-    sum_steps = [ring]
-    step = ring // 2
-    while step >= 1:
-        sum_steps.append(step)
-        step //= 2
-
     def sum_step(value, mask):
         return value + hop(value, [(i, i ^ mask) for i in range(members)])
 
@@ -93,7 +79,6 @@
     own_pieces[1], own_pieces[ring - 1] = own_right, own_left
     partner_pieces[0] = partner
     partner_right, partner_left = partner, partner
-    low_sum = None
     for step in range(2, ring // 2 + 2):
         moved = []
         if step < ring // 2:
@@ -104,18 +89,7 @@
             moved += [hop(partner_right, from_right), hop(partner_left, from_left)]
         else:
             moved += [hop(partner_right[:cut], from_right), hop(partner_left[cut:], from_left)]
-        if low_sum is None:
-            extra = (local_cols, panels)
-        else:
-            extra = (sum_step(low_sum, sum_steps.pop(0)),)
-        moved, extra = lax.optimization_barrier((moved, extra))
-        if low_sum is None:
-            local_cols, panels = extra
-            down_flat = panels[:, :rank_size, :].reshape(tenants * rank_size, local_width)
-            up_flat = panels[:, rank_size:, :].reshape(tenants * rank_size, columns)
-            low_sum = partial_of(local_cols)
-        else:
-            low_sum = extra[0]
+        moved = lax.optimization_barrier(moved)
         if step < ring // 2:
             own_right, own_left = moved[0], moved[1]
             own_pieces[step], own_pieces[ring - step] = own_right, own_left
@@ -128,9 +102,6 @@
             partner_pieces[step - 1], partner_pieces[ring - step + 1] = partner_right, partner_left
         else:
             partner_pieces[ring // 2] = jnp.concatenate(moved, axis=0)
-    for mask in sum_steps:
-        low_sum = sum_step(low_sum, mask)
-
     arrivals = [
         [("own", 0)],
         [("own", 1), ("own", ring - 1), ("partner", 0)],
@@ -140,12 +111,20 @@
     arrivals.append([("own", ring // 2), ("partner", ring // 2 - 1), ("partner", ring // 2 + 1)])
     arrivals.append([("partner", ring // 2)])
     pieces = {"own": own_pieces, "partner": partner_pieces}
+    down_flat = panels[:, :rank_size, :].reshape(tenants * rank_size, local_width)
+    up_flat = panels[:, rank_size:, :].reshape(tenants * rank_size, columns)
     base_of = {"own": [None] * ring, "partner": [None] * ring}
+    wide_of = {"own": [None] * ring, "partner": [None] * ring}
     for batch in arrivals:
         stacked = jnp.concatenate([pieces[side][k] for side, k in batch], axis=0)
         product = jnp.dot(stacked, q_weight, preferred_element_type=jnp.float32)
+        cols = lax.dynamic_slice_in_dim(stacked, width_start, local_width, 1)
+        wide = lax.dot_general(
+            cols, down_flat, (((1,), (1,)), ((), ())), preferred_element_type=jnp.float32
+        )
         for i, (side, k) in enumerate(batch):
             base_of[side][k] = product[i * shard_rows:(i + 1) * shard_rows]
+            wide_of[side][k] = wide[i * shard_rows:(i + 1) * shard_rows]
 
     def to_group_order(own_list, partner_list):
         def roll(stacked):
@@ -159,6 +138,15 @@
         return ordered.reshape((group_rows,) + own_list[0].shape[1:])
 
     base_projection = to_group_order(base_of["own"], base_of["partner"])
+    wide_part = to_group_order(wide_of["own"], wide_of["partner"]).reshape(group_rows, tenants, rank_size)
+    partial_low = jnp.sum(
+        jnp.where(tenant_masks[:, :, None], wide_part, jnp.zeros((), jnp.float32)), axis=1
+    )
+    low_sum = partial_low
+    step = 1
+    while step < members:
+        low_sum = sum_step(low_sum, step)
+        step *= 2
     low_rank = low_sum.astype(jnp.bfloat16)
     low_wide = jnp.where(
         tenant_masks[:, :, None], low_rank[:, None, :], jnp.zeros((), jnp.bfloat16)

time: 210 us -> 230 us (1.095)
  local copies, waits for them, and re-layouts: 15.9 us -> 38.5 us
  other arithmetic: 3.82 us -> 11.7 us
  waiting for transfers between devices: 100 us -> 93.6 us
  starting transfers between devices: 63.5 us -> 57.4 us
    all_to_all x1, waiting for transfers between devices: 12.7 us -> 0.01 us  [on_device(): recv = lax.all_to_all(send, 'dp', 0, 0, tiled=True)]
    unnamed x36 -> x99, local copies, waits for them, and re-layouts: 9.97 us -> 22.3 us
    all_to_all x1 -> x0, starting transfers between devices: 11 us -> none  [on_device(): local_cols = lax.all_to_all(tokens, 'tensor', 1, 0, tiled=True)]
    ppermute x21, waiting for transfers between devices: 84.1 us -> 93.6 us  [hop(): return lax.ppermute(value, 'tensor', pairs)]
    ppermute x21, starting transfers between devices: 46.6 us -> 52.3 us  [hop(): return lax.ppermute(value, 'tensor', pairs)]
    concatenate x0 -> x5, local copies, waits for them, and re-layouts: none -> 3.96 us  [the longest x4 3.93 us: on_device(): stacked = jnp.concatenate([pieces[side][k] for side, k in batch], axis=0)]
    select_n x0 -> x1, other arithmetic: none -> 3.87 us  [on_device(): jnp.where(tenant_masks[:, :, None], low_rank[:, None, :], jnp.zeros((), j...]
    reduce_sum x0 -> x1, other arithmetic: none -> 3.62 us  [on_device(): jnp.sum(jnp.where(tenant_masks[:, :, None], wide_part, jnp.zeros((), jnp....]
  transfers between devices with their start and end apart: 23 -> 22, of which waited for: 12 -> 15; matrix products, arithmetic and copies ran while one was open for 18% -> 22% of each run, Pallas kernels for 0% -> 0%
where the time goes in v6:
time: 230 us; the launch traced here: 228 us
  waiting for transfers between devices  93.6 us (41%)
  starting transfers between devices  57.4 us (25%)
  local copies, waits for them, and re-layouts  38.5 us (17%)
  matrix products  26.3 us (11%)
  other arithmetic  11.7 us (5%)
    ppermute x21, waiting for transfers between devices, hop(): return lax.ppermute(value, 'tensor', pairs)  93.6 us
    ppermute x21, starting transfers between devices, hop(): return lax.ppermute(value, 'tensor', pairs)  52.3 us
    unnamed x99, local copies, waits for them, and re-layouts  22.3 us
    dot_general x6, matrix products, on_device(): product = jnp.dot(stacked, q_weight, preferred_element_type=jnp.float32)  21.2 us
    all_to_all x1, starting transfers between devices, on_device(): recv = lax.all_to_all(send, 'dp', 0, 0, tiled=True)  5.09 us
  transfers between devices with their start and end apart: 22, of which 15 were waited for; matrix products, arithmetic and copies ran while one was open for 22% of the time, Pallas kernels for 0%

profile of v6, /device:TPU:2, one launch (start us, length us, event | category | flops | bytes accessed | tf_op | source)
XLA Modules:
  0.0 228.3 jit_solution(15206558490743461780)
XLA Ops:
  3.2 5.9 %collective-permute-start.1 = (bf16[48,8192]{1,0:T(8,128)(2,1)}, bf16[48,8192]{1,0:T(8,128)(2,1)}, u32[]{:S(2)}, u32[]{:S(2)}) collective-permute-start(bf16[48,8192]{1,0:T(8,128)(2,1)} %param.7), channel_id=1, source_target_pairs={{0,7},{1,0},{2,1},{3,2},{4,3},{5,4},{6,5},{7,6},{8,15},{9,8},{10,9... | collective-permute-start | bytes 2359304 | tf_op jit(solution)/shard_map/ppermute | solution.py:62
  13.8 5.1 %all-to-all-start = ((bf16[16,128,512]{2,1,0:T(8,128)(2,1)}), bf16[16,128,512]{2,1,0:T(8,128)(2,1)}, u32[]{:S(2)}, u32[]{:S(2)}) async-start(bf16[16,128,512]{2,1,0:T(8,128)(2,1)} %broadcast_select_fusion), calls=%async_computation | async-start | bytes 4194304 | tf_op jit(solution)/shard_map/all_to_all | solution.py:42
  19.7 5.6 %constant_dynamic-update-slice_fusion.30 = (f32[16,48,512]{2,1,0:T(8,128)}, f32[1,48,512]{2,1,0:T(8,128)}) fusion(bf16[48,8192]{1,0:T(8,128)(2,1)S(1)} %copy-done.3, bf16[8192,512]{1,0:T(8,128)(2,1)} %param.8), kind=kOutput, calls=%fused_computation.60 | convolution fusion | flops 402653184 | bytes 9371648 | tf_op jit(solution)/shard_map/dot_general | solution.py:120
  25.9 3.4 %collective-permute-done.2 = bf16[48,8192]{1,0:T(8,128)(2,1)} collective-permute-done((bf16[48,8192]{1,0:T(8,128)(2,1)}, bf16[48,8192]{1,0:T(8,128)(2,1)}, u32[]{:S(2)}, u32[]{:S(2)}) %collective-permute-start.2) | collective-permute-done | bytes 786464 | tf_op jit(solution)/shard_map/ppermute | solution.py:62
  30.5 7.3 %collective-permute-start.3 = (bf16[48,8192]{1,0:T(8,128)(2,1)}, bf16[48,8192]{1,0:T(8,128)(2,1)}, u32[]{:S(2)}, u32[]{:S(2)}) collective-permute-start(bf16[48,8192]{1,0:T(8,128)(2,1)} %collective-permute-done.1), channel_id=1, source_target_pairs={{0,7},{1,0},{2,1},{3,2},{4,3},{5,4},{6,5},{7,6},{8,15},{9,8},{10,9... | collective-permute-start | bytes 2359304 | tf_op jit(solution)/shard_map/ppermute | solution.py:62
  37.8 8.5 %collective-permute-start.5 = (bf16[48,8192]{1,0:T(8,128)(2,1)}, bf16[48,8192]{1,0:T(8,128)(2,1)}, u32[]{:S(2)}, u32[]{:S(2)}) collective-permute-start(bf16[48,8192]{1,0:T(8,128)(2,1)} %collective-permute-done), channel_id=1, source_target_pairs={{0,7},{1,0},{2,1},{3,2},{4,3},{5,4},{6,5},{7,6},{8,15},{9,8},{10,9... | collective-permute-start | bytes 2359304 | tf_op jit(solution)/shard_map/ppermute | solution.py:62
  48.9 4.9 %fusion.29 = f32[144,512]{1,0:T(8,128)S(1)} fusion(bf16[144,8192]{1,0:T(8,128)(2,1)S(1)} %constant_dynamic-update-slice_fusion, bf16[8192,512]{1,0:T(8,128)(2,1)} %param.8), kind=kOutput, calls=%fused_computation.179 | convolution fusion | flops 1207959552 | bytes 11042816 | tf_op jit(solution)/shard_map/dot_general | solution.py:120
  54.5 3.6 %collective-permute-done.3 = bf16[48,8192]{1,0:T(8,128)(2,1)} collective-permute-done((bf16[48,8192]{1,0:T(8,128)(2,1)}, bf16[48,8192]{1,0:T(8,128)(2,1)}, u32[]{:S(2)}, u32[]{:S(2)}) %collective-permute-start.3) | collective-permute-done | bytes 786464 | tf_op jit(solution)/shard_map/ppermute | solution.py:62
  58.2 15.8 %collective-permute-done.4 = bf16[48,8192]{1,0:T(8,128)(2,1)} collective-permute-done((bf16[48,8192]{1,0:T(8,128)(2,1)}, bf16[48,8192]{1,0:T(8,128)(2,1)}, u32[]{:S(2)}, u32[]{:S(2)}) %collective-permute-start.4) | collective-permute-done | bytes 786464 | tf_op jit(solution)/shard_map/ppermute | solution.py:62
  78.4 5.2 %collective-permute-start.9 = (bf16[48,8192]{1,0:T(8,128)(2,1)}, bf16[48,8192]{1,0:T(8,128)(2,1)}, u32[]{:S(2)}, u32[]{:S(2)}) collective-permute-start(bf16[48,8192]{1,0:T(8,128)(2,1)} %collective-permute-done.5), channel_id=1, source_target_pairs={{0,7},{1,0},{2,1},{3,2},{4,3},{5,4},{6,5},{7,6},{8,15},{9,8},{10,9... | collective-permute-start | bytes 2359304 | tf_op jit(solution)/shard_map/ppermute | solution.py:62
  94.8 4.5 %collective-permute-done.8 = bf16[48,8192]{1,0:T(8,128)(2,1)} collective-permute-done((bf16[48,8192]{1,0:T(8,128)(2,1)}, bf16[48,8192]{1,0:T(8,128)(2,1)}, u32[]{:S(2)}, u32[]{:S(2)}) %collective-permute-start.8) | collective-permute-done | bytes 786464 | tf_op jit(solution)/shard_map/ppermute | solution.py:62
  99.3 5.9 %collective-permute-done.9 = bf16[48,8192]{1,0:T(8,128)(2,1)} collective-permute-done((bf16[48,8192]{1,0:T(8,128)(2,1)}, bf16[48,8192]{1,0:T(8,128)(2,1)}, u32[]{:S(2)}, u32[]{:S(2)}) %collective-permute-start.9) | collective-permute-done | bytes 786464 | tf_op jit(solution)/shard_map/ppermute | solution.py:62
  114.8 5.3 %fusion.31 = f32[192,512]{1,0:T(8,128)S(1)} fusion(bf16[192,8192]{1,0:T(8,128)(2,1)S(1)} %constant_dynamic-update-slice_fusion.7, bf16[8192,512]{1,0:T(8,128)(2,1)} %param.8), kind=kOutput, calls=%fused_computation.181 | convolution fusion | flops 1610612736 | bytes 11927552 | tf_op jit(solution)/shard_map/dot_general | solution.py:120
  126.1 4.3 %collective-permute-done.11 = bf16[24,8192]{1,0:T(8,128)(2,1)S(1)} collective-permute-done((bf16[24,8192]{1,0:T(8,128)(2,1)S(1)}, bf16[24,8192]{1,0:T(8,128)(2,1)S(1)}, u32[]{:S(2)}, u32[]{:S(2)}) %collective-permute-start.11) | collective-permute-done | bytes 393248 | tf_op jit(solution)/shard_map/ppermute | solution.py:62
  130.4 4.3 %collective-permute-done.12 = bf16[24,8192]{1,0:T(8,128)(2,1)S(1)} collective-permute-done((bf16[24,8192]{1,0:T(8,128)(2,1)S(1)}, bf16[24,8192]{1,0:T(8,128)(2,1)S(1)}, u32[]{:S(2)}, u32[]{:S(2)}) %collective-permute-start.12) | collective-permute-done | bytes 393248 | tf_op jit(solution)/shard_map/ppermute | solution.py:62
  144.1 4.3 %collective-permute-done.15 = bf16[24,8192]{1,0:T(8,128)(2,1)S(1)} collective-permute-done((bf16[24,8192]{1,0:T(8,128)(2,1)S(1)}, bf16[24,8192]{1,0:T(8,128)(2,1)S(1)}, u32[]{:S(2)}, u32[]{:S(2)}) %collective-permute-start.15) | collective-permute-done | bytes 393248 | tf_op jit(solution)/shard_map/ppermute | solution.py:62
  161.6 3.6 %select_reduce_fusion = f32[768,64]{1,0:T(8,128)S(1)} fusion(f32[768,8,64]{2,1,0:T(8,128)S(1)} %select_n.152, pred[768,8]{1,0:T(8,128)(4,1)S(1)} %iota_compare_fusion), kind=kLoop, calls=%fused_computation.3 | loop fusion | flops 737280 | bytes 1775616 | tf_op jit(solution)/shard_map/reduce_sum | solution.py:142
  165.4 11.8 %collective-permute-done.17 = f32[768,64]{1,0:T(8,128)S(1)} collective-permute-done((f32[768,64]{1,0:T(8,128)S(1)}, f32[768,64]{1,0:T(8,128)S(1)}, u32[]{:S(2)}, u32[]{:S(2)}) %collective-permute-start.17) | collective-permute-done | bytes 196640 | tf_op jit(solution)/shard_map/ppermute | solution.py:62
  177.2 4.4 %collective-permute-start.18 = (f32[768,64]{1,0:T(8,128)S(1)}, f32[768,64]{1,0:T(8,128)S(1)}, u32[]{:S(2)}, u32[]{:S(2)}) collective-permute-start(f32[768,64]{1,0:T(8,128)S(1)} %add.102), channel_id=1, source_target_pairs={{0,2},{1,3},{2,0},{3,1},{4,6},{5,7},{6,4},{7,5},{8,10},{9,11},{10,... | collective-permute-start | bytes 589832 | tf_op jit(solution)/shard_map/ppermute | solution.py:62
  182.5 13.6 %collective-permute-done.18 = f32[768,64]{1,0:T(8,128)S(1)} collective-permute-done((f32[768,64]{1,0:T(8,128)S(1)}, f32[768,64]{1,0:T(8,128)S(1)}, u32[]{:S(2)}, u32[]{:S(2)}) %collective-permute-start.18) | collective-permute-done | bytes 196640 | tf_op jit(solution)/shard_map/ppermute | solution.py:62
  200.1 11.6 %collective-permute-done.19 = f32[768,64]{1,0:T(8,128)S(1)} collective-permute-done((f32[768,64]{1,0:T(8,128)S(1)}, f32[768,64]{1,0:T(8,128)S(1)}, u32[]{:S(2)}, u32[]{:S(2)}) %collective-permute-start.19) | collective-permute-done | bytes 196640 | tf_op jit(solution)/shard_map/ppermute | solution.py:62
  211.8 5.3 %collective-permute-start.20 = (f32[768,64]{1,0:T(8,128)S(1)}, f32[768,64]{1,0:T(8,128)S(1)}, u32[]{:S(2)}, u32[]{:S(2)}) collective-permute-start(f32[768,64]{1,0:T(8,128)S(1)} %add.104), channel_id=1, source_target_pairs={{0,8},{1,9},{2,10},{3,11},{4,12},{5,13},{6,14},{7,15},{8,0},{9,1},... | collective-permute-start | bytes 589832 | tf_op jit(solution)/shard_map/ppermute | solution.py:62
  218.6 4.2 %collective-permute-done.20 = f32[768,64]{1,0:T(8,128)S(1)} collective-permute-done((f32[768,64]{1,0:T(8,128)S(1)}, f32[768,64]{1,0:T(8,128)S(1)}, u32[]{:S(2)}, u32[]{:S(2)}) %collective-permute-start.20) | collective-permute-done | bytes 196640 | tf_op jit(solution)/shard_map/ppermute | solution.py:62
  222.9 3.9 %broadcast_select_fusion.1 = bf16[768,8,64]{2,1,0:T(8,128)(2,1)S(1)} fusion(pred[768,8]{1,0:T(8,128)(4,1)S(1)} %iota_compare_fusion, bf16[768,64]{1,0:T(8,128)(2,1)S(1)} %add_convert_fusion), kind=kLoop, calls=%fused_computation.12 | loop fusion | flops 393216 | bytes 890880 | tf_op jit(solution)/shard_map/jit(_where)/select_n | solution.py:151
  (181 shorter events, 75.1 us)
Async XLA Ops:
  0.0 25.3 %collective-permute-start = (bf16[48,8192]{1,0:T(8,128)(2,1)}, bf16[48,8192]{1,0:T(8,128)(2,1)}, u32[]{:S(2)}, u32[]{:S(2)}) collective-permute-start(bf16[48,8192]{1,0:T(8,128)(2,1)} %param.7), channel_id=1, source_target_pairs={{0,8},{1,9},{2,10},{3,11},{4,12},{5,13},{6,14},{7,15},{8,0},{9,1},... | collective-permute-start | bytes 2359304 | tf_op jit(solution)/shard_map/ppermute | solution.py:62
  3.2 22.7 %collective-permute-start.1 = (bf16[48,8192]{1,0:T(8,128)(2,1)}, bf16[48,8192]{1,0:T(8,128)(2,1)}, u32[]{:S(2)}, u32[]{:S(2)}) collective-permute-start(bf16[48,8192]{1,0:T(8,128)(2,1)} %param.7), channel_id=1, source_target_pairs={{0,7},{1,0},{2,1},{3,2},{4,3},{5,4},{6,5},{7,6},{8,15},{9,8},{10,9... | collective-permute-start | bytes 2359304 | tf_op jit(solution)/shard_map/ppermute | solution.py:62
  9.1 20.2 %collective-permute-start.2 = (bf16[48,8192]{1,0:T(8,128)(2,1)}, bf16[48,8192]{1,0:T(8,128)(2,1)}, u32[]{:S(2)}, u32[]{:S(2)}) collective-permute-start(bf16[48,8192]{1,0:T(8,128)(2,1)} %param.7), channel_id=1, source_target_pairs={{0,1},{1,2},{2,3},{3,4},{4,5},{5,6},{6,7},{7,0},{8,9},{9,10},{10,1... | collective-permute-start | bytes 2359304 | tf_op jit(solution)/shard_map/ppermute | solution.py:62
  13.8 75.8 %all-to-all-start = ((bf16[16,128,512]{2,1,0:T(8,128)(2,1)}), bf16[16,128,512]{2,1,0:T(8,128)(2,1)}, u32[]{:S(2)}, u32[]{:S(2)}) async-start(bf16[16,128,512]{2,1,0:T(8,128)(2,1)} %broadcast_select_fusion), calls=%async_computation | async-start | bytes 4194304 | tf_op jit(solution)/shard_map/all_to_all | solution.py:42
  30.5 27.7 %collective-permute-start.3 = (bf16[48,8192]{1,0:T(8,128)(2,1)}, bf16[48,8192]{1,0:T(8,128)(2,1)}, u32[]{:S(2)}, u32[]{:S(2)}) collective-permute-start(bf16[48,8192]{1,0:T(8,128)(2,1)} %collective-permute-done.1), channel_id=1, source_target_pairs={{0,7},{1,0},{2,1},{3,2},{4,3},{5,4},{6,5},{7,6},{8,15},{9,8},{10,9... | collective-permute-start | bytes 2359304 | tf_op jit(solution)/shard_map/ppermute | solution.py:62
  37.8 36.1 %collective-permute-start.5 = (bf16[48,8192]{1,0:T(8,128)(2,1)}, bf16[48,8192]{1,0:T(8,128)(2,1)}, u32[]{:S(2)}, u32[]{:S(2)}) collective-permute-start(bf16[48,8192]{1,0:T(8,128)(2,1)} %collective-permute-done), channel_id=1, source_target_pairs={{0,7},{1,0},{2,1},{3,2},{4,3},{5,4},{6,5},{7,6},{8,15},{9,8},{10,9... | collective-permute-start | bytes 2359304 | tf_op jit(solution)/shard_map/ppermute | solution.py:62
  46.3 27.7 %collective-permute-start.6 = (bf16[48,8192]{1,0:T(8,128)(2,1)}, bf16[48,8192]{1,0:T(8,128)(2,1)}, u32[]{:S(2)}, u32[]{:S(2)}) collective-permute-start(bf16[48,8192]{1,0:T(8,128)(2,1)} %collective-permute-done), channel_id=1, source_target_pairs={{0,1},{1,2},{2,3},{3,4},{4,5},{5,6},{6,7},{7,0},{8,9},{9,10},{10,1... | collective-permute-start | bytes 2359304 | tf_op jit(solution)/shard_map/ppermute | solution.py:62
  46.3 27.6 %collective-permute-start.4 = (bf16[48,8192]{1,0:T(8,128)(2,1)}, bf16[48,8192]{1,0:T(8,128)(2,1)}, u32[]{:S(2)}, u32[]{:S(2)}) collective-permute-start(bf16[48,8192]{1,0:T(8,128)(2,1)} %collective-permute-done.2), channel_id=1, source_target_pairs={{0,1},{1,2},{2,3},{3,4},{4,5},{5,6},{6,7},{7,0},{8,9},{9,10},{10,1... | collective-permute-start | bytes 2359304 | tf_op jit(solution)/shard_map/ppermute | solution.py:62
  47.5 38.9 %slice-start = ((s8[8388608]{0:T(1024)(128)(4,1)}), s8[4194304]{0:T(1024)(128)(4,1)S(1)}, s32[]{:S(2)}) async-start(s8[8388608]{0:T(1024)(128)(4,1)} %bitcast.226), calls=%async_computation.1 | async-start | bytes 8388608
  48.8 37.6 %slice-start.1 = ((s8[8388608]{0:T(1024)(128)(4,1)}), s8[4194304]{0:T(1024)(128)(4,1)S(1)}, s32[]{:S(2)}) async-start(s8[8388608]{0:T(1024)(128)(4,1)} %bitcast.226), calls=%async_computation.2 | async-start | bytes 8388608
  75.1 19.7 %collective-permute-start.7 = (bf16[48,8192]{1,0:T(8,128)(2,1)}, bf16[48,8192]{1,0:T(8,128)(2,1)}, u32[]{:S(2)}, u32[]{:S(2)}) collective-permute-start(bf16[48,8192]{1,0:T(8,128)(2,1)} %collective-permute-done.3), channel_id=1, source_target_pairs={{0,7},{1,0},{2,1},{3,2},{4,3},{5,4},{6,5},{7,6},{8,15},{9,8},{10,9... | collective-permute-start | bytes 2359304 | tf_op jit(solution)/shard_map/ppermute | solution.py:62
  75.5 23.7 %collective-permute-start.8 = (bf16[48,8192]{1,0:T(8,128)(2,1)}, bf16[48,8192]{1,0:T(8,128)(2,1)}, u32[]{:S(2)}, u32[]{:S(2)}) collective-permute-start(bf16[48,8192]{1,0:T(8,128)(2,1)} %collective-permute-done.4), channel_id=1, source_target_pairs={{0,1},{1,2},{2,3},{3,4},{4,5},{5,6},{6,7},{7,0},{8,9},{9,10},{10,1... | collective-permute-start | bytes 2359304 | tf_op jit(solution)/shard_map/ppermute | solution.py:62
  78.4 26.7 %collective-permute-start.9 = (bf16[48,8192]{1,0:T(8,128)(2,1)}, bf16[48,8192]{1,0:T(8,128)(2,1)}, u32[]{:S(2)}, u32[]{:S(2)}) collective-permute-start(bf16[48,8192]{1,0:T(8,128)(2,1)} %collective-permute-done.5), channel_id=1, source_target_pairs={{0,7},{1,0},{2,1},{3,2},{4,3},{5,4},{6,5},{7,6},{8,15},{9,8},{10,9... | collective-permute-start | bytes 2359304 | tf_op jit(solution)/shard_map/ppermute | solution.py:62
  84.9 22.8 %collective-permute-start.10 = (bf16[48,8192]{1,0:T(8,128)(2,1)}, bf16[48,8192]{1,0:T(8,128)(2,1)}, u32[]{:S(2)}, u32[]{:S(2)}) collective-permute-start(bf16[48,8192]{1,0:T(8,128)(2,1)} %collective-permute-done.6), channel_id=1, source_target_pairs={{0,1},{1,2},{2,3},{3,4},{4,5},{5,6},{6,7},{7,0},{8,9},{9,10},{10,1... | collective-permute-start | bytes 2359304 | tf_op jit(solution)/shard_map/ppermute | solution.py:62
  108.9 25.8 %collective-permute-start.13 = (bf16[48,8192]{1,0:T(8,128)(2,1)}, bf16[48,8192]{1,0:T(8,128)(2,1)S(1)}, u32[]{:S(2)}, u32[]{:S(2)}) collective-permute-start(bf16[48,8192]{1,0:T(8,128)(2,1)} %collective-permute-done.9), channel_id=1, source_target_pairs={{0,7},{1,0},{2,1},{3,2},{4,3},{5,4},{6,5},{7,6},{8,15},{9,8},{10,9... | collective-permute-start | bytes 2359304 | tf_op jit(solution)/shard_map/ppermute | solution.py:62
  112.5 22.2 %collective-permute-start.14 = (bf16[48,8192]{1,0:T(8,128)(2,1)}, bf16[48,8192]{1,0:T(8,128)(2,1)S(1)}, u32[]{:S(2)}, u32[]{:S(2)}) collective-permute-start(bf16[48,8192]{1,0:T(8,128)(2,1)} %collective-permute-done.10), channel_id=1, source_target_pairs={{0,1},{1,2},{2,3},{3,4},{4,5},{5,6},{6,7},{7,0},{8,9},{9,10},{10,1... | collective-permute-start | bytes 2359304 | tf_op jit(solution)/shard_map/ppermute | solution.py:62
  122.3 8.1 %collective-permute-start.11 = (bf16[24,8192]{1,0:T(8,128)(2,1)S(1)}, bf16[24,8192]{1,0:T(8,128)(2,1)S(1)}, u32[]{:S(2)}, u32[]{:S(2)}) collective-permute-start(bf16[24,8192]{1,0:T(8,128)(2,1)S(1)} %slice.105), channel_id=1, source_target_pairs={{0,7},{1,0},{2,1},{3,2},{4,3},{5,4},{6,5},{7,6},{8,15},{9,8},{10,9... | collective-permute-start | bytes 1179656 | tf_op jit(solution)/shard_map/ppermute | solution.py:62
  125.1 9.6 %collective-permute-start.12 = (bf16[24,8192]{1,0:T(8,128)(2,1)S(1)}, bf16[24,8192]{1,0:T(8,128)(2,1)S(1)}, u32[]{:S(2)}, u32[]{:S(2)}) collective-permute-start(bf16[24,8192]{1,0:T(8,128)(2,1)S(1)} %slice.106), channel_id=1, source_target_pairs={{0,1},{1,2},{2,3},{3,4},{4,5},{5,6},{6,7},{7,0},{8,9},{9,10},{10,1... | collective-permute-start | bytes 1179656 | tf_op jit(solution)/shard_map/ppermute | solution.py:62
  140.6 7.8 %collective-permute-start.15 = (bf16[24,8192]{1,0:T(8,128)(2,1)S(1)}, bf16[24,8192]{1,0:T(8,128)(2,1)S(1)}, u32[]{:S(2)}, u32[]{:S(2)}) collective-permute-start(bf16[24,8192]{1,0:T(8,128)(2,1)S(1)} %slice.115), channel_id=1, source_target_pairs={{0,7},{1,0},{2,1},{3,2},{4,3},{5,4},{6,5},{7,6},{8,15},{9,8},{10,9... | collective-permute-start | bytes 1179656 | tf_op jit(solution)/shard_map/ppermute | solution.py:62
  142.5 9.0 %collective-permute-start.16 = (bf16[24,8192]{1,0:T(8,128)(2,1)S(1)}, bf16[24,8192]{1,0:T(8,128)(2,1)S(1)}, u32[]{:S(2)}, u32[]{:S(2)}) collective-permute-start(bf16[24,8192]{1,0:T(8,128)(2,1)S(1)} %slice.116), channel_id=1, source_target_pairs={{0,1},{1,2},{2,3},{3,4},{4,5},{5,6},{6,7},{7,0},{8,9},{9,10},{10,1... | collective-permute-start | bytes 1179656 | tf_op jit(solution)/shard_map/ppermute | solution.py:62
  165.2 12.0 %collective-permute-start.17 = (f32[768,64]{1,0:T(8,128)S(1)}, f32[768,64]{1,0:T(8,128)S(1)}, u32[]{:S(2)}, u32[]{:S(2)}) collective-permute-start(f32[768,64]{1,0:T(8,128)S(1)} %select_reduce_fusion), channel_id=1, source_target_pairs={{0,1},{1,0},{2,3},{3,2},{4,5},{5,4},{6,7},{7,6},{8,9},{9,8},{10,11... | collective-permute-start | bytes 589832 | tf_op jit(solution)/shard_map/ppermute | solution.py:62
  177.2 18.9 %collective-permute-start.18 = (f32[768,64]{1,0:T(8,128)S(1)}, f32[768,64]{1,0:T(8,128)S(1)}, u32[]{:S(2)}, u32[]{:S(2)}) collective-permute-start(f32[768,64]{1,0:T(8,128)S(1)} %add.102), channel_id=1, source_target_pairs={{0,2},{1,3},{2,0},{3,1},{4,6},{5,7},{6,4},{7,5},{8,10},{9,11},{10,... | collective-permute-start | bytes 589832 | tf_op jit(solution)/shard_map/ppermute | solution.py:62
  196.1 15.6 %collective-permute-start.19 = (f32[768,64]{1,0:T(8,128)S(1)}, f32[768,64]{1,0:T(8,128)S(1)}, u32[]{:S(2)}, u32[]{:S(2)}) collective-permute-start(f32[768,64]{1,0:T(8,128)S(1)} %add.103), channel_id=1, source_target_pairs={{0,4},{1,5},{2,6},{3,7},{4,0},{5,1},{6,2},{7,3},{8,12},{9,13},{10,... | collective-permute-start | bytes 589832 | tf_op jit(solution)/shard_map/ppermute | solution.py:62
  211.8 11.0 %collective-permute-start.20 = (f32[768,64]{1,0:T(8,128)S(1)}, f32[768,64]{1,0:T(8,128)S(1)}, u32[]{:S(2)}, u32[]{:S(2)}) collective-permute-start(f32[768,64]{1,0:T(8,128)S(1)} %add.104), channel_id=1, source_target_pairs={{0,8},{1,9},{2,10},{3,11},{4,12},{5,13},{6,14},{7,15},{8,0},{9,1},... | collective-permute-start | bytes 589832 | tf_op jit(solution)/shard_map/ppermute | solution.py:62
  (20 other events, 176.1 us)

commit v7 on v5

--- a/solution.py
+++ b/solution.py
@@ -107,7 +107,11 @@
         if low_sum is None:
             extra = (local_cols, panels)
         else:
-            extra = (sum_step(low_sum, sum_steps.pop(0)),)
+            low_next = sum_step(low_sum, sum_steps.pop(0))
+            if step == ring // 2 + 1:
+                while sum_steps:
+                    low_next = sum_step(low_next, sum_steps.pop(0))
+            extra = (low_next,)
         moved, extra = lax.optimization_barrier((moved, extra))
         if low_sum is None:
             local_cols, panels = extra

time: 210 us -> 209 us (level)
  starting transfers between devices: 63.5 us -> 60.4 us
  waiting for transfers between devices: 100 us -> 103 us
    ppermute x21, starting transfers between devices: 46.6 us -> 43.4 us  [hop(): return lax.ppermute(value, 'tensor', pairs)]
    ppermute x21, waiting for transfers between devices: 84.1 us -> 86.2 us  [hop(): return lax.ppermute(value, 'tensor', pairs)]
  transfers between devices with their start and end apart: 23 -> 23, of which waited for: 12 -> 12; matrix products, arithmetic and copies ran while one was open for 18% -> 15% of each run, Pallas kernels for 0% -> 0%
where the time goes in v7:
time: 209 us; the launch traced here: 208 us
  waiting for transfers between devices  103 us (49%)
  starting transfers between devices  60.4 us (29%)
  matrix products  25.3 us (12%)
  local copies, waits for them, and re-layouts  15.9 us (8%)
  other arithmetic  3.82 us (2%)
    ppermute x21, waiting for transfers between devices, hop(): return lax.ppermute(value, 'tensor', pairs)  86.2 us
    ppermute x21, starting transfers between devices, hop(): return lax.ppermute(value, 'tensor', pairs)  43.4 us
    dot_general x6, matrix products, on_device(): product = jnp.dot(stacked, q_weight, preferred_element_type=jnp.float32)  21.9 us
    all_to_all x1, waiting for transfers between devices, on_device(): recv = lax.all_to_all(send, 'dp', 0, 0, tiled=True)  12.7 us
    all_to_all x1, starting transfers between devices, on_device(): local_cols = lax.all_to_all(tokens, 'tensor', 1, 0, tiled=True)  11 us
    unnamed x36, local copies, waits for them, and re-layouts  9.97 us
    all_to_all x1, starting transfers between devices, on_device(): recv = lax.all_to_all(send, 'dp', 0, 0, tiled=True)  5.99 us
  transfers between devices with their start and end apart: 23, of which 12 were waited for; matrix products, arithmetic and copies ran while one was open for 15% of the time, Pallas kernels for 0%

profile of v7, /device:TPU:2, one launch (start us, length us, event | category | flops | bytes accessed | tf_op | source)
XLA Modules:
  0.0 208.3 jit_solution(11405006931931658652)
XLA Ops:
  4.8 6.0 %all-to-all-start.1 = ((bf16[16,128,512]{2,1,0:T(8,128)(2,1)}), bf16[16,128,512]{2,1,0:T(8,128)(2,1)S(1)}, u32[]{:S(2)}, u32[]{:S(2)}) async-start(bf16[16,128,512]{2,1,0:T(8,128)(2,1)} %broadcast_select_fusion), calls=%async_computation.1 | async-start | bytes 4194304 | tf_op jit(solution)/shard_map/all_to_all | solution.py:42
  10.8 5.9 %collective-permute-start.1 = (bf16[48,8192]{1,0:T(8,128)(2,1)S(1)}, bf16[48,8192]{1,0:T(8,128)(2,1)}, u32[]{:S(2)}, u32[]{:S(2)}) collective-permute-start(bf16[48,8192]{1,0:T(8,128)(2,1)S(1)} %copy-done.2), channel_id=1, source_target_pairs={{0,7},{1,0},{2,1},{3,2},{4,3},{5,4},{6,5},{7,6},{8,15},{9,8},{10,9... | collective-permute-start | bytes 2359304 | tf_op jit(solution)/shard_map/ppermute | solution.py:62
  16.7 2.9 %collective-permute-start = (bf16[48,8192]{1,0:T(8,128)(2,1)S(1)}, bf16[48,8192]{1,0:T(8,128)(2,1)}, u32[]{:S(2)}, u32[]{:S(2)}) collective-permute-start(bf16[48,8192]{1,0:T(8,128)(2,1)S(1)} %copy-done.2), channel_id=1, source_target_pairs={{0,8},{1,9},{2,10},{3,11},{4,12},{5,13},{6,14},{7,15},{8,0},{9,1},... | collective-permute-start | bytes 2359304 | tf_op jit(solution)/shard_map/ppermute | solution.py:62
  21.1 5.6 %constant_dynamic-update-slice_fusion.1 = (f32[16,48,512]{2,1,0:T(8,128)}, f32[1,48,512]{2,1,0:T(8,128)S(1)}) fusion(bf16[48,8192]{1,0:T(8,128)(2,1)S(1)} %copy-done.2, bf16[8192,512]{1,0:T(8,128)(2,1)} %param.8), kind=kOutput, calls=%fused_computation.99 | convolution fusion | flops 402653184 | bytes 9371648 | tf_op jit(solution)/shard_map/dot_general | solution.py:150
  26.6 12.7 %all-to-all-done.1 = bf16[16,128,512]{2,1,0:T(8,128)(2,1)S(1)} async-done(((bf16[16,128,512]{2,1,0:T(8,128)(2,1)}), bf16[16,128,512]{2,1,0:T(8,128)(2,1)S(1)}, u32[]{:S(2)}, u32[]{:S(2)}) %all-to-all-start.1) | async-done | bytes 2097184 | tf_op jit(solution)/shard_map/all_to_all | solution.py:42
  39.3 11.0 %all-to-all-start = ((bf16[48,16,512]{2,0,1:T(8,128)(2,1)}), bf16[48,16,512]{2,0,1:T(8,128)(2,1)}, u32[]{:S(2)}, u32[]{:S(2)}) async-start(bf16[48,16,512]{2,0,1:T(8,128)(2,1)} %bitcast.133), calls=%async_computation | async-start | bytes 1572864 | tf_op jit(solution)/shard_map/all_to_all | solution.py:69
  50.9 3.4 %collective-permute-done = bf16[48,8192]{1,0:T(8,128)(2,1)} collective-permute-done((bf16[48,8192]{1,0:T(8,128)(2,1)S(1)}, bf16[48,8192]{1,0:T(8,128)(2,1)}, u32[]{:S(2)}, u32[]{:S(2)}) %collective-permute-start) | collective-permute-done | bytes 786464 | tf_op jit(solution)/shard_map/ppermute | solution.py:62
  54.3 2.4 %collective-permute-start.6 = (bf16[48,8192]{1,0:T(8,128)(2,1)}, bf16[48,8192]{1,0:T(8,128)(2,1)}, u32[]{:S(2)}, u32[]{:S(2)}) collective-permute-start(bf16[48,8192]{1,0:T(8,128)(2,1)} %collective-permute-done), channel_id=1, source_target_pairs={{0,1},{1,2},{2,3},{3,4},{4,5},{5,6},{6,7},{7,0},{8,9},{9,10},{10,1... | collective-permute-start | bytes 2359304 | tf_op jit(solution)/shard_map/ppermute | solution.py:62
  56.6 4.9 %collective-permute-start.5 = (bf16[48,8192]{1,0:T(8,128)(2,1)}, bf16[48,8192]{1,0:T(8,128)(2,1)}, u32[]{:S(2)}, u32[]{:S(2)}) collective-permute-start(bf16[48,8192]{1,0:T(8,128)(2,1)} %collective-permute-done), channel_id=1, source_target_pairs={{0,7},{1,0},{2,1},{3,2},{4,3},{5,4},{6,5},{7,6},{8,15},{9,8},{10,9... | collective-permute-start | bytes 2359304 | tf_op jit(solution)/shard_map/ppermute | solution.py:62
  63.5 5.5 %fusion.16 = f32[144,512]{1,0:T(8,128)S(1)} fusion(bf16[8192,512]{1,0:T(8,128)(2,1)} %param.8, bf16[48,8192]{1,0:T(8,128)(2,1)} %collective-permute-done, bf16[48,8192]{1,0:T(8,128)(2,1)} %collective-permute-done.2, bf16[48,8192]{1,0:T(8,128)(2,1)} %collective-permute-done.1), kind=kOutput, calls=%fused_computation.19 | convolution fusion | flops 1215037440 | bytes 11042816 | tf_op jit(solution)/shard_map/dot_general | solution.py:150
  71.1 3.6 %all-to-all-done = bf16[48,16,512]{2,0,1:T(8,128)(2,1)} async-done(((bf16[48,16,512]{2,0,1:T(8,128)(2,1)}), bf16[48,16,512]{2,0,1:T(8,128)(2,1)}, u32[]{:S(2)}, u32[]{:S(2)}) %all-to-all-start) | async-done | bytes 786464 | tf_op jit(solution)/shard_map/all_to_all | solution.py:69
  74.7 28.6 %collective-permute-done.3 = bf16[48,8192]{1,0:T(8,128)(2,1)} collective-permute-done((bf16[48,8192]{1,0:T(8,128)(2,1)}, bf16[48,8192]{1,0:T(8,128)(2,1)}, u32[]{:S(2)}, u32[]{:S(2)}) %collective-permute-start.3) | collective-permute-done | bytes 786464 | tf_op jit(solution)/shard_map/ppermute | solution.py:62
  106.5 3.1 %collective-permute-start.11 = (f32[768,64]{0,1:T(8,128)S(1)}, f32[768,64]{0,1:T(8,128)S(1)}, u32[]{:S(2)}, u32[]{:S(2)}) collective-permute-start(f32[768,64]{0,1:T(8,128)S(1)} %select_reduce_fusion), channel_id=1, source_target_pairs={{0,8},{1,9},{2,10},{3,11},{4,12},{5,13},{6,14},{7,15},{8,0},{9,1},... | collective-permute-start | bytes 589832 | tf_op jit(solution)/shard_map/ppermute | solution.py:62
  111.6 2.7 %collective-permute-start.9 = (bf16[48,8192]{1,0:T(8,128)(2,1)}, bf16[48,8192]{1,0:T(8,128)(2,1)S(1)}, u32[]{:S(2)}, u32[]{:S(2)}) collective-permute-start(bf16[48,8192]{1,0:T(8,128)(2,1)} %collective-permute-done.5), channel_id=1, source_target_pairs={{0,7},{1,0},{2,1},{3,2},{4,3},{5,4},{6,5},{7,6},{8,15},{9,8},{10,9... | collective-permute-start | bytes 2359304 | tf_op jit(solution)/shard_map/ppermute | solution.py:62
  114.3 6.1 %fusion = f32[192,512]{1,0:T(8,128)S(1)} fusion(bf16[8192,512]{1,0:T(8,128)(2,1)} %param.8, bf16[48,8192]{1,0:T(8,128)(2,1)} %collective-permute-done.6, bf16[48,8192]{1,0:T(8,128)(2,1)} %collective-permute-done.5, bf16[48,8192]{1,0:T(8,128)(2,1)} %collective-permute-done.4, bf16[48,8192]{1,0:T(8,128)(2,1)} %collective-permute-done.3), kind=kOutput, calls=%fused_computation.3 | convolution fusion | flops 1623195648 | bytes 11927552 | tf_op jit(solution)/shard_map/dot_general | solution.py:150
  121.1 9.1 %collective-permute-done.7 = bf16[48,8192]{1,0:T(8,128)(2,1)S(1)} collective-permute-done((bf16[48,8192]{1,0:T(8,128)(2,1)}, bf16[48,8192]{1,0:T(8,128)(2,1)S(1)}, u32[]{:S(2)}, u32[]{:S(2)}) %collective-permute-start.7) | collective-permute-done | bytes 786464 | tf_op jit(solution)/shard_map/ppermute | solution.py:62
  130.2 2.7 %collective-permute-done.8 = bf16[48,8192]{1,0:T(8,128)(2,1)S(1)} collective-permute-done((bf16[48,8192]{1,0:T(8,128)(2,1)}, bf16[48,8192]{1,0:T(8,128)(2,1)S(1)}, u32[]{:S(2)}, u32[]{:S(2)}) %collective-permute-start.8) | collective-permute-done | bytes 786464 | tf_op jit(solution)/shard_map/ppermute | solution.py:62
  132.9 12.0 %collective-permute-done.9 = bf16[48,8192]{1,0:T(8,128)(2,1)S(1)} collective-permute-done((bf16[48,8192]{1,0:T(8,128)(2,1)}, bf16[48,8192]{1,0:T(8,128)(2,1)S(1)}, u32[]{:S(2)}, u32[]{:S(2)}) %collective-permute-start.9) | collective-permute-done | bytes 786464 | tf_op jit(solution)/shard_map/ppermute | solution.py:62
  144.9 2.4 %collective-permute-done.10 = bf16[48,8192]{1,0:T(8,128)(2,1)S(1)} collective-permute-done((bf16[48,8192]{1,0:T(8,128)(2,1)}, bf16[48,8192]{1,0:T(8,128)(2,1)S(1)}, u32[]{:S(2)}, u32[]{:S(2)}) %collective-permute-start.10) | collective-permute-done | bytes 786464 | tf_op jit(solution)/shard_map/ppermute | solution.py:62
  147.4 3.2 %collective-permute-start.12 = (bf16[24,8192]{1,0:T(8,128)(2,1)S(1)}, bf16[24,8192]{1,0:T(8,128)(2,1)S(1)}, u32[]{:S(2)}, u32[]{:S(2)}) collective-permute-start(bf16[24,8192]{1,0:T(8,128)(2,1)S(1)} %slice.64), channel_id=1, source_target_pairs={{0,7},{1,0},{2,1},{3,2},{4,3},{5,4},{6,5},{7,6},{8,15},{9,8},{10,9... | collective-permute-start | bytes 1179656 | tf_op jit(solution)/shard_map/ppermute | solution.py:62
  154.5 4.6 %collective-permute-start.16 = (f32[768,64]{0,1:T(8,128)S(1)}, f32[768,64]{0,1:T(8,128)S(1)}, u32[]{:S(2)}, u32[]{:S(2)}) collective-permute-start(f32[768,64]{0,1:T(8,128)S(1)} %add.86), channel_id=1, source_target_pairs={{0,4},{1,5},{2,6},{3,7},{4,0},{5,1},{6,2},{7,3},{8,12},{9,13},{10,... | collective-permute-start | bytes 589832 | tf_op jit(solution)/shard_map/ppermute | solution.py:62
  159.8 22.4 %collective-permute-done.16 = f32[768,64]{0,1:T(8,128)S(1)} collective-permute-done((f32[768,64]{0,1:T(8,128)S(1)}, f32[768,64]{0,1:T(8,128)S(1)}, u32[]{:S(2)}, u32[]{:S(2)}) %collective-permute-start.16) | collective-permute-done | bytes 196640 | tf_op jit(solution)/shard_map/ppermute | solution.py:62
  183.1 5.5 %collective-permute-start.18 = (bf16[24,8192]{1,0:T(8,128)(2,1)S(1)}, bf16[24,8192]{1,0:T(8,128)(2,1)S(1)}, u32[]{:S(2)}, u32[]{:S(2)}) collective-permute-start(bf16[24,8192]{1,0:T(8,128)(2,1)S(1)} %slice.75), channel_id=1, source_target_pairs={{0,1},{1,2},{2,3},{3,4},{4,5},{5,6},{6,7},{7,0},{8,9},{9,10},{10,1... | collective-permute-start | bytes 1179656 | tf_op jit(solution)/shard_map/ppermute | solution.py:62
  197.3 3.7 %collective-permute-done.20 = f32[768,64]{0,1:T(8,128)S(1)} collective-permute-done((f32[768,64]{0,1:T(8,128)S(1)}, f32[768,64]{0,1:T(8,128)S(1)}, u32[]{:S(2)}, u32[]{:S(2)}) %collective-permute-start.20) | collective-permute-done | bytes 196640 | tf_op jit(solution)/shard_map/ppermute | solution.py:62
  (102 shorter events, 38.2 us)
Async XLA Ops:
  4.8 34.5 %all-to-all-start.1 = ((bf16[16,128,512]{2,1,0:T(8,128)(2,1)}), bf16[16,128,512]{2,1,0:T(8,128)(2,1)S(1)}, u32[]{:S(2)}, u32[]{:S(2)}) async-start(bf16[16,128,512]{2,1,0:T(8,128)(2,1)} %broadcast_select_fusion), calls=%async_computation.1 | async-start | bytes 4194304 | tf_op jit(solution)/shard_map/all_to_all | solution.py:42
  10.8 40.1 %collective-permute-start.1 = (bf16[48,8192]{1,0:T(8,128)(2,1)S(1)}, bf16[48,8192]{1,0:T(8,128)(2,1)}, u32[]{:S(2)}, u32[]{:S(2)}) collective-permute-start(bf16[48,8192]{1,0:T(8,128)(2,1)S(1)} %copy-done.2), channel_id=1, source_target_pairs={{0,7},{1,0},{2,1},{3,2},{4,3},{5,4},{6,5},{7,6},{8,15},{9,8},{10,9... | collective-permute-start | bytes 2359304 | tf_op jit(solution)/shard_map/ppermute | solution.py:62
  16.7 37.6 %collective-permute-start = (bf16[48,8192]{1,0:T(8,128)(2,1)S(1)}, bf16[48,8192]{1,0:T(8,128)(2,1)}, u32[]{:S(2)}, u32[]{:S(2)}) collective-permute-start(bf16[48,8192]{1,0:T(8,128)(2,1)S(1)} %copy-done.2), channel_id=1, source_target_pairs={{0,8},{1,9},{2,10},{3,11},{4,12},{5,13},{6,14},{7,15},{8,0},{9,1},... | collective-permute-start | bytes 2359304 | tf_op jit(solution)/shard_map/ppermute | solution.py:62
  19.6 34.7 %collective-permute-start.2 = (bf16[48,8192]{1,0:T(8,128)(2,1)S(1)}, bf16[48,8192]{1,0:T(8,128)(2,1)}, u32[]{:S(2)}, u32[]{:S(2)}) collective-permute-start(bf16[48,8192]{1,0:T(8,128)(2,1)S(1)} %copy-done.2), channel_id=1, source_target_pairs={{0,1},{1,2},{2,3},{3,4},{4,5},{5,6},{6,7},{7,0},{8,9},{9,10},{10,1... | collective-permute-start | bytes 2359304 | tf_op jit(solution)/shard_map/ppermute | solution.py:62
  39.3 35.4 %all-to-all-start = ((bf16[48,16,512]{2,0,1:T(8,128)(2,1)}), bf16[48,16,512]{2,0,1:T(8,128)(2,1)}, u32[]{:S(2)}, u32[]{:S(2)}) async-start(bf16[48,16,512]{2,0,1:T(8,128)(2,1)} %bitcast.133), calls=%async_computation | async-start | bytes 1572864 | tf_op jit(solution)/shard_map/all_to_all | solution.py:69
  54.3 50.3 %collective-permute-start.6 = (bf16[48,8192]{1,0:T(8,128)(2,1)}, bf16[48,8192]{1,0:T(8,128)(2,1)}, u32[]{:S(2)}, u32[]{:S(2)}) collective-permute-start(bf16[48,8192]{1,0:T(8,128)(2,1)} %collective-permute-done), channel_id=1, source_target_pairs={{0,1},{1,2},{2,3},{3,4},{4,5},{5,6},{6,7},{7,0},{8,9},{9,10},{10,1... | collective-permute-start | bytes 2359304 | tf_op jit(solution)/shard_map/ppermute | solution.py:62
  56.6 47.9 %collective-permute-start.5 = (bf16[48,8192]{1,0:T(8,128)(2,1)}, bf16[48,8192]{1,0:T(8,128)(2,1)}, u32[]{:S(2)}, u32[]{:S(2)}) collective-permute-start(bf16[48,8192]{1,0:T(8,128)(2,1)} %collective-permute-done), channel_id=1, source_target_pairs={{0,7},{1,0},{2,1},{3,2},{4,3},{5,4},{6,5},{7,6},{8,15},{9,8},{10,9... | collective-permute-start | bytes 2359304 | tf_op jit(solution)/shard_map/ppermute | solution.py:62
  61.5 41.9 %collective-permute-start.3 = (bf16[48,8192]{1,0:T(8,128)(2,1)}, bf16[48,8192]{1,0:T(8,128)(2,1)}, u32[]{:S(2)}, u32[]{:S(2)}) collective-permute-start(bf16[48,8192]{1,0:T(8,128)(2,1)} %collective-permute-done.1), channel_id=1, source_target_pairs={{0,7},{1,0},{2,1},{3,2},{4,3},{5,4},{6,5},{7,6},{8,15},{9,8},{10,9... | collective-permute-start | bytes 2359304 | tf_op jit(solution)/shard_map/ppermute | solution.py:62
  63.5 41.0 %collective-permute-start.4 = (bf16[48,8192]{1,0:T(8,128)(2,1)}, bf16[48,8192]{1,0:T(8,128)(2,1)}, u32[]{:S(2)}, u32[]{:S(2)}) collective-permute-start(bf16[48,8192]{1,0:T(8,128)(2,1)} %collective-permute-done.2), channel_id=1, source_target_pairs={{0,1},{1,2},{2,3},{3,4},{4,5},{5,6},{6,7},{7,0},{8,9},{9,10},{10,1... | collective-permute-start | bytes 2359304 | tf_op jit(solution)/shard_map/ppermute | solution.py:62
  104.6 48.1 %slice-start = ((s8[8388608]{0:T(1024)(128)(4,1)}), s8[4194304]{0:T(1024)(128)(4,1)S(1)}, s32[]{:S(2)}) async-start(s8[8388608]{0:T(1024)(128)(4,1)} %bitcast.130), calls=%async_computation.2 | async-start | bytes 8388608
  106.5 14.5 %collective-permute-start.11 = (f32[768,64]{0,1:T(8,128)S(1)}, f32[768,64]{0,1:T(8,128)S(1)}, u32[]{:S(2)}, u32[]{:S(2)}) collective-permute-start(f32[768,64]{0,1:T(8,128)S(1)} %select_reduce_fusion), channel_id=1, source_target_pairs={{0,8},{1,9},{2,10},{3,11},{4,12},{5,13},{6,14},{7,15},{8,0},{9,1},... | collective-permute-start | bytes 589832 | tf_op jit(solution)/shard_map/ppermute | solution.py:62
  109.6 20.6 %collective-permute-start.7 = (bf16[48,8192]{1,0:T(8,128)(2,1)}, bf16[48,8192]{1,0:T(8,128)(2,1)S(1)}, u32[]{:S(2)}, u32[]{:S(2)}) collective-permute-start(bf16[48,8192]{1,0:T(8,128)(2,1)} %collective-permute-done.3), channel_id=1, source_target_pairs={{0,7},{1,0},{2,1},{3,2},{4,3},{5,4},{6,5},{7,6},{8,15},{9,8},{10,9... | collective-permute-start | bytes 2359304 | tf_op jit(solution)/shard_map/ppermute | solution.py:62
  111.0 21.8 %collective-permute-start.8 = (bf16[48,8192]{1,0:T(8,128)(2,1)}, bf16[48,8192]{1,0:T(8,128)(2,1)S(1)}, u32[]{:S(2)}, u32[]{:S(2)}) collective-permute-start(bf16[48,8192]{1,0:T(8,128)(2,1)} %collective-permute-done.4), channel_id=1, source_target_pairs={{0,1},{1,2},{2,3},{3,4},{4,5},{5,6},{6,7},{7,0},{8,9},{9,10},{10,1... | collective-permute-start | bytes 2359304 | tf_op jit(solution)/shard_map/ppermute | solution.py:62
  111.6 33.3 %collective-permute-start.9 = (bf16[48,8192]{1,0:T(8,128)(2,1)}, bf16[48,8192]{1,0:T(8,128)(2,1)S(1)}, u32[]{:S(2)}, u32[]{:S(2)}) collective-permute-start(bf16[48,8192]{1,0:T(8,128)(2,1)} %collective-permute-done.5), channel_id=1, source_target_pairs={{0,7},{1,0},{2,1},{3,2},{4,3},{5,4},{6,5},{7,6},{8,15},{9,8},{10,9... | collective-permute-start | bytes 2359304 | tf_op jit(solution)/shard_map/ppermute | solution.py:62
  114.3 33.0 %collective-permute-start.10 = (bf16[48,8192]{1,0:T(8,128)(2,1)}, bf16[48,8192]{1,0:T(8,128)(2,1)S(1)}, u32[]{:S(2)}, u32[]{:S(2)}) collective-permute-start(bf16[48,8192]{1,0:T(8,128)(2,1)} %collective-permute-done.6), channel_id=1, source_target_pairs={{0,1},{1,2},{2,3},{3,4},{4,5},{5,6},{6,7},{7,0},{8,9},{9,10},{10,1... | collective-permute-start | bytes 2359304 | tf_op jit(solution)/shard_map/ppermute | solution.py:62
  147.4 34.8 %collective-permute-start.13 = (bf16[24,8192]{1,0:T(8,128)(2,1)S(1)}, bf16[24,8192]{1,0:T(8,128)(2,1)S(1)}, u32[]{:S(2)}, u32[]{:S(2)}) collective-permute-start(bf16[24,8192]{1,0:T(8,128)(2,1)S(1)} %slice.65), channel_id=1, source_target_pairs={{0,1},{1,2},{2,3},{3,4},{4,5},{5,6},{6,7},{7,0},{8,9},{9,10},{10,1... | collective-permute-start | bytes 1179656 | tf_op jit(solution)/shard_map/ppermute | solution.py:62
  147.4 34.7 %collective-permute-start.12 = (bf16[24,8192]{1,0:T(8,128)(2,1)S(1)}, bf16[24,8192]{1,0:T(8,128)(2,1)S(1)}, u32[]{:S(2)}, u32[]{:S(2)}) collective-permute-start(bf16[24,8192]{1,0:T(8,128)(2,1)S(1)} %slice.64), channel_id=1, source_target_pairs={{0,7},{1,0},{2,1},{3,2},{4,3},{5,4},{6,5},{7,6},{8,15},{9,8},{10,9... | collective-permute-start | bytes 1179656 | tf_op jit(solution)/shard_map/ppermute | solution.py:62
  150.7 31.5 %collective-permute-start.14 = (bf16[48,8192]{1,0:T(8,128)(2,1)S(1)}, bf16[48,8192]{1,0:T(8,128)(2,1)S(1)}, u32[]{:S(2)}, u32[]{:S(2)}) collective-permute-start(bf16[48,8192]{1,0:T(8,128)(2,1)S(1)} %collective-permute-done.9), channel_id=1, source_target_pairs={{0,7},{1,0},{2,1},{3,2},{4,3},{5,4},{6,5},{7,6},{8,15},{9,8},{10,9... | collective-permute-start | bytes 2359304 | tf_op jit(solution)/shard_map/ppermute | solution.py:62
  150.7 32.2 %collective-permute-start.15 = (bf16[48,8192]{1,0:T(8,128)(2,1)S(1)}, bf16[48,8192]{1,0:T(8,128)(2,1)S(1)}, u32[]{:S(2)}, u32[]{:S(2)}) collective-permute-start(bf16[48,8192]{1,0:T(8,128)(2,1)S(1)} %collective-permute-done.10), channel_id=1, source_target_pairs={{0,1},{1,2},{2,3},{3,4},{4,5},{5,6},{6,7},{7,0},{8,9},{9,10},{10,1... | collective-permute-start | bytes 2359304 | tf_op jit(solution)/shard_map/ppermute | solution.py:62
  154.5 27.6 %collective-permute-start.16 = (f32[768,64]{0,1:T(8,128)S(1)}, f32[768,64]{0,1:T(8,128)S(1)}, u32[]{:S(2)}, u32[]{:S(2)}) collective-permute-start(f32[768,64]{0,1:T(8,128)S(1)} %add.86), channel_id=1, source_target_pairs={{0,4},{1,5},{2,6},{3,7},{4,0},{5,1},{6,2},{7,3},{8,12},{9,13},{10,... | collective-permute-start | bytes 589832 | tf_op jit(solution)/shard_map/ppermute | solution.py:62
  183.0 12.1 %collective-permute-start.19 = (f32[768,64]{0,1:T(8,128)S(1)}, f32[768,64]{0,1:T(8,128)S(1)}, u32[]{:S(2)}, u32[]{:S(2)}) collective-permute-start(f32[768,64]{0,1:T(8,128)S(1)} %add.87), channel_id=1, source_target_pairs={{0,2},{1,3},{2,0},{3,1},{4,6},{5,7},{6,4},{7,5},{8,10},{9,11},{10,... | collective-permute-start | bytes 589832 | tf_op jit(solution)/shard_map/ppermute | solution.py:62
  183.1 17.9 %collective-permute-start.18 = (bf16[24,8192]{1,0:T(8,128)(2,1)S(1)}, bf16[24,8192]{1,0:T(8,128)(2,1)S(1)}, u32[]{:S(2)}, u32[]{:S(2)}) collective-permute-start(bf16[24,8192]{1,0:T(8,128)(2,1)S(1)} %slice.75), channel_id=1, source_target_pairs={{0,1},{1,2},{2,3},{3,4},{4,5},{5,6},{6,7},{7,0},{8,9},{9,10},{10,1... | collective-permute-start | bytes 1179656 | tf_op jit(solution)/shard_map/ppermute | solution.py:62
  188.5 12.4 %collective-permute-start.17 = (bf16[24,8192]{1,0:T(8,128)(2,1)S(1)}, bf16[24,8192]{1,0:T(8,128)(2,1)S(1)}, u32[]{:S(2)}, u32[]{:S(2)}) collective-permute-start(bf16[24,8192]{1,0:T(8,128)(2,1)S(1)} %slice.74), channel_id=1, source_target_pairs={{0,7},{1,0},{2,1},{3,2},{4,3},{5,4},{6,5},{7,6},{8,15},{9,8},{10,9... | collective-permute-start | bytes 1179656 | tf_op jit(solution)/shard_map/ppermute | solution.py:62
  195.1 5.8 %collective-permute-start.20 = (f32[768,64]{0,1:T(8,128)S(1)}, f32[768,64]{0,1:T(8,128)S(1)}, u32[]{:S(2)}, u32[]{:S(2)}) collective-permute-start(f32[768,64]{0,1:T(8,128)S(1)} %add.91), channel_id=1, source_target_pairs={{0,1},{1,0},{2,3},{3,2},{4,5},{5,4},{6,7},{7,6},{8,9},{9,8},{10,11... | collective-permute-start | bytes 589832 | tf_op jit(solution)/shard_map/ppermute | solution.py:62
  (6 other events, 75.8 us)

commit v8 on v7

--- a/solution.py
+++ b/solution.py
@@ -81,7 +81,8 @@
         step //= 2
 
     def sum_step(value, mask):
-        return value + hop(value, [(i, i ^ mask) for i in range(members)])
+        sent = hop(value.astype(jnp.bfloat16), [(i, i ^ mask) for i in range(members)])
+        return value + sent.astype(jnp.float32)
 
     own_pieces = [tokens] + [None] * (ring - 1)
     partner_pieces = [None] * ring

time: 209 us -> 197 us (0.943)
  waiting for transfers between devices: 103 us -> 91.4 us
  starting transfers between devices: 60.4 us -> 57.7 us
  matrix products: 25.3 us -> 27.8 us
    ppermute x21, waiting for transfers between devices: 86.2 us -> 75.1 us  [hop(): return lax.ppermute(value, 'tensor', pairs)]
    ppermute x21, starting transfers between devices: 43.4 us -> 40.7 us  [hop(): return lax.ppermute(value, 'tensor', pairs)]
    dot_general x6, matrix products: 21.9 us -> 24.6 us  [on_device(): product = jnp.dot(stacked, q_weight, preferred_element_type=jnp.float32)]
  transfers between devices with their start and end apart: 23 -> 23, of which waited for: 12 -> 13; matrix products, arithmetic and copies ran while one was open for 15% -> 18% of each run, Pallas kernels for 0% -> 0%
where the time goes in v8:
time: 197 us
  waiting for transfers between devices  91.4 us (46%)
  starting transfers between devices  57.7 us (29%)
  matrix products  27.8 us (14%)
  local copies, waits for them, and re-layouts  15.9 us (8%)
  other arithmetic  3.84 us (2%)
    ppermute x21, waiting for transfers between devices, hop(): return lax.ppermute(value, 'tensor', pairs)  75.1 us
    ppermute x21, starting transfers between devices, hop(): return lax.ppermute(value, 'tensor', pairs)  40.7 us
    dot_general x6, matrix products, on_device(): product = jnp.dot(stacked, q_weight, preferred_element_type=jnp.float32)  24.6 us
    all_to_all x1, waiting for transfers between devices, on_device(): recv = lax.all_to_all(send, 'dp', 0, 0, tiled=True)  12.7 us
    all_to_all x1, starting transfers between devices, on_device(): local_cols = lax.all_to_all(tokens, 'tensor', 1, 0, tiled=True)  11 us
    unnamed x36, local copies, waits for them, and re-layouts  9.97 us
    all_to_all x1, starting transfers between devices, on_device(): recv = lax.all_to_all(send, 'dp', 0, 0, tiled=True)  5.99 us
  transfers between devices with their start and end apart: 23, of which 13 were waited for; matrix products, arithmetic and copies ran while one was open for 18% of the time, Pallas kernels for 0%

profile of v8, /device:TPU:2, one launch (start us, length us, event | category | flops | bytes accessed | tf_op | source)
XLA Modules:
  0.0 197.1 jit_solution(1608396104146888113)
XLA Ops:
  4.8 6.0 %all-to-all-start.1 = ((bf16[16,128,512]{2,1,0:T(8,128)(2,1)}), bf16[16,128,512]{2,1,0:T(8,128)(2,1)S(1)}, u32[]{:S(2)}, u32[]{:S(2)}) async-start(bf16[16,128,512]{2,1,0:T(8,128)(2,1)} %broadcast_select_fusion), calls=%async_computation.1 | async-start | bytes 4194304 | tf_op jit(solution)/shard_map/all_to_all | solution.py:42
  10.8 5.9 %collective-permute-start.1 = (bf16[48,8192]{1,0:T(8,128)(2,1)S(1)}, bf16[48,8192]{1,0:T(8,128)(2,1)}, u32[]{:S(2)}, u32[]{:S(2)}) collective-permute-start(bf16[48,8192]{1,0:T(8,128)(2,1)S(1)} %copy-done.2), channel_id=1, source_target_pairs={{0,7},{1,0},{2,1},{3,2},{4,3},{5,4},{6,5},{7,6},{8,15},{9,8},{10,9... | collective-permute-start | bytes 2359304 | tf_op jit(solution)/shard_map/ppermute | solution.py:62
  16.7 2.9 %collective-permute-start = (bf16[48,8192]{1,0:T(8,128)(2,1)S(1)}, bf16[48,8192]{1,0:T(8,128)(2,1)}, u32[]{:S(2)}, u32[]{:S(2)}) collective-permute-start(bf16[48,8192]{1,0:T(8,128)(2,1)S(1)} %copy-done.2), channel_id=1, source_target_pairs={{0,8},{1,9},{2,10},{3,11},{4,12},{5,13},{6,14},{7,15},{8,0},{9,1},... | collective-permute-start | bytes 2359304 | tf_op jit(solution)/shard_map/ppermute | solution.py:62
  21.1 5.6 %constant_dynamic-update-slice_fusion.1 = (f32[16,48,512]{2,1,0:T(8,128)}, f32[1,48,512]{2,1,0:T(8,128)S(1)}) fusion(bf16[48,8192]{1,0:T(8,128)(2,1)S(1)} %copy-done.2, bf16[8192,512]{1,0:T(8,128)(2,1)} %param.8), kind=kOutput, calls=%fused_computation.104 | convolution fusion | flops 402653184 | bytes 9371648 | tf_op jit(solution)/shard_map/dot_general | solution.py:151
  26.6 12.7 %all-to-all-done.1 = bf16[16,128,512]{2,1,0:T(8,128)(2,1)S(1)} async-done(((bf16[16,128,512]{2,1,0:T(8,128)(2,1)}), bf16[16,128,512]{2,1,0:T(8,128)(2,1)S(1)}, u32[]{:S(2)}, u32[]{:S(2)}) %all-to-all-start.1) | async-done | bytes 2097184 | tf_op jit(solution)/shard_map/all_to_all | solution.py:42
  39.3 11.0 %all-to-all-start = ((bf16[48,16,512]{2,0,1:T(8,128)(2,1)}), bf16[48,16,512]{2,0,1:T(8,128)(2,1)}, u32[]{:S(2)}, u32[]{:S(2)}) async-start(bf16[48,16,512]{2,0,1:T(8,128)(2,1)} %bitcast.133), calls=%async_computation | async-start | bytes 1572864 | tf_op jit(solution)/shard_map/all_to_all | solution.py:69
  50.9 3.4 %collective-permute-done = bf16[48,8192]{1,0:T(8,128)(2,1)} collective-permute-done((bf16[48,8192]{1,0:T(8,128)(2,1)S(1)}, bf16[48,8192]{1,0:T(8,128)(2,1)}, u32[]{:S(2)}, u32[]{:S(2)}) %collective-permute-start) | collective-permute-done | bytes 786464 | tf_op jit(solution)/shard_map/ppermute | solution.py:62
  56.6 4.9 %collective-permute-start.5 = (bf16[48,8192]{1,0:T(8,128)(2,1)}, bf16[48,8192]{1,0:T(8,128)(2,1)}, u32[]{:S(2)}, u32[]{:S(2)}) collective-permute-start(bf16[48,8192]{1,0:T(8,128)(2,1)} %collective-permute-done), channel_id=1, source_target_pairs={{0,7},{1,0},{2,1},{3,2},{4,3},{5,4},{6,5},{7,6},{8,15},{9,8},{10,9... | collective-permute-start | bytes 2359304 | tf_op jit(solution)/shard_map/ppermute | solution.py:62
  63.5 5.5 %fusion.16 = f32[144,512]{1,0:T(8,128)S(1)} fusion(bf16[8192,512]{1,0:T(8,128)(2,1)} %param.8, bf16[48,8192]{1,0:T(8,128)(2,1)} %collective-permute-done, bf16[48,8192]{1,0:T(8,128)(2,1)} %collective-permute-done.2, bf16[48,8192]{1,0:T(8,128)(2,1)} %collective-permute-done.1), kind=kOutput, calls=%fused_computation.19 | convolution fusion | flops 1215037440 | bytes 11042816 | tf_op jit(solution)/shard_map/dot_general | solution.py:151
  71.1 3.6 %all-to-all-done = bf16[48,16,512]{2,0,1:T(8,128)(2,1)} async-done(((bf16[48,16,512]{2,0,1:T(8,128)(2,1)}), bf16[48,16,512]{2,0,1:T(8,128)(2,1)}, u32[]{:S(2)}, u32[]{:S(2)}) %all-to-all-start) | async-done | bytes 786464 | tf_op jit(solution)/shard_map/all_to_all | solution.py:69
  74.7 28.6 %collective-permute-done.3 = bf16[48,8192]{1,0:T(8,128)(2,1)} collective-permute-done((bf16[48,8192]{1,0:T(8,128)(2,1)}, bf16[48,8192]{1,0:T(8,128)(2,1)}, u32[]{:S(2)}, u32[]{:S(2)}) %collective-permute-start.3) | collective-permute-done | bytes 786464 | tf_op jit(solution)/shard_map/ppermute | solution.py:62
  106.6 2.7 %collective-permute-start.9 = (bf16[48,8192]{1,0:T(8,128)(2,1)}, bf16[48,8192]{1,0:T(8,128)(2,1)S(1)}, u32[]{:S(2)}, u32[]{:S(2)}) collective-permute-start(bf16[48,8192]{1,0:T(8,128)(2,1)} %collective-permute-done.5), channel_id=1, source_target_pairs={{0,7},{1,0},{2,1},{3,2},{4,3},{5,4},{6,5},{7,6},{8,15},{9,8},{10,9... | collective-permute-start | bytes 2359304 | tf_op jit(solution)/shard_map/ppermute | solution.py:62
  109.3 6.1 %fusion = f32[192,512]{1,0:T(8,128)S(1)} fusion(bf16[8192,512]{1,0:T(8,128)(2,1)} %param.8, bf16[48,8192]{1,0:T(8,128)(2,1)} %collective-permute-done.6, bf16[48,8192]{1,0:T(8,128)(2,1)} %collective-permute-done.5, bf16[48,8192]{1,0:T(8,128)(2,1)} %collective-permute-done.4, bf16[48,8192]{1,0:T(8,128)(2,1)} %collective-permute-done.3), kind=kOutput, calls=%fused_computation.3 | convolution fusion | flops 1623195648 | bytes 11927552 | tf_op jit(solution)/shard_map/dot_general | solution.py:151
  117.2 3.1 %collective-permute-start.11 = (bf16[768,64]{0,1:T(8,128)(2,1)S(1)}, bf16[768,64]{0,1:T(8,128)(2,1)S(1)}, u32[]{:S(2)}, u32[]{:S(2)}) collective-permute-start(bf16[768,64]{0,1:T(8,128)(2,1)S(1)} %convert_element_type.34), channel_id=1, source_target_pairs={{0,8},{1,9},{2,10},{3,11},{4,12},{5,13},{6,14},{7,15},{8,0},{9,1},... | collective-permute-start | bytes 294920 | tf_op jit(solution)/shard_map/ppermute | solution.py:62
  120.9 2.5 %collective-permute-done.11 = bf16[768,64]{0,1:T(8,128)(2,1)S(1)} collective-permute-done((bf16[768,64]{0,1:T(8,128)(2,1)S(1)}, bf16[768,64]{0,1:T(8,128)(2,1)S(1)}, u32[]{:S(2)}, u32[]{:S(2)}) %collective-permute-start.11) | collective-permute-done | bytes 98336 | tf_op jit(solution)/shard_map/ppermute | solution.py:62
  125.2 2.7 %collective-permute-done.8 = bf16[48,8192]{1,0:T(8,128)(2,1)S(1)} collective-permute-done((bf16[48,8192]{1,0:T(8,128)(2,1)}, bf16[48,8192]{1,0:T(8,128)(2,1)S(1)}, u32[]{:S(2)}, u32[]{:S(2)}) %collective-permute-start.8) | collective-permute-done | bytes 786464 | tf_op jit(solution)/shard_map/ppermute | solution.py:62
  127.9 12.3 %collective-permute-done.9 = bf16[48,8192]{1,0:T(8,128)(2,1)S(1)} collective-permute-done((bf16[48,8192]{1,0:T(8,128)(2,1)}, bf16[48,8192]{1,0:T(8,128)(2,1)S(1)}, u32[]{:S(2)}, u32[]{:S(2)}) %collective-permute-start.9) | collective-permute-done | bytes 786464 | tf_op jit(solution)/shard_map/ppermute | solution.py:62
  140.2 2.4 %collective-permute-done.10 = bf16[48,8192]{1,0:T(8,128)(2,1)S(1)} collective-permute-done((bf16[48,8192]{1,0:T(8,128)(2,1)}, bf16[48,8192]{1,0:T(8,128)(2,1)S(1)}, u32[]{:S(2)}, u32[]{:S(2)}) %collective-permute-start.10) | collective-permute-done | bytes 786464 | tf_op jit(solution)/shard_map/ppermute | solution.py:62
  144.6 4.5 %fusion.8 = f32[192,512]{1,0:T(8,128)S(1)} fusion(bf16[8192,512]{1,0:T(8,128)(2,1)} %param.8, bf16[48,8192]{1,0:T(8,128)(2,1)S(1)} %collective-permute-done.10, bf16[48,8192]{1,0:T(8,128)(2,1)S(1)} %collective-permute-done.9, bf16[48,8192]{1,0:T(8,128)(2,1)S(1)} %collective-permute-done.8, bf16[48,8192]{1,0:T(8,128)(2,1)S(1)} %collective-permute-done.7), kind=kOutput, calls=%fused_computation.11 | convolution fusion | flops 1623195648 | bytes 11927552 | tf_op jit(solution)/shard_map/dot_general | solution.py:151
  149.2 4.7 %collective-permute-start.16 = (bf16[768,64]{0,1:T(8,128)(2,1)S(1)}, bf16[768,64]{0,1:T(8,128)(2,1)S(1)}, u32[]{:S(2)}, u32[]{:S(2)}) collective-permute-start(bf16[768,64]{0,1:T(8,128)(2,1)S(1)} %convert_element_type.36), channel_id=1, source_target_pairs={{0,4},{1,5},{2,6},{3,7},{4,0},{5,1},{6,2},{7,3},{8,12},{9,13},{10,... | collective-permute-start | bytes 294920 | tf_op jit(solution)/shard_map/ppermute | solution.py:62
  153.9 3.2 %collective-permute-start.12 = (bf16[24,8192]{1,0:T(8,128)(2,1)S(1)}, bf16[24,8192]{1,0:T(8,128)(2,1)S(1)}, u32[]{:S(2)}, u32[]{:S(2)}) collective-permute-start(bf16[24,8192]{1,0:T(8,128)(2,1)S(1)} %slice.64), channel_id=1, source_target_pairs={{0,7},{1,0},{2,1},{3,2},{4,3},{5,4},{6,5},{7,6},{8,15},{9,8},{10,9... | collective-permute-start | bytes 1179656 | tf_op jit(solution)/shard_map/ppermute | solution.py:62
  157.7 14.1 %collective-permute-done.16 = bf16[768,64]{0,1:T(8,128)(2,1)S(1)} collective-permute-done((bf16[768,64]{0,1:T(8,128)(2,1)S(1)}, bf16[768,64]{0,1:T(8,128)(2,1)S(1)}, u32[]{:S(2)}, u32[]{:S(2)}) %collective-permute-start.16) | collective-permute-done | bytes 98336 | tf_op jit(solution)/shard_map/ppermute | solution.py:62
  174.3 2.8 %collective-permute-start.18 = (bf16[24,8192]{1,0:T(8,128)(2,1)S(1)}, bf16[24,8192]{1,0:T(8,128)(2,1)S(1)}, u32[]{:S(2)}, u32[]{:S(2)}) collective-permute-start(bf16[24,8192]{1,0:T(8,128)(2,1)S(1)} %slice.75), channel_id=1, source_target_pairs={{0,1},{1,2},{2,3},{3,4},{4,5},{5,6},{6,7},{7,0},{8,9},{9,10},{10,1... | collective-permute-start | bytes 1179656 | tf_op jit(solution)/shard_map/ppermute | solution.py:62
  185.9 3.8 %collective-permute-done.20 = bf16[768,64]{0,1:T(8,128)(2,1)S(1)} collective-permute-done((bf16[768,64]{0,1:T(8,128)(2,1)S(1)}, bf16[768,64]{0,1:T(8,128)(2,1)S(1)}, u32[]{:S(2)}, u32[]{:S(2)}) %collective-permute-start.20) | collective-permute-done | bytes 98336 | tf_op jit(solution)/shard_map/ppermute | solution.py:62
  (105 shorter events, 41.9 us)
Async XLA Ops:
  4.8 34.5 %all-to-all-start.1 = ((bf16[16,128,512]{2,1,0:T(8,128)(2,1)}), bf16[16,128,512]{2,1,0:T(8,128)(2,1)S(1)}, u32[]{:S(2)}, u32[]{:S(2)}) async-start(bf16[16,128,512]{2,1,0:T(8,128)(2,1)} %broadcast_select_fusion), calls=%async_computation.1 | async-start | bytes 4194304 | tf_op jit(solution)/shard_map/all_to_all | solution.py:42
  10.8 40.1 %collective-permute-start.1 = (bf16[48,8192]{1,0:T(8,128)(2,1)S(1)}, bf16[48,8192]{1,0:T(8,128)(2,1)}, u32[]{:S(2)}, u32[]{:S(2)}) collective-permute-start(bf16[48,8192]{1,0:T(8,128)(2,1)S(1)} %copy-done.2), channel_id=1, source_target_pairs={{0,7},{1,0},{2,1},{3,2},{4,3},{5,4},{6,5},{7,6},{8,15},{9,8},{10,9... | collective-permute-start | bytes 2359304 | tf_op jit(solution)/shard_map/ppermute | solution.py:62
  16.7 37.6 %collective-permute-start = (bf16[48,8192]{1,0:T(8,128)(2,1)S(1)}, bf16[48,8192]{1,0:T(8,128)(2,1)}, u32[]{:S(2)}, u32[]{:S(2)}) collective-permute-start(bf16[48,8192]{1,0:T(8,128)(2,1)S(1)} %copy-done.2), channel_id=1, source_target_pairs={{0,8},{1,9},{2,10},{3,11},{4,12},{5,13},{6,14},{7,15},{8,0},{9,1},... | collective-permute-start | bytes 2359304 | tf_op jit(solution)/shard_map/ppermute | solution.py:62
  19.6 34.7 %collective-permute-start.2 = (bf16[48,8192]{1,0:T(8,128)(2,1)S(1)}, bf16[48,8192]{1,0:T(8,128)(2,1)}, u32[]{:S(2)}, u32[]{:S(2)}) collective-permute-start(bf16[48,8192]{1,0:T(8,128)(2,1)S(1)} %copy-done.2), channel_id=1, source_target_pairs={{0,1},{1,2},{2,3},{3,4},{4,5},{5,6},{6,7},{7,0},{8,9},{9,10},{10,1... | collective-permute-start | bytes 2359304 | tf_op jit(solution)/shard_map/ppermute | solution.py:62
  39.3 35.4 %all-to-all-start = ((bf16[48,16,512]{2,0,1:T(8,128)(2,1)}), bf16[48,16,512]{2,0,1:T(8,128)(2,1)}, u32[]{:S(2)}, u32[]{:S(2)}) async-start(bf16[48,16,512]{2,0,1:T(8,128)(2,1)} %bitcast.133), calls=%async_computation | async-start | bytes 1572864 | tf_op jit(solution)/shard_map/all_to_all | solution.py:69
  54.3 50.3 %collective-permute-start.6 = (bf16[48,8192]{1,0:T(8,128)(2,1)}, bf16[48,8192]{1,0:T(8,128)(2,1)}, u32[]{:S(2)}, u32[]{:S(2)}) collective-permute-start(bf16[48,8192]{1,0:T(8,128)(2,1)} %collective-permute-done), channel_id=1, source_target_pairs={{0,1},{1,2},{2,3},{3,4},{4,5},{5,6},{6,7},{7,0},{8,9},{9,10},{10,1... | collective-permute-start | bytes 2359304 | tf_op jit(solution)/shard_map/ppermute | solution.py:62
  56.6 47.9 %collective-permute-start.5 = (bf16[48,8192]{1,0:T(8,128)(2,1)}, bf16[48,8192]{1,0:T(8,128)(2,1)}, u32[]{:S(2)}, u32[]{:S(2)}) collective-permute-start(bf16[48,8192]{1,0:T(8,128)(2,1)} %collective-permute-done), channel_id=1, source_target_pairs={{0,7},{1,0},{2,1},{3,2},{4,3},{5,4},{6,5},{7,6},{8,15},{9,8},{10,9... | collective-permute-start | bytes 2359304 | tf_op jit(solution)/shard_map/ppermute | solution.py:62
  61.5 41.9 %collective-permute-start.3 = (bf16[48,8192]{1,0:T(8,128)(2,1)}, bf16[48,8192]{1,0:T(8,128)(2,1)}, u32[]{:S(2)}, u32[]{:S(2)}) collective-permute-start(bf16[48,8192]{1,0:T(8,128)(2,1)} %collective-permute-done.1), channel_id=1, source_target_pairs={{0,7},{1,0},{2,1},{3,2},{4,3},{5,4},{6,5},{7,6},{8,15},{9,8},{10,9... | collective-permute-start | bytes 2359304 | tf_op jit(solution)/shard_map/ppermute | solution.py:62
  63.5 41.0 %collective-permute-start.4 = (bf16[48,8192]{1,0:T(8,128)(2,1)}, bf16[48,8192]{1,0:T(8,128)(2,1)}, u32[]{:S(2)}, u32[]{:S(2)}) collective-permute-start(bf16[48,8192]{1,0:T(8,128)(2,1)} %collective-permute-done.2), channel_id=1, source_target_pairs={{0,1},{1,2},{2,3},{3,4},{4,5},{5,6},{6,7},{7,0},{8,9},{9,10},{10,1... | collective-permute-start | bytes 2359304 | tf_op jit(solution)/shard_map/ppermute | solution.py:62
  104.6 20.6 %collective-permute-start.7 = (bf16[48,8192]{1,0:T(8,128)(2,1)}, bf16[48,8192]{1,0:T(8,128)(2,1)S(1)}, u32[]{:S(2)}, u32[]{:S(2)}) collective-permute-start(bf16[48,8192]{1,0:T(8,128)(2,1)} %collective-permute-done.3), channel_id=1, source_target_pairs={{0,7},{1,0},{2,1},{3,2},{4,3},{5,4},{6,5},{7,6},{8,15},{9,8},{10,9... | collective-permute-start | bytes 2359304 | tf_op jit(solution)/shard_map/ppermute | solution.py:62
  106.0 21.8 %collective-permute-start.8 = (bf16[48,8192]{1,0:T(8,128)(2,1)}, bf16[48,8192]{1,0:T(8,128)(2,1)S(1)}, u32[]{:S(2)}, u32[]{:S(2)}) collective-permute-start(bf16[48,8192]{1,0:T(8,128)(2,1)} %collective-permute-done.4), channel_id=1, source_target_pairs={{0,1},{1,2},{2,3},{3,4},{4,5},{5,6},{6,7},{7,0},{8,9},{9,10},{10,1... | collective-permute-start | bytes 2359304 | tf_op jit(solution)/shard_map/ppermute | solution.py:62
  106.6 33.6 %collective-permute-start.9 = (bf16[48,8192]{1,0:T(8,128)(2,1)}, bf16[48,8192]{1,0:T(8,128)(2,1)S(1)}, u32[]{:S(2)}, u32[]{:S(2)}) collective-permute-start(bf16[48,8192]{1,0:T(8,128)(2,1)} %collective-permute-done.5), channel_id=1, source_target_pairs={{0,7},{1,0},{2,1},{3,2},{4,3},{5,4},{6,5},{7,6},{8,15},{9,8},{10,9... | collective-permute-start | bytes 2359304 | tf_op jit(solution)/shard_map/ppermute | solution.py:62
  109.3 33.3 %collective-permute-start.10 = (bf16[48,8192]{1,0:T(8,128)(2,1)}, bf16[48,8192]{1,0:T(8,128)(2,1)S(1)}, u32[]{:S(2)}, u32[]{:S(2)}) collective-permute-start(bf16[48,8192]{1,0:T(8,128)(2,1)} %collective-permute-done.6), channel_id=1, source_target_pairs={{0,1},{1,2},{2,3},{3,4},{4,5},{5,6},{6,7},{7,0},{8,9},{9,10},{10,1... | collective-permute-start | bytes 2359304 | tf_op jit(solution)/shard_map/ppermute | solution.py:62
  117.2 6.2 %collective-permute-start.11 = (bf16[768,64]{0,1:T(8,128)(2,1)S(1)}, bf16[768,64]{0,1:T(8,128)(2,1)S(1)}, u32[]{:S(2)}, u32[]{:S(2)}) collective-permute-start(bf16[768,64]{0,1:T(8,128)(2,1)S(1)} %convert_element_type.34), channel_id=1, source_target_pairs={{0,8},{1,9},{2,10},{3,11},{4,12},{5,13},{6,14},{7,15},{8,0},{9,1},... | collective-permute-start | bytes 294920 | tf_op jit(solution)/shard_map/ppermute | solution.py:62
  123.4 54.9 %slice-start = ((s8[8388608]{0:T(1024)(128)(4,1)}), s8[4194304]{0:T(1024)(128)(4,1)S(1)}, s32[]{:S(2)}) async-start(s8[8388608]{0:T(1024)(128)(4,1)} %bitcast.130), calls=%async_computation.2 | async-start | bytes 8388608
  142.6 31.6 %collective-permute-start.14 = (bf16[48,8192]{1,0:T(8,128)(2,1)S(1)}, bf16[48,8192]{1,0:T(8,128)(2,1)S(1)}, u32[]{:S(2)}, u32[]{:S(2)}) collective-permute-start(bf16[48,8192]{1,0:T(8,128)(2,1)S(1)} %collective-permute-done.9), channel_id=1, source_target_pairs={{0,7},{1,0},{2,1},{3,2},{4,3},{5,4},{6,5},{7,6},{8,15},{9,8},{10,9... | collective-permute-start | bytes 2359304 | tf_op jit(solution)/shard_map/ppermute | solution.py:62
  143.0 31.2 %collective-permute-start.15 = (bf16[48,8192]{1,0:T(8,128)(2,1)S(1)}, bf16[48,8192]{1,0:T(8,128)(2,1)S(1)}, u32[]{:S(2)}, u32[]{:S(2)}) collective-permute-start(bf16[48,8192]{1,0:T(8,128)(2,1)S(1)} %collective-permute-done.10), channel_id=1, source_target_pairs={{0,1},{1,2},{2,3},{3,4},{4,5},{5,6},{6,7},{7,0},{8,9},{9,10},{10,1... | collective-permute-start | bytes 2359304 | tf_op jit(solution)/shard_map/ppermute | solution.py:62
  149.2 22.6 %collective-permute-start.16 = (bf16[768,64]{0,1:T(8,128)(2,1)S(1)}, bf16[768,64]{0,1:T(8,128)(2,1)S(1)}, u32[]{:S(2)}, u32[]{:S(2)}) collective-permute-start(bf16[768,64]{0,1:T(8,128)(2,1)S(1)} %convert_element_type.36), channel_id=1, source_target_pairs={{0,4},{1,5},{2,6},{3,7},{4,0},{5,1},{6,2},{7,3},{8,12},{9,13},{10,... | collective-permute-start | bytes 294920 | tf_op jit(solution)/shard_map/ppermute | solution.py:62
  153.9 20.3 %collective-permute-start.13 = (bf16[24,8192]{1,0:T(8,128)(2,1)S(1)}, bf16[24,8192]{1,0:T(8,128)(2,1)S(1)}, u32[]{:S(2)}, u32[]{:S(2)}) collective-permute-start(bf16[24,8192]{1,0:T(8,128)(2,1)S(1)} %slice.65), channel_id=1, source_target_pairs={{0,1},{1,2},{2,3},{3,4},{4,5},{5,6},{6,7},{7,0},{8,9},{9,10},{10,1... | collective-permute-start | bytes 1179656 | tf_op jit(solution)/shard_map/ppermute | solution.py:62
  153.9 20.3 %collective-permute-start.12 = (bf16[24,8192]{1,0:T(8,128)(2,1)S(1)}, bf16[24,8192]{1,0:T(8,128)(2,1)S(1)}, u32[]{:S(2)}, u32[]{:S(2)}) collective-permute-start(bf16[24,8192]{1,0:T(8,128)(2,1)S(1)} %slice.64), channel_id=1, source_target_pairs={{0,7},{1,0},{2,1},{3,2},{4,3},{5,4},{6,5},{7,6},{8,15},{9,8},{10,9... | collective-permute-start | bytes 1179656 | tf_op jit(solution)/shard_map/ppermute | solution.py:62
  174.2 10.7 %collective-permute-start.19 = (bf16[768,64]{0,1:T(8,128)(2,1)S(1)}, bf16[768,64]{0,1:T(8,128)(2,1)S(1)}, u32[]{:S(2)}, u32[]{:S(2)}) collective-permute-start(bf16[768,64]{0,1:T(8,128)(2,1)S(1)} %convert_element_type.38), channel_id=1, source_target_pairs={{0,2},{1,3},{2,0},{3,1},{4,6},{5,7},{6,4},{7,5},{8,10},{9,11},{10,... | collective-permute-start | bytes 294920 | tf_op jit(solution)/shard_map/ppermute | solution.py:62
  174.3 15.3 %collective-permute-start.18 = (bf16[24,8192]{1,0:T(8,128)(2,1)S(1)}, bf16[24,8192]{1,0:T(8,128)(2,1)S(1)}, u32[]{:S(2)}, u32[]{:S(2)}) collective-permute-start(bf16[24,8192]{1,0:T(8,128)(2,1)S(1)} %slice.75), channel_id=1, source_target_pairs={{0,1},{1,2},{2,3},{3,4},{4,5},{5,6},{6,7},{7,0},{8,9},{9,10},{10,1... | collective-permute-start | bytes 1179656 | tf_op jit(solution)/shard_map/ppermute | solution.py:62
  177.1 12.6 %collective-permute-start.17 = (bf16[24,8192]{1,0:T(8,128)(2,1)S(1)}, bf16[24,8192]{1,0:T(8,128)(2,1)S(1)}, u32[]{:S(2)}, u32[]{:S(2)}) collective-permute-start(bf16[24,8192]{1,0:T(8,128)(2,1)S(1)} %slice.74), channel_id=1, source_target_pairs={{0,7},{1,0},{2,1},{3,2},{4,3},{5,4},{6,5},{7,6},{8,15},{9,8},{10,9... | collective-permute-start | bytes 1179656 | tf_op jit(solution)/shard_map/ppermute | solution.py:62
  184.9 4.7 %collective-permute-start.20 = (bf16[768,64]{0,1:T(8,128)(2,1)S(1)}, bf16[768,64]{0,1:T(8,128)(2,1)S(1)}, u32[]{:S(2)}, u32[]{:S(2)}) collective-permute-start(bf16[768,64]{0,1:T(8,128)(2,1)S(1)} %fusion.42), channel_id=1, source_target_pairs={{0,1},{1,0},{2,3},{3,2},{4,5},{5,4},{6,7},{7,6},{8,9},{9,8},{10,11... | collective-permute-start | bytes 294920 | tf_op jit(solution)/shard_map/ppermute | solution.py:62
  (6 other events, 84.5 us)

commit v9 on v7

--- a/solution.py
+++ b/solution.py
@@ -74,14 +74,32 @@
         ).reshape(group_rows, tenants, rank_size)
         return jnp.sum(jnp.where(tenant_masks[:, :, None], wide, jnp.zeros((), jnp.float32)), axis=1)
 
-    sum_steps = [ring]
+    masks_down = [ring]
     step = ring // 2
     while step >= 1:
-        sum_steps.append(step)
+        masks_down.append(step)
         step //= 2
 
-    def sum_step(value, mask):
-        return value + hop(value, [(i, i ^ mask) for i in range(members)])
+    def halve(value, mask):
+        upper = (tensor_at & mask) != 0
+        cut_at = value.shape[0] // 2
+        low_rows, high_rows = value[:cut_at], value[cut_at:]
+        kept = jnp.where(upper, high_rows, low_rows)
+        sent = jnp.where(upper, low_rows, high_rows)
+        return kept + hop(sent, [(i, i ^ mask) for i in range(members)])
+
+    def double(value, mask):
+        upper = (tensor_at & mask) != 0
+        got = hop(value, [(i, i ^ mask) for i in range(members)])
+        return jnp.where(upper, jnp.concatenate([got, value]), jnp.concatenate([value, got]))
+
+    sum_steps = [lambda v, m=m: halve(v, m) for m in masks_down]
+    sum_steps.append(lambda v: v.astype(jnp.bfloat16))
+    sum_steps += [lambda v, m=m: double(v, m) for m in reversed(masks_down)]
+    late_steps = 2
+
+    def sum_step(value, step_fn):
+        return step_fn(value)
 
     own_pieces = [tokens] + [None] * (ring - 1)
     partner_pieces = [None] * ring
@@ -109,7 +127,7 @@
         else:
             low_next = sum_step(low_sum, sum_steps.pop(0))
             if step == ring // 2 + 1:
-                while sum_steps:
+                while len(sum_steps) > late_steps:
                     low_next = sum_step(low_next, sum_steps.pop(0))
             extra = (low_next,)
         moved, extra = lax.optimization_barrier((moved, extra))
@@ -163,7 +181,7 @@
         return ordered.reshape((group_rows,) + own_list[0].shape[1:])
 
     base_projection = to_group_order(base_of["own"], base_of["partner"])
-    low_rank = low_sum.astype(jnp.bfloat16)
+    low_rank = low_sum
     low_wide = jnp.where(
         tenant_masks[:, :, None], low_rank[:, None, :], jnp.zeros((), jnp.bfloat16)
     )

time: 209 us -> 213 us (1.019)
  starting transfers between devices: 60.4 us -> 66.8 us
  waiting for transfers between devices: 103 us -> 97.2 us
  matrix products: 25.3 us -> 27.8 us
    ppermute x21 -> x25, starting transfers between devices: 43.4 us -> 49.8 us  [hop(): return lax.ppermute(value, 'tensor', pairs)]
    ppermute x21 -> x25, waiting for transfers between devices: 86.2 us -> 80.8 us  [hop(): return lax.ppermute(value, 'tensor', pairs)]
    dot_general x6, matrix products: 21.9 us -> 24.6 us  [on_device(): product = jnp.dot(stacked, q_weight, preferred_element_type=jnp.float32)]
  transfers between devices with their start and end apart: 23 -> 27, of which waited for: 12 -> 16; matrix products, arithmetic and copies ran while one was open for 15% -> 20% of each run, Pallas kernels for 0% -> 0%
where the time goes in v9:
time: 213 us
  waiting for transfers between devices  97.2 us (46%)
  starting transfers between devices  66.8 us (31%)
  matrix products  27.8 us (13%)
  local copies, waits for them, and re-layouts  15.9 us (7%)
  other arithmetic  4.4 us (2%)
    ppermute x25, waiting for transfers between devices, hop(): return lax.ppermute(value, 'tensor', pairs)  80.8 us
    ppermute x25, starting transfers between devices, hop(): return lax.ppermute(value, 'tensor', pairs)  49.8 us
    dot_general x6, matrix products, on_device(): product = jnp.dot(stacked, q_weight, preferred_element_type=jnp.float32)  24.6 us
    all_to_all x1, waiting for transfers between devices, on_device(): recv = lax.all_to_all(send, 'dp', 0, 0, tiled=True)  12.7 us
    all_to_all x1, starting transfers between devices, on_device(): local_cols = lax.all_to_all(tokens, 'tensor', 1, 0, tiled=True)  11 us
    unnamed x36, local copies, waits for them, and re-layouts  9.98 us
    all_to_all x1, starting transfers between devices, on_device(): recv = lax.all_to_all(send, 'dp', 0, 0, tiled=True)  5.99 us
  transfers between devices with their start and end apart: 27, of which 16 were waited for; matrix products, arithmetic and copies ran while one was open for 20% of the time, Pallas kernels for 0%

profile of v9, /device:TPU:2, one launch (start us, length us, event | category | flops | bytes accessed | tf_op | source)
XLA Modules:
  0.0 212.5 jit_solution(790844815972649657)
XLA Ops:
  4.8 6.0 %all-to-all-start.1 = ((bf16[16,128,512]{2,1,0:T(8,128)(2,1)}), bf16[16,128,512]{2,1,0:T(8,128)(2,1)S(1)}, u32[]{:S(2)}, u32[]{:S(2)}) async-start(bf16[16,128,512]{2,1,0:T(8,128)(2,1)} %broadcast_select_fusion), calls=%async_computation.1 | async-start | bytes 4194304 | tf_op jit(solution)/shard_map/all_to_all | solution.py:42
  10.8 5.9 %collective-permute-start.1 = (bf16[48,8192]{1,0:T(8,128)(2,1)S(1)}, bf16[48,8192]{1,0:T(8,128)(2,1)}, u32[]{:S(2)}, u32[]{:S(2)}) collective-permute-start(bf16[48,8192]{1,0:T(8,128)(2,1)S(1)} %copy-done.2), channel_id=1, source_target_pairs={{0,7},{1,0},{2,1},{3,2},{4,3},{5,4},{6,5},{7,6},{8,15},{9,8},{10,9... | collective-permute-start | bytes 2359304 | tf_op jit(solution)/shard_map/ppermute | solution.py:62
  16.7 2.9 %collective-permute-start = (bf16[48,8192]{1,0:T(8,128)(2,1)S(1)}, bf16[48,8192]{1,0:T(8,128)(2,1)}, u32[]{:S(2)}, u32[]{:S(2)}) collective-permute-start(bf16[48,8192]{1,0:T(8,128)(2,1)S(1)} %copy-done.2), channel_id=1, source_target_pairs={{0,8},{1,9},{2,10},{3,11},{4,12},{5,13},{6,14},{7,15},{8,0},{9,1},... | collective-permute-start | bytes 2359304 | tf_op jit(solution)/shard_map/ppermute | solution.py:62
  21.1 5.6 %constant_dynamic-update-slice_fusion.1 = (f32[16,48,512]{2,1,0:T(8,128)}, f32[1,48,512]{2,1,0:T(8,128)S(1)}) fusion(bf16[48,8192]{1,0:T(8,128)(2,1)S(1)} %copy-done.2, bf16[8192,512]{1,0:T(8,128)(2,1)} %param.8), kind=kOutput, calls=%fused_computation.102 | convolution fusion | flops 402653184 | bytes 9371648 | tf_op jit(solution)/shard_map/dot_general | solution.py:168
  26.6 12.7 %all-to-all-done.1 = bf16[16,128,512]{2,1,0:T(8,128)(2,1)S(1)} async-done(((bf16[16,128,512]{2,1,0:T(8,128)(2,1)}), bf16[16,128,512]{2,1,0:T(8,128)(2,1)S(1)}, u32[]{:S(2)}, u32[]{:S(2)}) %all-to-all-start.1) | async-done | bytes 2097184 | tf_op jit(solution)/shard_map/all_to_all | solution.py:42
  39.3 11.0 %all-to-all-start = ((bf16[48,16,512]{2,0,1:T(8,128)(2,1)}), bf16[48,16,512]{2,0,1:T(8,128)(2,1)}, u32[]{:S(2)}, u32[]{:S(2)}) async-start(bf16[48,16,512]{2,0,1:T(8,128)(2,1)} %bitcast.133), calls=%async_computation | async-start | bytes 1572864 | tf_op jit(solution)/shard_map/all_to_all | solution.py:69
  50.8 3.4 %collective-permute-done = bf16[48,8192]{1,0:T(8,128)(2,1)} collective-permute-done((bf16[48,8192]{1,0:T(8,128)(2,1)S(1)}, bf16[48,8192]{1,0:T(8,128)(2,1)}, u32[]{:S(2)}, u32[]{:S(2)}) %collective-permute-start) | collective-permute-done | bytes 786464 | tf_op jit(solution)/shard_map/ppermute | solution.py:62
  56.6 4.9 %collective-permute-start.5 = (bf16[48,8192]{1,0:T(8,128)(2,1)}, bf16[48,8192]{1,0:T(8,128)(2,1)}, u32[]{:S(2)}, u32[]{:S(2)}) collective-permute-start(bf16[48,8192]{1,0:T(8,128)(2,1)} %collective-permute-done), channel_id=1, source_target_pairs={{0,7},{1,0},{2,1},{3,2},{4,3},{5,4},{6,5},{7,6},{8,15},{9,8},{10,9... | collective-permute-start | bytes 2359304 | tf_op jit(solution)/shard_map/ppermute | solution.py:62
  63.5 5.5 %fusion.16 = f32[144,512]{1,0:T(8,128)S(1)} fusion(bf16[8192,512]{1,0:T(8,128)(2,1)} %param.8, bf16[48,8192]{1,0:T(8,128)(2,1)} %collective-permute-done, bf16[48,8192]{1,0:T(8,128)(2,1)} %collective-permute-done.2, bf16[48,8192]{1,0:T(8,128)(2,1)} %collective-permute-done.1), kind=kOutput, calls=%fused_computation.19 | convolution fusion | flops 1215037440 | bytes 11042816 | tf_op jit(solution)/shard_map/dot_general | solution.py:168
  71.1 3.7 %all-to-all-done = bf16[48,16,512]{2,0,1:T(8,128)(2,1)} async-done(((bf16[48,16,512]{2,0,1:T(8,128)(2,1)}), bf16[48,16,512]{2,0,1:T(8,128)(2,1)}, u32[]{:S(2)}, u32[]{:S(2)}) %all-to-all-start) | async-done | bytes 786464 | tf_op jit(solution)/shard_map/all_to_all | solution.py:69
  74.7 28.6 %collective-permute-done.3 = bf16[48,8192]{1,0:T(8,128)(2,1)} collective-permute-done((bf16[48,8192]{1,0:T(8,128)(2,1)}, bf16[48,8192]{1,0:T(8,128)(2,1)}, u32[]{:S(2)}, u32[]{:S(2)}) %collective-permute-start.3) | collective-permute-done | bytes 786464 | tf_op jit(solution)/shard_map/ppermute | solution.py:62
  106.6 2.7 %collective-permute-start.9 = (bf16[48,8192]{1,0:T(8,128)(2,1)}, bf16[48,8192]{1,0:T(8,128)(2,1)S(1)}, u32[]{:S(2)}, u32[]{:S(2)}) collective-permute-start(bf16[48,8192]{1,0:T(8,128)(2,1)} %collective-permute-done.5), channel_id=1, source_target_pairs={{0,7},{1,0},{2,1},{3,2},{4,3},{5,4},{6,5},{7,6},{8,15},{9,8},{10,9... | collective-permute-start | bytes 2359304 | tf_op jit(solution)/shard_map/ppermute | solution.py:62
  109.3 6.1 %fusion = f32[192,512]{1,0:T(8,128)S(1)} fusion(bf16[8192,512]{1,0:T(8,128)(2,1)} %param.8, bf16[48,8192]{1,0:T(8,128)(2,1)} %collective-permute-done.6, bf16[48,8192]{1,0:T(8,128)(2,1)} %collective-permute-done.5, bf16[48,8192]{1,0:T(8,128)(2,1)} %collective-permute-done.4, bf16[48,8192]{1,0:T(8,128)(2,1)} %collective-permute-done.3), kind=kOutput, calls=%fused_computation.3 | convolution fusion | flops 1623195648 | bytes 11927552 | tf_op jit(solution)/shard_map/dot_general | solution.py:168
  117.3 3.0 %collective-permute-start.11 = (f32[384,64]{0,1:T(8,128)S(1)}, f32[384,64]{0,1:T(8,128)S(1)}, u32[]{:S(2)}, u32[]{:S(2)}) collective-permute-start(f32[384,64]{0,1:T(8,128)S(1)} %slice_select_fusion), channel_id=1, source_target_pairs={{0,8},{1,9},{2,10},{3,11},{4,12},{5,13},{6,14},{7,15},{8,0},{9,1},... | collective-permute-start | bytes 294920 | tf_op jit(solution)/shard_map/ppermute | solution.py:62
  125.2 2.7 %collective-permute-done.8 = bf16[48,8192]{1,0:T(8,128)(2,1)S(1)} collective-permute-done((bf16[48,8192]{1,0:T(8,128)(2,1)}, bf16[48,8192]{1,0:T(8,128)(2,1)S(1)}, u32[]{:S(2)}, u32[]{:S(2)}) %collective-permute-start.8) | collective-permute-done | bytes 786464 | tf_op jit(solution)/shard_map/ppermute | solution.py:62
  127.9 12.3 %collective-permute-done.9 = bf16[48,8192]{1,0:T(8,128)(2,1)S(1)} collective-permute-done((bf16[48,8192]{1,0:T(8,128)(2,1)}, bf16[48,8192]{1,0:T(8,128)(2,1)S(1)}, u32[]{:S(2)}, u32[]{:S(2)}) %collective-permute-start.9) | collective-permute-done | bytes 786464 | tf_op jit(solution)/shard_map/ppermute | solution.py:62
  144.6 4.5 %fusion.8 = f32[192,512]{1,0:T(8,128)S(1)} fusion(bf16[8192,512]{1,0:T(8,128)(2,1)} %param.8, bf16[48,8192]{1,0:T(8,128)(2,1)S(1)} %collective-permute-done.10, bf16[48,8192]{1,0:T(8,128)(2,1)S(1)} %collective-permute-done.9, bf16[48,8192]{1,0:T(8,128)(2,1)S(1)} %collective-permute-done.8, bf16[48,8192]{1,0:T(8,128)(2,1)S(1)} %collective-permute-done.7), kind=kOutput, calls=%fused_computation.11 | convolution fusion | flops 1623195648 | bytes 11927552 | tf_op jit(solution)/shard_map/dot_general | solution.py:168
  149.2 4.7 %collective-permute-start.16 = (f32[192,64]{0,1:T(8,128)S(1)}, f32[192,64]{0,1:T(8,128)S(1)}, u32[]{:S(2)}, u32[]{:S(2)}) collective-permute-start(f32[192,64]{0,1:T(8,128)S(1)} %slice_select_fusion.1), channel_id=1, source_target_pairs={{0,4},{1,5},{2,6},{3,7},{4,0},{5,1},{6,2},{7,3},{8,12},{9,13},{10,... | collective-permute-start | bytes 147464 | tf_op jit(solution)/shard_map/ppermute | solution.py:62
  153.9 3.2 %collective-permute-start.12 = (bf16[24,8192]{1,0:T(8,128)(2,1)S(1)}, bf16[24,8192]{1,0:T(8,128)(2,1)S(1)}, u32[]{:S(2)}, u32[]{:S(2)}) collective-permute-start(bf16[24,8192]{1,0:T(8,128)(2,1)S(1)} %slice.90), channel_id=1, source_target_pairs={{0,7},{1,0},{2,1},{3,2},{4,3},{5,4},{6,5},{7,6},{8,15},{9,8},{10,9... | collective-permute-start | bytes 1179656 | tf_op jit(solution)/shard_map/ppermute | solution.py:62
  157.8 12.6 %collective-permute-done.16 = f32[192,64]{0,1:T(8,128)S(1)} collective-permute-done((f32[192,64]{0,1:T(8,128)S(1)}, f32[192,64]{0,1:T(8,128)S(1)}, u32[]{:S(2)}, u32[]{:S(2)}) %collective-permute-start.16) | collective-permute-done | bytes 49184 | tf_op jit(solution)/shard_map/ppermute | solution.py:62
  172.9 2.8 %collective-permute-start.18 = (bf16[24,8192]{1,0:T(8,128)(2,1)S(1)}, bf16[24,8192]{1,0:T(8,128)(2,1)S(1)}, u32[]{:S(2)}, u32[]{:S(2)}) collective-permute-start(bf16[24,8192]{1,0:T(8,128)(2,1)S(1)} %slice.103), channel_id=1, source_target_pairs={{0,1},{1,2},{2,3},{3,4},{4,5},{5,6},{6,7},{7,0},{8,9},{9,10},{10,1... | collective-permute-start | bytes 1179656 | tf_op jit(solution)/shard_map/ppermute | solution.py:62
  191.5 3.9 %collective-permute-done.22 = bf16[96,64]{0,1:T(8,128)(2,1)S(1)} collective-permute-done((bf16[96,64]{0,1:T(8,128)(2,1)S(1)}, bf16[96,64]{0,1:T(8,128)(2,1)S(1)}, u32[]{:S(2)}, u32[]{:S(2)}) %collective-permute-start.22) | collective-permute-done | bytes 12320 | tf_op jit(solution)/shard_map/ppermute | solution.py:62
  195.6 4.0 %collective-permute-start.23 = (bf16[192,64]{0,1:T(8,128)(2,1)S(1)}, bf16[192,64]{0,1:T(8,128)(2,1)S(1)}, u32[]{:S(2)}, u32[]{:S(2)}) collective-permute-start(bf16[192,64]{0,1:T(8,128)(2,1)S(1)} %maximum_select_fusion.3), channel_id=1, source_target_pairs={{0,4},{1,5},{2,6},{3,7},{4,0},{5,1},{6,2},{7,3},{8,12},{9,13},{10,... | collective-permute-start | bytes 73736 | tf_op jit(solution)/shard_map/ppermute | solution.py:62
  205.3 3.0 %collective-permute-start.24 = (bf16[384,64]{0,1:T(8,128)(2,1)S(1)}, bf16[384,64]{0,1:T(8,128)(2,1)S(1)}, u32[]{:S(2)}, u32[]{:S(2)}) collective-permute-start(bf16[384,64]{0,1:T(8,128)(2,1)S(1)} %maximum_select_fusion.2), channel_id=1, source_target_pairs={{0,8},{1,9},{2,10},{3,11},{4,12},{5,13},{6,14},{7,15},{8,0},{9,1},... | collective-permute-start | bytes 147464 | tf_op jit(solution)/shard_map/ppermute | solution.py:62
  (118 shorter events, 56.4 us)
Async XLA Ops:
  4.8 34.5 %all-to-all-start.1 = ((bf16[16,128,512]{2,1,0:T(8,128)(2,1)}), bf16[16,128,512]{2,1,0:T(8,128)(2,1)S(1)}, u32[]{:S(2)}, u32[]{:S(2)}) async-start(bf16[16,128,512]{2,1,0:T(8,128)(2,1)} %broadcast_select_fusion), calls=%async_computation.1 | async-start | bytes 4194304 | tf_op jit(solution)/shard_map/all_to_all | solution.py:42
  10.8 40.0 %collective-permute-start.1 = (bf16[48,8192]{1,0:T(8,128)(2,1)S(1)}, bf16[48,8192]{1,0:T(8,128)(2,1)}, u32[]{:S(2)}, u32[]{:S(2)}) collective-permute-start(bf16[48,8192]{1,0:T(8,128)(2,1)S(1)} %copy-done.2), channel_id=1, source_target_pairs={{0,7},{1,0},{2,1},{3,2},{4,3},{5,4},{6,5},{7,6},{8,15},{9,8},{10,9... | collective-permute-start | bytes 2359304 | tf_op jit(solution)/shard_map/ppermute | solution.py:62
  16.7 37.6 %collective-permute-start = (bf16[48,8192]{1,0:T(8,128)(2,1)S(1)}, bf16[48,8192]{1,0:T(8,128)(2,1)}, u32[]{:S(2)}, u32[]{:S(2)}) collective-permute-start(bf16[48,8192]{1,0:T(8,128)(2,1)S(1)} %copy-done.2), channel_id=1, source_target_pairs={{0,8},{1,9},{2,10},{3,11},{4,12},{5,13},{6,14},{7,15},{8,0},{9,1},... | collective-permute-start | bytes 2359304 | tf_op jit(solution)/shard_map/ppermute | solution.py:62
  19.6 34.7 %collective-permute-start.2 = (bf16[48,8192]{1,0:T(8,128)(2,1)S(1)}, bf16[48,8192]{1,0:T(8,128)(2,1)}, u32[]{:S(2)}, u32[]{:S(2)}) collective-permute-start(bf16[48,8192]{1,0:T(8,128)(2,1)S(1)} %copy-done.2), channel_id=1, source_target_pairs={{0,1},{1,2},{2,3},{3,4},{4,5},{5,6},{6,7},{7,0},{8,9},{9,10},{10,1... | collective-permute-start | bytes 2359304 | tf_op jit(solution)/shard_map/ppermute | solution.py:62
  39.3 35.4 %all-to-all-start = ((bf16[48,16,512]{2,0,1:T(8,128)(2,1)}), bf16[48,16,512]{2,0,1:T(8,128)(2,1)}, u32[]{:S(2)}, u32[]{:S(2)}) async-start(bf16[48,16,512]{2,0,1:T(8,128)(2,1)} %bitcast.133), calls=%async_computation | async-start | bytes 1572864 | tf_op jit(solution)/shard_map/all_to_all | solution.py:69
  54.3 50.3 %collective-permute-start.6 = (bf16[48,8192]{1,0:T(8,128)(2,1)}, bf16[48,8192]{1,0:T(8,128)(2,1)}, u32[]{:S(2)}, u32[]{:S(2)}) collective-permute-start(bf16[48,8192]{1,0:T(8,128)(2,1)} %collective-permute-done), channel_id=1, source_target_pairs={{0,1},{1,2},{2,3},{3,4},{4,5},{5,6},{6,7},{7,0},{8,9},{9,10},{10,1... | collective-permute-start | bytes 2359304 | tf_op jit(solution)/shard_map/ppermute | solution.py:62
  56.6 47.9 %collective-permute-start.5 = (bf16[48,8192]{1,0:T(8,128)(2,1)}, bf16[48,8192]{1,0:T(8,128)(2,1)}, u32[]{:S(2)}, u32[]{:S(2)}) collective-permute-start(bf16[48,8192]{1,0:T(8,128)(2,1)} %collective-permute-done), channel_id=1, source_target_pairs={{0,7},{1,0},{2,1},{3,2},{4,3},{5,4},{6,5},{7,6},{8,15},{9,8},{10,9... | collective-permute-start | bytes 2359304 | tf_op jit(solution)/shard_map/ppermute | solution.py:62
  61.5 41.9 %collective-permute-start.3 = (bf16[48,8192]{1,0:T(8,128)(2,1)}, bf16[48,8192]{1,0:T(8,128)(2,1)}, u32[]{:S(2)}, u32[]{:S(2)}) collective-permute-start(bf16[48,8192]{1,0:T(8,128)(2,1)} %collective-permute-done.1), channel_id=1, source_target_pairs={{0,7},{1,0},{2,1},{3,2},{4,3},{5,4},{6,5},{7,6},{8,15},{9,8},{10,9... | collective-permute-start | bytes 2359304 | tf_op jit(solution)/shard_map/ppermute | solution.py:62
  63.5 41.0 %collective-permute-start.4 = (bf16[48,8192]{1,0:T(8,128)(2,1)}, bf16[48,8192]{1,0:T(8,128)(2,1)}, u32[]{:S(2)}, u32[]{:S(2)}) collective-permute-start(bf16[48,8192]{1,0:T(8,128)(2,1)} %collective-permute-done.2), channel_id=1, source_target_pairs={{0,1},{1,2},{2,3},{3,4},{4,5},{5,6},{6,7},{7,0},{8,9},{9,10},{10,1... | collective-permute-start | bytes 2359304 | tf_op jit(solution)/shard_map/ppermute | solution.py:62
  104.6 20.6 %collective-permute-start.7 = (bf16[48,8192]{1,0:T(8,128)(2,1)}, bf16[48,8192]{1,0:T(8,128)(2,1)S(1)}, u32[]{:S(2)}, u32[]{:S(2)}) collective-permute-start(bf16[48,8192]{1,0:T(8,128)(2,1)} %collective-permute-done.3), channel_id=1, source_target_pairs={{0,7},{1,0},{2,1},{3,2},{4,3},{5,4},{6,5},{7,6},{8,15},{9,8},{10,9... | collective-permute-start | bytes 2359304 | tf_op jit(solution)/shard_map/ppermute | solution.py:62
  106.0 21.8 %collective-permute-start.8 = (bf16[48,8192]{1,0:T(8,128)(2,1)}, bf16[48,8192]{1,0:T(8,128)(2,1)S(1)}, u32[]{:S(2)}, u32[]{:S(2)}) collective-permute-start(bf16[48,8192]{1,0:T(8,128)(2,1)} %collective-permute-done.4), channel_id=1, source_target_pairs={{0,1},{1,2},{2,3},{3,4},{4,5},{5,6},{6,7},{7,0},{8,9},{9,10},{10,1... | collective-permute-start | bytes 2359304 | tf_op jit(solution)/shard_map/ppermute | solution.py:62
  106.6 33.6 %collective-permute-start.9 = (bf16[48,8192]{1,0:T(8,128)(2,1)}, bf16[48,8192]{1,0:T(8,128)(2,1)S(1)}, u32[]{:S(2)}, u32[]{:S(2)}) collective-permute-start(bf16[48,8192]{1,0:T(8,128)(2,1)} %collective-permute-done.5), channel_id=1, source_target_pairs={{0,7},{1,0},{2,1},{3,2},{4,3},{5,4},{6,5},{7,6},{8,15},{9,8},{10,9... | collective-permute-start | bytes 2359304 | tf_op jit(solution)/shard_map/ppermute | solution.py:62
  115.4 27.2 %collective-permute-start.10 = (bf16[48,8192]{1,0:T(8,128)(2,1)}, bf16[48,8192]{1,0:T(8,128)(2,1)S(1)}, u32[]{:S(2)}, u32[]{:S(2)}) collective-permute-start(bf16[48,8192]{1,0:T(8,128)(2,1)} %collective-permute-done.6), channel_id=1, source_target_pairs={{0,1},{1,2},{2,3},{3,4},{4,5},{5,6},{6,7},{7,0},{8,9},{9,10},{10,1... | collective-permute-start | bytes 2359304 | tf_op jit(solution)/shard_map/ppermute | solution.py:62
  117.3 6.2 %collective-permute-start.11 = (f32[384,64]{0,1:T(8,128)S(1)}, f32[384,64]{0,1:T(8,128)S(1)}, u32[]{:S(2)}, u32[]{:S(2)}) collective-permute-start(f32[384,64]{0,1:T(8,128)S(1)} %slice_select_fusion), channel_id=1, source_target_pairs={{0,8},{1,9},{2,10},{3,11},{4,12},{5,13},{6,14},{7,15},{8,0},{9,1},... | collective-permute-start | bytes 294920 | tf_op jit(solution)/shard_map/ppermute | solution.py:62
  142.6 30.2 %collective-permute-start.14 = (bf16[48,8192]{1,0:T(8,128)(2,1)S(1)}, bf16[48,8192]{1,0:T(8,128)(2,1)S(1)}, u32[]{:S(2)}, u32[]{:S(2)}) collective-permute-start(bf16[48,8192]{1,0:T(8,128)(2,1)S(1)} %collective-permute-done.9), channel_id=1, source_target_pairs={{0,7},{1,0},{2,1},{3,2},{4,3},{5,4},{6,5},{7,6},{8,15},{9,8},{10,9... | collective-permute-start | bytes 2359304 | tf_op jit(solution)/shard_map/ppermute | solution.py:62
  143.0 29.8 %collective-permute-start.15 = (bf16[48,8192]{1,0:T(8,128)(2,1)S(1)}, bf16[48,8192]{1,0:T(8,128)(2,1)S(1)}, u32[]{:S(2)}, u32[]{:S(2)}) collective-permute-start(bf16[48,8192]{1,0:T(8,128)(2,1)S(1)} %collective-permute-done.10), channel_id=1, source_target_pairs={{0,1},{1,2},{2,3},{3,4},{4,5},{5,6},{6,7},{7,0},{8,9},{9,10},{10,1... | collective-permute-start | bytes 2359304 | tf_op jit(solution)/shard_map/ppermute | solution.py:62
  149.2 21.2 %collective-permute-start.16 = (f32[192,64]{0,1:T(8,128)S(1)}, f32[192,64]{0,1:T(8,128)S(1)}, u32[]{:S(2)}, u32[]{:S(2)}) collective-permute-start(f32[192,64]{0,1:T(8,128)S(1)} %slice_select_fusion.1), channel_id=1, source_target_pairs={{0,4},{1,5},{2,6},{3,7},{4,0},{5,1},{6,2},{7,3},{8,12},{9,13},{10,... | collective-permute-start | bytes 147464 | tf_op jit(solution)/shard_map/ppermute | solution.py:62
  153.9 18.8 %collective-permute-start.13 = (bf16[24,8192]{1,0:T(8,128)(2,1)S(1)}, bf16[24,8192]{1,0:T(8,128)(2,1)S(1)}, u32[]{:S(2)}, u32[]{:S(2)}) collective-permute-start(bf16[24,8192]{1,0:T(8,128)(2,1)S(1)} %slice.91), channel_id=1, source_target_pairs={{0,1},{1,2},{2,3},{3,4},{4,5},{5,6},{6,7},{7,0},{8,9},{9,10},{10,1... | collective-permute-start | bytes 1179656 | tf_op jit(solution)/shard_map/ppermute | solution.py:62
  153.9 18.8 %collective-permute-start.12 = (bf16[24,8192]{1,0:T(8,128)(2,1)S(1)}, bf16[24,8192]{1,0:T(8,128)(2,1)S(1)}, u32[]{:S(2)}, u32[]{:S(2)}) collective-permute-start(bf16[24,8192]{1,0:T(8,128)(2,1)S(1)} %slice.90), channel_id=1, source_target_pairs={{0,7},{1,0},{2,1},{3,2},{4,3},{5,4},{6,5},{7,6},{8,15},{9,8},{10,9... | collective-permute-start | bytes 1179656 | tf_op jit(solution)/shard_map/ppermute | solution.py:62
  172.9 9.3 %collective-permute-start.19 = (f32[96,64]{0,1:T(8,128)S(1)}, f32[96,64]{0,1:T(8,128)S(1)}, u32[]{:S(2)}, u32[]{:S(2)}) collective-permute-start(f32[96,64]{0,1:T(8,128)S(1)} %slice_select_fusion.3), channel_id=1, source_target_pairs={{0,2},{1,3},{2,0},{3,1},{4,6},{5,7},{6,4},{7,5},{8,10},{9,11},{10,... | collective-permute-start | bytes 73736 | tf_op jit(solution)/shard_map/ppermute | solution.py:62
  172.9 22.6 %collective-permute-start.18 = (bf16[24,8192]{1,0:T(8,128)(2,1)S(1)}, bf16[24,8192]{1,0:T(8,128)(2,1)S(1)}, u32[]{:S(2)}, u32[]{:S(2)}) collective-permute-start(bf16[24,8192]{1,0:T(8,128)(2,1)S(1)} %slice.103), channel_id=1, source_target_pairs={{0,1},{1,2},{2,3},{3,4},{4,5},{5,6},{6,7},{7,0},{8,9},{9,10},{10,1... | collective-permute-start | bytes 1179656 | tf_op jit(solution)/shard_map/ppermute | solution.py:62
  175.7 19.9 %collective-permute-start.17 = (bf16[24,8192]{1,0:T(8,128)(2,1)S(1)}, bf16[24,8192]{1,0:T(8,128)(2,1)S(1)}, u32[]{:S(2)}, u32[]{:S(2)}) collective-permute-start(bf16[24,8192]{1,0:T(8,128)(2,1)S(1)} %slice.102), channel_id=1, source_target_pairs={{0,7},{1,0},{2,1},{3,2},{4,3},{5,4},{6,5},{7,6},{8,15},{9,8},{10,9... | collective-permute-start | bytes 1179656 | tf_op jit(solution)/shard_map/ppermute | solution.py:62
  195.6 9.6 %collective-permute-start.23 = (bf16[192,64]{0,1:T(8,128)(2,1)S(1)}, bf16[192,64]{0,1:T(8,128)(2,1)S(1)}, u32[]{:S(2)}, u32[]{:S(2)}) collective-permute-start(bf16[192,64]{0,1:T(8,128)(2,1)S(1)} %maximum_select_fusion.3), channel_id=1, source_target_pairs={{0,4},{1,5},{2,6},{3,7},{4,0},{5,1},{6,2},{7,3},{8,12},{9,13},{10,... | collective-permute-start | bytes 73736 | tf_op jit(solution)/shard_map/ppermute | solution.py:62
  205.3 5.7 %collective-permute-start.24 = (bf16[384,64]{0,1:T(8,128)(2,1)S(1)}, bf16[384,64]{0,1:T(8,128)(2,1)S(1)}, u32[]{:S(2)}, u32[]{:S(2)}) collective-permute-start(bf16[384,64]{0,1:T(8,128)(2,1)S(1)} %maximum_select_fusion.2), channel_id=1, source_target_pairs={{0,8},{1,9},{2,10},{3,11},{4,12},{5,13},{6,14},{7,15},{8,0},{9,1},... | collective-permute-start | bytes 147464 | tf_op jit(solution)/shard_map/ppermute | solution.py:62
  (10 other events, 149.3 us)

commit v10 on v7

--- a/solution.py
+++ b/solution.py
@@ -75,10 +75,10 @@
         return jnp.sum(jnp.where(tenant_masks[:, :, None], wide, jnp.zeros((), jnp.float32)), axis=1)
 
     sum_steps = [ring]
-    step = ring // 2
-    while step >= 1:
+    step = 1
+    while step < ring:
         sum_steps.append(step)
-        step //= 2
+        step *= 2
 
     def sum_step(value, mask):
         return value + hop(value, [(i, i ^ mask) for i in range(members)])
@@ -108,6 +108,8 @@
             extra = (local_cols, panels)
         else:
             low_next = sum_step(low_sum, sum_steps.pop(0))
+            if step == 3:
+                low_next = sum_step(low_next, sum_steps.pop(0))
             if step == ring // 2 + 1:
                 while sum_steps:
                     low_next = sum_step(low_next, sum_steps.pop(0))

time: 209 us -> 212 us (1.014)
  waiting for transfers between devices: 103 us -> 109 us
  starting transfers between devices: 60.4 us -> 56.1 us
    ppermute x21, waiting for transfers between devices: 86.2 us -> 92.7 us  [hop(): return lax.ppermute(value, 'tensor', pairs)]
    ppermute x21, starting transfers between devices: 43.4 us -> 39.2 us  [hop(): return lax.ppermute(value, 'tensor', pairs)]
  transfers between devices with their start and end apart: 23 -> 23, of which waited for: 12 -> 9; matrix products, arithmetic and copies ran while one was open for 15% -> 15% of each run, Pallas kernels for 0% -> 0%
where the time goes in v10:
time: 212 us; the launch traced here: 211 us
  waiting for transfers between devices  109 us (51%)
  starting transfers between devices  56.1 us (26%)
  matrix products  25.3 us (12%)
  local copies, waits for them, and re-layouts  15.9 us (8%)
  other arithmetic  3.81 us (2%)
    ppermute x21, waiting for transfers between devices, hop(): return lax.ppermute(value, 'tensor', pairs)  92.7 us
    ppermute x21, starting transfers between devices, hop(): return lax.ppermute(value, 'tensor', pairs)  39.2 us
    dot_general x6, matrix products, on_device(): product = jnp.dot(stacked, q_weight, preferred_element_type=jnp.float32)  21.9 us
    all_to_all x1, waiting for transfers between devices, on_device(): recv = lax.all_to_all(send, 'dp', 0, 0, tiled=True)  12.7 us
    all_to_all x1, starting transfers between devices, on_device(): local_cols = lax.all_to_all(tokens, 'tensor', 1, 0, tiled=True)  11 us
    unnamed x36, local copies, waits for them, and re-layouts  9.97 us
    all_to_all x1, starting transfers between devices, on_device(): recv = lax.all_to_all(send, 'dp', 0, 0, tiled=True)  5.99 us
  transfers between devices with their start and end apart: 23, of which 9 were waited for; matrix products, arithmetic and copies ran while one was open for 15% of the time, Pallas kernels for 0%

profile of v10, /device:TPU:2, one launch (start us, length us, event | category | flops | bytes accessed | tf_op | source)
XLA Modules:
  0.0 210.6 jit_solution(6304781651202136914)
XLA Ops:
  4.8 6.0 %all-to-all-start.1 = ((bf16[16,128,512]{2,1,0:T(8,128)(2,1)}), bf16[16,128,512]{2,1,0:T(8,128)(2,1)S(1)}, u32[]{:S(2)}, u32[]{:S(2)}) async-start(bf16[16,128,512]{2,1,0:T(8,128)(2,1)} %broadcast_select_fusion), calls=%async_computation.1 | async-start | bytes 4194304 | tf_op jit(solution)/shard_map/all_to_all | solution.py:42
  10.8 5.9 %collective-permute-start.1 = (bf16[48,8192]{1,0:T(8,128)(2,1)S(1)}, bf16[48,8192]{1,0:T(8,128)(2,1)}, u32[]{:S(2)}, u32[]{:S(2)}) collective-permute-start(bf16[48,8192]{1,0:T(8,128)(2,1)S(1)} %copy-done.2), channel_id=1, source_target_pairs={{0,7},{1,0},{2,1},{3,2},{4,3},{5,4},{6,5},{7,6},{8,15},{9,8},{10,9... | collective-permute-start | bytes 2359304 | tf_op jit(solution)/shard_map/ppermute | solution.py:62
  16.7 2.9 %collective-permute-start = (bf16[48,8192]{1,0:T(8,128)(2,1)S(1)}, bf16[48,8192]{1,0:T(8,128)(2,1)}, u32[]{:S(2)}, u32[]{:S(2)}) collective-permute-start(bf16[48,8192]{1,0:T(8,128)(2,1)S(1)} %copy-done.2), channel_id=1, source_target_pairs={{0,8},{1,9},{2,10},{3,11},{4,12},{5,13},{6,14},{7,15},{8,0},{9,1},... | collective-permute-start | bytes 2359304 | tf_op jit(solution)/shard_map/ppermute | solution.py:62
  21.1 5.6 %constant_dynamic-update-slice_fusion.1 = (f32[16,48,512]{2,1,0:T(8,128)}, f32[1,48,512]{2,1,0:T(8,128)S(1)}) fusion(bf16[48,8192]{1,0:T(8,128)(2,1)S(1)} %copy-done.2, bf16[8192,512]{1,0:T(8,128)(2,1)} %param.8), kind=kOutput, calls=%fused_computation.99 | convolution fusion | flops 402653184 | bytes 9371648 | tf_op jit(solution)/shard_map/dot_general | solution.py:152
  26.6 12.7 %all-to-all-done.1 = bf16[16,128,512]{2,1,0:T(8,128)(2,1)S(1)} async-done(((bf16[16,128,512]{2,1,0:T(8,128)(2,1)}), bf16[16,128,512]{2,1,0:T(8,128)(2,1)S(1)}, u32[]{:S(2)}, u32[]{:S(2)}) %all-to-all-start.1) | async-done | bytes 2097184 | tf_op jit(solution)/shard_map/all_to_all | solution.py:42
  39.3 11.0 %all-to-all-start = ((bf16[48,16,512]{2,0,1:T(8,128)(2,1)}), bf16[48,16,512]{2,0,1:T(8,128)(2,1)}, u32[]{:S(2)}, u32[]{:S(2)}) async-start(bf16[48,16,512]{2,0,1:T(8,128)(2,1)} %bitcast.133), calls=%async_computation | async-start | bytes 1572864 | tf_op jit(solution)/shard_map/all_to_all | solution.py:69
  50.9 3.4 %collective-permute-done = bf16[48,8192]{1,0:T(8,128)(2,1)} collective-permute-done((bf16[48,8192]{1,0:T(8,128)(2,1)S(1)}, bf16[48,8192]{1,0:T(8,128)(2,1)}, u32[]{:S(2)}, u32[]{:S(2)}) %collective-permute-start) | collective-permute-done | bytes 786464 | tf_op jit(solution)/shard_map/ppermute | solution.py:62
  54.3 2.4 %collective-permute-start.6 = (bf16[48,8192]{1,0:T(8,128)(2,1)}, bf16[48,8192]{1,0:T(8,128)(2,1)}, u32[]{:S(2)}, u32[]{:S(2)}) collective-permute-start(bf16[48,8192]{1,0:T(8,128)(2,1)} %collective-permute-done), channel_id=1, source_target_pairs={{0,1},{1,2},{2,3},{3,4},{4,5},{5,6},{6,7},{7,0},{8,9},{9,10},{10,1... | collective-permute-start | bytes 2359304 | tf_op jit(solution)/shard_map/ppermute | solution.py:62
  56.6 4.9 %collective-permute-start.5 = (bf16[48,8192]{1,0:T(8,128)(2,1)}, bf16[48,8192]{1,0:T(8,128)(2,1)}, u32[]{:S(2)}, u32[]{:S(2)}) collective-permute-start(bf16[48,8192]{1,0:T(8,128)(2,1)} %collective-permute-done), channel_id=1, source_target_pairs={{0,7},{1,0},{2,1},{3,2},{4,3},{5,4},{6,5},{7,6},{8,15},{9,8},{10,9... | collective-permute-start | bytes 2359304 | tf_op jit(solution)/shard_map/ppermute | solution.py:62
  61.5 2.0 collective-permute-start.3
  63.5 5.5 %fusion.16 = f32[144,512]{1,0:T(8,128)S(1)} fusion(bf16[8192,512]{1,0:T(8,128)(2,1)} %param.8, bf16[48,8192]{1,0:T(8,128)(2,1)} %collective-permute-done, bf16[48,8192]{1,0:T(8,128)(2,1)} %collective-permute-done.2, bf16[48,8192]{1,0:T(8,128)(2,1)} %collective-permute-done.1), kind=kOutput, calls=%fused_computation.19 | convolution fusion | flops 1215037440 | bytes 11042816 | tf_op jit(solution)/shard_map/dot_general | solution.py:152
  71.1 3.6 %all-to-all-done = bf16[48,16,512]{2,0,1:T(8,128)(2,1)} async-done(((bf16[48,16,512]{2,0,1:T(8,128)(2,1)}), bf16[48,16,512]{2,0,1:T(8,128)(2,1)}, u32[]{:S(2)}, u32[]{:S(2)}) %all-to-all-start) | async-done | bytes 786464 | tf_op jit(solution)/shard_map/all_to_all | solution.py:69
  74.7 28.6 %collective-permute-done.3 = bf16[48,8192]{1,0:T(8,128)(2,1)} collective-permute-done((bf16[48,8192]{1,0:T(8,128)(2,1)}, bf16[48,8192]{1,0:T(8,128)(2,1)}, u32[]{:S(2)}, u32[]{:S(2)}) %collective-permute-start.3) | collective-permute-done | bytes 786464 | tf_op jit(solution)/shard_map/ppermute | solution.py:62
  104.6 1.9 select_reduce_fusion
  106.5 3.1 %collective-permute-start.11 = (f32[768,64]{0,1:T(8,128)S(1)}, f32[768,64]{0,1:T(8,128)S(1)}, u32[]{:S(2)}, u32[]{:S(2)}) collective-permute-start(f32[768,64]{0,1:T(8,128)S(1)} %select_reduce_fusion), channel_id=1, source_target_pairs={{0,8},{1,9},{2,10},{3,11},{4,12},{5,13},{6,14},{7,15},{8,0},{9,1},... | collective-permute-start | bytes 589832 | tf_op jit(solution)/shard_map/ppermute | solution.py:62
  111.6 2.7 %collective-permute-start.9 = (bf16[48,8192]{1,0:T(8,128)(2,1)}, bf16[48,8192]{1,0:T(8,128)(2,1)S(1)}, u32[]{:S(2)}, u32[]{:S(2)}) collective-permute-start(bf16[48,8192]{1,0:T(8,128)(2,1)} %collective-permute-done.5), channel_id=1, source_target_pairs={{0,7},{1,0},{2,1},{3,2},{4,3},{5,4},{6,5},{7,6},{8,15},{9,8},{10,9... | collective-permute-start | bytes 2359304 | tf_op jit(solution)/shard_map/ppermute | solution.py:62
  114.3 6.1 %fusion = f32[192,512]{1,0:T(8,128)S(1)} fusion(bf16[8192,512]{1,0:T(8,128)(2,1)} %param.8, bf16[48,8192]{1,0:T(8,128)(2,1)} %collective-permute-done.6, bf16[48,8192]{1,0:T(8,128)(2,1)} %collective-permute-done.5, bf16[48,8192]{1,0:T(8,128)(2,1)} %collective-permute-done.4, bf16[48,8192]{1,0:T(8,128)(2,1)} %collective-permute-done.3), kind=kOutput, calls=%fused_computation.3 | convolution fusion | flops 1623195648 | bytes 11927552 | tf_op jit(solution)/shard_map/dot_general | solution.py:152
  121.2 27.9 %collective-permute-done.12 = f32[768,64]{0,1:T(8,128)S(1)} collective-permute-done((f32[768,64]{0,1:T(8,128)S(1)}, f32[768,64]{0,1:T(8,128)S(1)}, u32[]{:S(2)}, u32[]{:S(2)}) %collective-permute-start.12) | collective-permute-done | bytes 196640 | tf_op jit(solution)/shard_map/ppermute | solution.py:62
  149.3 1.8 collective-permute-start.14
  154.6 1.8 fusion.8
  158.1 27.8 %collective-permute-done.17 = f32[768,64]{0,1:T(8,128)S(1)} collective-permute-done((f32[768,64]{0,1:T(8,128)S(1)}, f32[768,64]{0,1:T(8,128)S(1)}, u32[]{:S(2)}, u32[]{:S(2)}) %collective-permute-start.17) | collective-permute-done | bytes 196640 | tf_op jit(solution)/shard_map/ppermute | solution.py:62
  186.0 3.7 %collective-permute-start.20 = (f32[768,64]{0,1:T(8,128)S(1)}, f32[768,64]{0,1:T(8,128)S(1)}, u32[]{:S(2)}, u32[]{:S(2)}) collective-permute-start(f32[768,64]{0,1:T(8,128)S(1)} %add.88), channel_id=1, source_target_pairs={{0,4},{1,5},{2,6},{3,7},{4,0},{5,1},{6,2},{7,3},{8,12},{9,13},{10,... | collective-permute-start | bytes 589832 | tf_op jit(solution)/shard_map/ppermute | solution.py:62
  189.7 3.2 %collective-permute-start.18 = (bf16[24,8192]{1,0:T(8,128)(2,1)S(1)}, bf16[24,8192]{1,0:T(8,128)(2,1)S(1)}, u32[]{:S(2)}, u32[]{:S(2)}) collective-permute-start(bf16[24,8192]{1,0:T(8,128)(2,1)S(1)} %slice.74), channel_id=1, source_target_pairs={{0,7},{1,0},{2,1},{3,2},{4,3},{5,4},{6,5},{7,6},{8,15},{9,8},{10,9... | collective-permute-start | bytes 1179656 | tf_op jit(solution)/shard_map/ppermute | solution.py:62
  199.9 3.4 %collective-permute-done.19 = bf16[24,8192]{1,0:T(8,128)(2,1)S(1)} collective-permute-done((bf16[24,8192]{1,0:T(8,128)(2,1)S(1)}, bf16[24,8192]{1,0:T(8,128)(2,1)S(1)}, u32[]{:S(2)}, u32[]{:S(2)}) %collective-permute-start.19) | collective-permute-done | bytes 393248 | tf_op jit(solution)/shard_map/ppermute | solution.py:62
  (102 shorter events, 32.4 us)
Async XLA Ops:
  4.8 34.5 %all-to-all-start.1 = ((bf16[16,128,512]{2,1,0:T(8,128)(2,1)}), bf16[16,128,512]{2,1,0:T(8,128)(2,1)S(1)}, u32[]{:S(2)}, u32[]{:S(2)}) async-start(bf16[16,128,512]{2,1,0:T(8,128)(2,1)} %broadcast_select_fusion), calls=%async_computation.1 | async-start | bytes 4194304 | tf_op jit(solution)/shard_map/all_to_all | solution.py:42
  10.8 40.1 %collective-permute-start.1 = (bf16[48,8192]{1,0:T(8,128)(2,1)S(1)}, bf16[48,8192]{1,0:T(8,128)(2,1)}, u32[]{:S(2)}, u32[]{:S(2)}) collective-permute-start(bf16[48,8192]{1,0:T(8,128)(2,1)S(1)} %copy-done.2), channel_id=1, source_target_pairs={{0,7},{1,0},{2,1},{3,2},{4,3},{5,4},{6,5},{7,6},{8,15},{9,8},{10,9... | collective-permute-start | bytes 2359304 | tf_op jit(solution)/shard_map/ppermute | solution.py:62
  16.7 37.6 %collective-permute-start = (bf16[48,8192]{1,0:T(8,128)(2,1)S(1)}, bf16[48,8192]{1,0:T(8,128)(2,1)}, u32[]{:S(2)}, u32[]{:S(2)}) collective-permute-start(bf16[48,8192]{1,0:T(8,128)(2,1)S(1)} %copy-done.2), channel_id=1, source_target_pairs={{0,8},{1,9},{2,10},{3,11},{4,12},{5,13},{6,14},{7,15},{8,0},{9,1},... | collective-permute-start | bytes 2359304 | tf_op jit(solution)/shard_map/ppermute | solution.py:62
  19.6 34.7 %collective-permute-start.2 = (bf16[48,8192]{1,0:T(8,128)(2,1)S(1)}, bf16[48,8192]{1,0:T(8,128)(2,1)}, u32[]{:S(2)}, u32[]{:S(2)}) collective-permute-start(bf16[48,8192]{1,0:T(8,128)(2,1)S(1)} %copy-done.2), channel_id=1, source_target_pairs={{0,1},{1,2},{2,3},{3,4},{4,5},{5,6},{6,7},{7,0},{8,9},{9,10},{10,1... | collective-permute-start | bytes 2359304 | tf_op jit(solution)/shard_map/ppermute | solution.py:62
  39.3 35.4 %all-to-all-start = ((bf16[48,16,512]{2,0,1:T(8,128)(2,1)}), bf16[48,16,512]{2,0,1:T(8,128)(2,1)}, u32[]{:S(2)}, u32[]{:S(2)}) async-start(bf16[48,16,512]{2,0,1:T(8,128)(2,1)} %bitcast.133), calls=%async_computation | async-start | bytes 1572864 | tf_op jit(solution)/shard_map/all_to_all | solution.py:69
  54.3 50.3 %collective-permute-start.6 = (bf16[48,8192]{1,0:T(8,128)(2,1)}, bf16[48,8192]{1,0:T(8,128)(2,1)}, u32[]{:S(2)}, u32[]{:S(2)}) collective-permute-start(bf16[48,8192]{1,0:T(8,128)(2,1)} %collective-permute-done), channel_id=1, source_target_pairs={{0,1},{1,2},{2,3},{3,4},{4,5},{5,6},{6,7},{7,0},{8,9},{9,10},{10,1... | collective-permute-start | bytes 2359304 | tf_op jit(solution)/shard_map/ppermute | solution.py:62
  56.6 47.9 %collective-permute-start.5 = (bf16[48,8192]{1,0:T(8,128)(2,1)}, bf16[48,8192]{1,0:T(8,128)(2,1)}, u32[]{:S(2)}, u32[]{:S(2)}) collective-permute-start(bf16[48,8192]{1,0:T(8,128)(2,1)} %collective-permute-done), channel_id=1, source_target_pairs={{0,7},{1,0},{2,1},{3,2},{4,3},{5,4},{6,5},{7,6},{8,15},{9,8},{10,9... | collective-permute-start | bytes 2359304 | tf_op jit(solution)/shard_map/ppermute | solution.py:62
  61.5 41.9 %collective-permute-start.3 = (bf16[48,8192]{1,0:T(8,128)(2,1)}, bf16[48,8192]{1,0:T(8,128)(2,1)}, u32[]{:S(2)}, u32[]{:S(2)}) collective-permute-start(bf16[48,8192]{1,0:T(8,128)(2,1)} %collective-permute-done.1), channel_id=1, source_target_pairs={{0,7},{1,0},{2,1},{3,2},{4,3},{5,4},{6,5},{7,6},{8,15},{9,8},{10,9... | collective-permute-start | bytes 2359304 | tf_op jit(solution)/shard_map/ppermute | solution.py:62
  63.5 41.0 %collective-permute-start.4 = (bf16[48,8192]{1,0:T(8,128)(2,1)}, bf16[48,8192]{1,0:T(8,128)(2,1)}, u32[]{:S(2)}, u32[]{:S(2)}) collective-permute-start(bf16[48,8192]{1,0:T(8,128)(2,1)} %collective-permute-done.2), channel_id=1, source_target_pairs={{0,1},{1,2},{2,3},{3,4},{4,5},{5,6},{6,7},{7,0},{8,9},{9,10},{10,1... | collective-permute-start | bytes 2359304 | tf_op jit(solution)/shard_map/ppermute | solution.py:62
  104.6 50.0 %slice-start = ((s8[8388608]{0:T(1024)(128)(4,1)}), s8[4194304]{0:T(1024)(128)(4,1)S(1)}, s32[]{:S(2)}) async-start(s8[8388608]{0:T(1024)(128)(4,1)} %bitcast.130), calls=%async_computation.2 | async-start | bytes 8388608
  106.5 13.9 %collective-permute-start.11 = (f32[768,64]{0,1:T(8,128)S(1)}, f32[768,64]{0,1:T(8,128)S(1)}, u32[]{:S(2)}, u32[]{:S(2)}) collective-permute-start(f32[768,64]{0,1:T(8,128)S(1)} %select_reduce_fusion), channel_id=1, source_target_pairs={{0,8},{1,9},{2,10},{3,11},{4,12},{5,13},{6,14},{7,15},{8,0},{9,1},... | collective-permute-start | bytes 589832 | tf_op jit(solution)/shard_map/ppermute | solution.py:62
  109.6 39.6 %collective-permute-start.7 = (bf16[48,8192]{1,0:T(8,128)(2,1)}, bf16[48,8192]{1,0:T(8,128)(2,1)S(1)}, u32[]{:S(2)}, u32[]{:S(2)}) collective-permute-start(bf16[48,8192]{1,0:T(8,128)(2,1)} %collective-permute-done.3), channel_id=1, source_target_pairs={{0,7},{1,0},{2,1},{3,2},{4,3},{5,4},{6,5},{7,6},{8,15},{9,8},{10,9... | collective-permute-start | bytes 2359304 | tf_op jit(solution)/shard_map/ppermute | solution.py:62
  111.0 38.1 %collective-permute-start.8 = (bf16[48,8192]{1,0:T(8,128)(2,1)}, bf16[48,8192]{1,0:T(8,128)(2,1)S(1)}, u32[]{:S(2)}, u32[]{:S(2)}) collective-permute-start(bf16[48,8192]{1,0:T(8,128)(2,1)} %collective-permute-done.4), channel_id=1, source_target_pairs={{0,1},{1,2},{2,3},{3,4},{4,5},{5,6},{6,7},{7,0},{8,9},{9,10},{10,1... | collective-permute-start | bytes 2359304 | tf_op jit(solution)/shard_map/ppermute | solution.py:62
  111.6 37.6 %collective-permute-start.9 = (bf16[48,8192]{1,0:T(8,128)(2,1)}, bf16[48,8192]{1,0:T(8,128)(2,1)S(1)}, u32[]{:S(2)}, u32[]{:S(2)}) collective-permute-start(bf16[48,8192]{1,0:T(8,128)(2,1)} %collective-permute-done.5), channel_id=1, source_target_pairs={{0,7},{1,0},{2,1},{3,2},{4,3},{5,4},{6,5},{7,6},{8,15},{9,8},{10,9... | collective-permute-start | bytes 2359304 | tf_op jit(solution)/shard_map/ppermute | solution.py:62
  114.3 34.9 %collective-permute-start.10 = (bf16[48,8192]{1,0:T(8,128)(2,1)}, bf16[48,8192]{1,0:T(8,128)(2,1)S(1)}, u32[]{:S(2)}, u32[]{:S(2)}) collective-permute-start(bf16[48,8192]{1,0:T(8,128)(2,1)} %collective-permute-done.6), channel_id=1, source_target_pairs={{0,1},{1,2},{2,3},{3,4},{4,5},{5,6},{6,7},{7,0},{8,9},{9,10},{10,1... | collective-permute-start | bytes 2359304 | tf_op jit(solution)/shard_map/ppermute | solution.py:62
  120.4 28.7 %collective-permute-start.12 = (f32[768,64]{0,1:T(8,128)S(1)}, f32[768,64]{0,1:T(8,128)S(1)}, u32[]{:S(2)}, u32[]{:S(2)}) collective-permute-start(f32[768,64]{0,1:T(8,128)S(1)} %add.86), channel_id=1, source_target_pairs={{0,1},{1,0},{2,3},{3,2},{4,5},{5,4},{6,7},{7,6},{8,9},{9,8},{10,11... | collective-permute-start | bytes 589832 | tf_op jit(solution)/shard_map/ppermute | solution.py:62
  149.3 36.7 %collective-permute-start.14 = (bf16[24,8192]{1,0:T(8,128)(2,1)S(1)}, bf16[24,8192]{1,0:T(8,128)(2,1)S(1)}, u32[]{:S(2)}, u32[]{:S(2)}) collective-permute-start(bf16[24,8192]{1,0:T(8,128)(2,1)S(1)} %slice.65), channel_id=1, source_target_pairs={{0,1},{1,2},{2,3},{3,4},{4,5},{5,6},{6,7},{7,0},{8,9},{9,10},{10,1... | collective-permute-start | bytes 1179656 | tf_op jit(solution)/shard_map/ppermute | solution.py:62
  151.1 34.8 %collective-permute-start.13 = (bf16[24,8192]{1,0:T(8,128)(2,1)S(1)}, bf16[24,8192]{1,0:T(8,128)(2,1)S(1)}, u32[]{:S(2)}, u32[]{:S(2)}) collective-permute-start(bf16[24,8192]{1,0:T(8,128)(2,1)S(1)} %slice.64), channel_id=1, source_target_pairs={{0,7},{1,0},{2,1},{3,2},{4,3},{5,4},{6,5},{7,6},{8,15},{9,8},{10,9... | collective-permute-start | bytes 1179656 | tf_op jit(solution)/shard_map/ppermute | solution.py:62
  152.6 33.4 %collective-permute-start.15 = (bf16[48,8192]{1,0:T(8,128)(2,1)S(1)}, bf16[48,8192]{1,0:T(8,128)(2,1)S(1)}, u32[]{:S(2)}, u32[]{:S(2)}) collective-permute-start(bf16[48,8192]{1,0:T(8,128)(2,1)S(1)} %collective-permute-done.9), channel_id=1, source_target_pairs={{0,7},{1,0},{2,1},{3,2},{4,3},{5,4},{6,5},{7,6},{8,15},{9,8},{10,9... | collective-permute-start | bytes 2359304 | tf_op jit(solution)/shard_map/ppermute | solution.py:62
  154.1 31.8 %collective-permute-start.16 = (bf16[48,8192]{1,0:T(8,128)(2,1)S(1)}, bf16[48,8192]{1,0:T(8,128)(2,1)S(1)}, u32[]{:S(2)}, u32[]{:S(2)}) collective-permute-start(bf16[48,8192]{1,0:T(8,128)(2,1)S(1)} %collective-permute-done.10), channel_id=1, source_target_pairs={{0,1},{1,2},{2,3},{3,4},{4,5},{5,6},{6,7},{7,0},{8,9},{9,10},{10,1... | collective-permute-start | bytes 2359304 | tf_op jit(solution)/shard_map/ppermute | solution.py:62
  156.4 29.5 %collective-permute-start.17 = (f32[768,64]{0,1:T(8,128)S(1)}, f32[768,64]{0,1:T(8,128)S(1)}, u32[]{:S(2)}, u32[]{:S(2)}) collective-permute-start(f32[768,64]{0,1:T(8,128)S(1)} %add.87), channel_id=1, source_target_pairs={{0,2},{1,3},{2,0},{3,1},{4,6},{5,7},{6,4},{7,5},{8,10},{9,11},{10,... | collective-permute-start | bytes 589832 | tf_op jit(solution)/shard_map/ppermute | solution.py:62
  186.0 13.9 %collective-permute-start.20 = (f32[768,64]{0,1:T(8,128)S(1)}, f32[768,64]{0,1:T(8,128)S(1)}, u32[]{:S(2)}, u32[]{:S(2)}) collective-permute-start(f32[768,64]{0,1:T(8,128)S(1)} %add.88), channel_id=1, source_target_pairs={{0,4},{1,5},{2,6},{3,7},{4,0},{5,1},{6,2},{7,3},{8,12},{9,13},{10,... | collective-permute-start | bytes 589832 | tf_op jit(solution)/shard_map/ppermute | solution.py:62
  189.7 13.6 %collective-permute-start.19 = (bf16[24,8192]{1,0:T(8,128)(2,1)S(1)}, bf16[24,8192]{1,0:T(8,128)(2,1)S(1)}, u32[]{:S(2)}, u32[]{:S(2)}) collective-permute-start(bf16[24,8192]{1,0:T(8,128)(2,1)S(1)} %slice.75), channel_id=1, source_target_pairs={{0,1},{1,2},{2,3},{3,4},{4,5},{5,6},{6,7},{7,0},{8,9},{9,10},{10,1... | collective-permute-start | bytes 1179656 | tf_op jit(solution)/shard_map/ppermute | solution.py:62
  189.7 13.6 %collective-permute-start.18 = (bf16[24,8192]{1,0:T(8,128)(2,1)S(1)}, bf16[24,8192]{1,0:T(8,128)(2,1)S(1)}, u32[]{:S(2)}, u32[]{:S(2)}) collective-permute-start(bf16[24,8192]{1,0:T(8,128)(2,1)S(1)} %slice.74), channel_id=1, source_target_pairs={{0,7},{1,0},{2,1},{3,2},{4,3},{5,4},{6,5},{7,6},{8,15},{9,8},{10,9... | collective-permute-start | bytes 1179656 | tf_op jit(solution)/shard_map/ppermute | solution.py:62
  (6 other events, 77.7 us)

commit v11 on v7

--- a/solution.py
+++ b/solution.py
@@ -80,8 +80,15 @@
         sum_steps.append(step)
         step //= 2
 
+    back_two = [(i, (i // ring) * ring + (i % ring - 2) % ring) for i in range(members)]
+
     def sum_step(value, mask):
-        return value + hop(value, [(i, i ^ mask) for i in range(members)])
+        if mask != ring // 2:
+            return value + hop(value, [(i, i ^ mask) for i in range(members)])
+        split = value.shape[0] // 2
+        straight = hop(value[:split], [(i, i ^ mask) for i in range(members)])
+        around = hop(hop(value[split:], back_two), back_two)
+        return value + jnp.concatenate([straight, around], axis=0)
 
     own_pieces = [tokens] + [None] * (ring - 1)
     partner_pieces = [None] * ring

time: 209 us -> 217 us (1.038)
  waiting for transfers between devices: 103 us -> 110 us
    ppermute x21 -> x23, waiting for transfers between devices: 86.2 us -> 93.7 us  [hop(): return lax.ppermute(value, 'tensor', pairs)]
    ppermute x21 -> x23, starting transfers between devices: 43.4 us -> 44 us  [hop(): return lax.ppermute(value, 'tensor', pairs)]
  transfers between devices with their start and end apart: 23 -> 25, of which waited for: 12 -> 13; matrix products, arithmetic and copies ran while one was open for 15% -> 14% of each run, Pallas kernels for 0% -> 0%
where the time goes in v11:
time: 217 us; the launch traced here: 216 us
  waiting for transfers between devices  110 us (51%)
  starting transfers between devices  60.9 us (28%)
  matrix products  25.3 us (12%)
  local copies, waits for them, and re-layouts  15.9 us (7%)
  other arithmetic  3.7 us (2%)
    ppermute x23, waiting for transfers between devices, hop(): return lax.ppermute(value, 'tensor', pairs)  93.7 us
    ppermute x23, starting transfers between devices, hop(): return lax.ppermute(value, 'tensor', pairs)  44 us
    dot_general x6, matrix products, on_device(): product = jnp.dot(stacked, q_weight, preferred_element_type=jnp.float32)  21.9 us
    all_to_all x1, waiting for transfers between devices, on_device(): recv = lax.all_to_all(send, 'dp', 0, 0, tiled=True)  12.7 us
    all_to_all x1, starting transfers between devices, on_device(): local_cols = lax.all_to_all(tokens, 'tensor', 1, 0, tiled=True)  11 us
    unnamed x36, local copies, waits for them, and re-layouts  9.94 us
    all_to_all x1, starting transfers between devices, on_device(): recv = lax.all_to_all(send, 'dp', 0, 0, tiled=True)  5.99 us
  transfers between devices with their start and end apart: 25, of which 13 were waited for; matrix products, arithmetic and copies ran while one was open for 14% of the time, Pallas kernels for 0%

profile of v11, /device:TPU:2, one launch (start us, length us, event | category | flops | bytes accessed | tf_op | source)
XLA Modules:
  0.0 216.2 jit_solution(14178451706293807024)
XLA Ops:
  4.8 6.0 %all-to-all-start.1 = ((bf16[16,128,512]{2,1,0:T(8,128)(2,1)}), bf16[16,128,512]{2,1,0:T(8,128)(2,1)S(1)}, u32[]{:S(2)}, u32[]{:S(2)}) async-start(bf16[16,128,512]{2,1,0:T(8,128)(2,1)} %broadcast_select_fusion), calls=%async_computation.1 | async-start | bytes 4194304 | tf_op jit(solution)/shard_map/all_to_all | solution.py:42
  10.8 5.9 %collective-permute-start.1 = (bf16[48,8192]{1,0:T(8,128)(2,1)S(1)}, bf16[48,8192]{1,0:T(8,128)(2,1)}, u32[]{:S(2)}, u32[]{:S(2)}) collective-permute-start(bf16[48,8192]{1,0:T(8,128)(2,1)S(1)} %copy-done.2), channel_id=1, source_target_pairs={{0,7},{1,0},{2,1},{3,2},{4,3},{5,4},{6,5},{7,6},{8,15},{9,8},{10,9... | collective-permute-start | bytes 2359304 | tf_op jit(solution)/shard_map/ppermute | solution.py:62
  16.7 2.9 %collective-permute-start = (bf16[48,8192]{1,0:T(8,128)(2,1)S(1)}, bf16[48,8192]{1,0:T(8,128)(2,1)}, u32[]{:S(2)}, u32[]{:S(2)}) collective-permute-start(bf16[48,8192]{1,0:T(8,128)(2,1)S(1)} %copy-done.2), channel_id=1, source_target_pairs={{0,8},{1,9},{2,10},{3,11},{4,12},{5,13},{6,14},{7,15},{8,0},{9,1},... | collective-permute-start | bytes 2359304 | tf_op jit(solution)/shard_map/ppermute | solution.py:62
  21.1 5.6 %constant_dynamic-update-slice_fusion.1 = (f32[16,48,512]{2,1,0:T(8,128)}, f32[1,48,512]{2,1,0:T(8,128)S(1)}) fusion(bf16[48,8192]{1,0:T(8,128)(2,1)S(1)} %copy-done.2, bf16[8192,512]{1,0:T(8,128)(2,1)} %param.8), kind=kOutput, calls=%fused_computation.100 | convolution fusion | flops 402653184 | bytes 9371648 | tf_op jit(solution)/shard_map/dot_general | solution.py:157
  26.6 12.7 %all-to-all-done.1 = bf16[16,128,512]{2,1,0:T(8,128)(2,1)S(1)} async-done(((bf16[16,128,512]{2,1,0:T(8,128)(2,1)}), bf16[16,128,512]{2,1,0:T(8,128)(2,1)S(1)}, u32[]{:S(2)}, u32[]{:S(2)}) %all-to-all-start.1) | async-done | bytes 2097184 | tf_op jit(solution)/shard_map/all_to_all | solution.py:42
  39.3 11.0 %all-to-all-start = ((bf16[48,16,512]{2,0,1:T(8,128)(2,1)}), bf16[48,16,512]{2,0,1:T(8,128)(2,1)}, u32[]{:S(2)}, u32[]{:S(2)}) async-start(bf16[48,16,512]{2,0,1:T(8,128)(2,1)} %bitcast.133), calls=%async_computation | async-start | bytes 1572864 | tf_op jit(solution)/shard_map/all_to_all | solution.py:69
  50.8 3.4 %collective-permute-done = bf16[48,8192]{1,0:T(8,128)(2,1)} collective-permute-done((bf16[48,8192]{1,0:T(8,128)(2,1)S(1)}, bf16[48,8192]{1,0:T(8,128)(2,1)}, u32[]{:S(2)}, u32[]{:S(2)}) %collective-permute-start) | collective-permute-done | bytes 786464 | tf_op jit(solution)/shard_map/ppermute | solution.py:62
  56.6 4.9 %collective-permute-start.5 = (bf16[48,8192]{1,0:T(8,128)(2,1)}, bf16[48,8192]{1,0:T(8,128)(2,1)}, u32[]{:S(2)}, u32[]{:S(2)}) collective-permute-start(bf16[48,8192]{1,0:T(8,128)(2,1)} %collective-permute-done), channel_id=1, source_target_pairs={{0,7},{1,0},{2,1},{3,2},{4,3},{5,4},{6,5},{7,6},{8,15},{9,8},{10,9... | collective-permute-start | bytes 2359304 | tf_op jit(solution)/shard_map/ppermute | solution.py:62
  63.5 5.5 %fusion.16 = f32[144,512]{1,0:T(8,128)S(1)} fusion(bf16[8192,512]{1,0:T(8,128)(2,1)} %param.8, bf16[48,8192]{1,0:T(8,128)(2,1)} %collective-permute-done, bf16[48,8192]{1,0:T(8,128)(2,1)} %collective-permute-done.2, bf16[48,8192]{1,0:T(8,128)(2,1)} %collective-permute-done.1), kind=kOutput, calls=%fused_computation.19 | convolution fusion | flops 1215037440 | bytes 11042816 | tf_op jit(solution)/shard_map/dot_general | solution.py:157
  71.0 3.7 %all-to-all-done = bf16[48,16,512]{2,0,1:T(8,128)(2,1)} async-done(((bf16[48,16,512]{2,0,1:T(8,128)(2,1)}), bf16[48,16,512]{2,0,1:T(8,128)(2,1)}, u32[]{:S(2)}, u32[]{:S(2)}) %all-to-all-start) | async-done | bytes 786464 | tf_op jit(solution)/shard_map/all_to_all | solution.py:69
  74.7 28.6 %collective-permute-done.3 = bf16[48,8192]{1,0:T(8,128)(2,1)} collective-permute-done((bf16[48,8192]{1,0:T(8,128)(2,1)}, bf16[48,8192]{1,0:T(8,128)(2,1)}, u32[]{:S(2)}, u32[]{:S(2)}) %collective-permute-start.3) | collective-permute-done | bytes 786464 | tf_op jit(solution)/shard_map/ppermute | solution.py:62
  106.5 3.1 %collective-permute-start.11 = (f32[768,64]{0,1:T(8,128)S(1)}, f32[768,64]{0,1:T(8,128)S(1)}, u32[]{:S(2)}, u32[]{:S(2)}) collective-permute-start(f32[768,64]{0,1:T(8,128)S(1)} %select_reduce_fusion), channel_id=1, source_target_pairs={{0,8},{1,9},{2,10},{3,11},{4,12},{5,13},{6,14},{7,15},{8,0},{9,1},... | collective-permute-start | bytes 589832 | tf_op jit(solution)/shard_map/ppermute | solution.py:62
  111.6 2.7 %collective-permute-start.9 = (bf16[48,8192]{1,0:T(8,128)(2,1)}, bf16[48,8192]{1,0:T(8,128)(2,1)S(1)}, u32[]{:S(2)}, u32[]{:S(2)}) collective-permute-start(bf16[48,8192]{1,0:T(8,128)(2,1)} %collective-permute-done.5), channel_id=1, source_target_pairs={{0,7},{1,0},{2,1},{3,2},{4,3},{5,4},{6,5},{7,6},{8,15},{9,8},{10,9... | collective-permute-start | bytes 2359304 | tf_op jit(solution)/shard_map/ppermute | solution.py:62
  114.3 6.1 %fusion = f32[192,512]{1,0:T(8,128)S(1)} fusion(bf16[8192,512]{1,0:T(8,128)(2,1)} %param.8, bf16[48,8192]{1,0:T(8,128)(2,1)} %collective-permute-done.6, bf16[48,8192]{1,0:T(8,128)(2,1)} %collective-permute-done.5, bf16[48,8192]{1,0:T(8,128)(2,1)} %collective-permute-done.4, bf16[48,8192]{1,0:T(8,128)(2,1)} %collective-permute-done.3), kind=kOutput, calls=%fused_computation.3 | convolution fusion | flops 1623195648 | bytes 11927552 | tf_op jit(solution)/shard_map/dot_general | solution.py:157
  121.1 9.1 %collective-permute-done.7 = bf16[48,8192]{1,0:T(8,128)(2,1)S(1)} collective-permute-done((bf16[48,8192]{1,0:T(8,128)(2,1)}, bf16[48,8192]{1,0:T(8,128)(2,1)S(1)}, u32[]{:S(2)}, u32[]{:S(2)}) %collective-permute-start.7) | collective-permute-done | bytes 786464 | tf_op jit(solution)/shard_map/ppermute | solution.py:62
  130.2 2.7 %collective-permute-done.8 = bf16[48,8192]{1,0:T(8,128)(2,1)S(1)} collective-permute-done((bf16[48,8192]{1,0:T(8,128)(2,1)}, bf16[48,8192]{1,0:T(8,128)(2,1)S(1)}, u32[]{:S(2)}, u32[]{:S(2)}) %collective-permute-start.8) | collective-permute-done | bytes 786464 | tf_op jit(solution)/shard_map/ppermute | solution.py:62
  132.8 12.0 %collective-permute-done.9 = bf16[48,8192]{1,0:T(8,128)(2,1)S(1)} collective-permute-done((bf16[48,8192]{1,0:T(8,128)(2,1)}, bf16[48,8192]{1,0:T(8,128)(2,1)S(1)}, u32[]{:S(2)}, u32[]{:S(2)}) %collective-permute-start.9) | collective-permute-done | bytes 786464 | tf_op jit(solution)/shard_map/ppermute | solution.py:62
  144.9 2.4 %collective-permute-done.10 = bf16[48,8192]{1,0:T(8,128)(2,1)S(1)} collective-permute-done((bf16[48,8192]{1,0:T(8,128)(2,1)}, bf16[48,8192]{1,0:T(8,128)(2,1)S(1)}, u32[]{:S(2)}, u32[]{:S(2)}) %collective-permute-start.10) | collective-permute-done | bytes 786464 | tf_op jit(solution)/shard_map/ppermute | solution.py:62
  147.3 4.6 %collective-permute-start.16 = (f32[384,64]{0,1:T(8,128)S(1)}, f32[384,64]{0,1:T(8,128)S(1)}, u32[]{:S(2)}, u32[]{:S(2)}) collective-permute-start(f32[384,64]{0,1:T(8,128)S(1)} %get-tuple-element.63), channel_id=1, source_target_pairs={{0,4},{1,5},{2,6},{3,7},{4,0},{5,1},{6,2},{7,3},{8,12},{9,13},{10,... | collective-permute-start | bytes 294920 | tf_op jit(solution)/shard_map/ppermute | solution.py:62
  159.5 2.5 %collective-permute-start.18 = (f32[384,64]{0,1:T(8,128)S(1)}, f32[384,64]{0,1:T(8,128)S(1)}, u32[]{:S(2)}, u32[]{:S(2)}) collective-permute-start(f32[384,64]{0,1:T(8,128)S(1)} %collective-permute-done.17), channel_id=1, source_target_pairs={{0,6},{1,7},{2,0},{3,1},{4,2},{5,3},{6,4},{7,5},{8,14},{9,15},{10,... | collective-permute-start | bytes 294920 | tf_op jit(solution)/shard_map/ppermute | solution.py:62
  162.6 25.0 %collective-permute-done.18 = f32[384,64]{0,1:T(8,128)S(1)} collective-permute-done((f32[384,64]{0,1:T(8,128)S(1)}, f32[384,64]{0,1:T(8,128)S(1)}, u32[]{:S(2)}, u32[]{:S(2)}) %collective-permute-start.18) | collective-permute-done | bytes 98336 | tf_op jit(solution)/shard_map/ppermute | solution.py:62
  187.7 2.8 %collective-permute-start.21 = (f32[768,64]{0,1:T(8,128)S(1)}, f32[768,64]{0,1:T(8,128)S(1)}, u32[]{:S(2)}, u32[]{:S(2)}) collective-permute-start(f32[768,64]{0,1:T(8,128)S(1)} %maximum_add_fusion), channel_id=1, source_target_pairs={{0,2},{1,3},{2,0},{3,1},{4,6},{5,7},{6,4},{7,5},{8,10},{9,11},{10,... | collective-permute-start | bytes 589832 | tf_op jit(solution)/shard_map/ppermute | solution.py:62
  190.5 3.2 %collective-permute-start.19 = (bf16[24,8192]{1,0:T(8,128)(2,1)S(1)}, bf16[24,8192]{1,0:T(8,128)(2,1)S(1)}, u32[]{:S(2)}, u32[]{:S(2)}) collective-permute-start(bf16[24,8192]{1,0:T(8,128)(2,1)S(1)} %slice.82), channel_id=1, source_target_pairs={{0,7},{1,0},{2,1},{3,2},{4,3},{5,4},{6,5},{7,6},{8,15},{9,8},{10,9... | collective-permute-start | bytes 1179656 | tf_op jit(solution)/shard_map/ppermute | solution.py:62
  200.5 8.4 %collective-permute-done.22 = f32[768,64]{0,1:T(8,128)S(1)} collective-permute-done((f32[768,64]{0,1:T(8,128)S(1)}, f32[768,64]{0,1:T(8,128)S(1)}, u32[]{:S(2)}, u32[]{:S(2)}) %collective-permute-start.22) | collective-permute-done | bytes 196640 | tf_op jit(solution)/shard_map/ppermute | solution.py:62
  (107 shorter events, 41.1 us)
Async XLA Ops:
  4.8 34.5 %all-to-all-start.1 = ((bf16[16,128,512]{2,1,0:T(8,128)(2,1)}), bf16[16,128,512]{2,1,0:T(8,128)(2,1)S(1)}, u32[]{:S(2)}, u32[]{:S(2)}) async-start(bf16[16,128,512]{2,1,0:T(8,128)(2,1)} %broadcast_select_fusion), calls=%async_computation.1 | async-start | bytes 4194304 | tf_op jit(solution)/shard_map/all_to_all | solution.py:42
  10.8 40.0 %collective-permute-start.1 = (bf16[48,8192]{1,0:T(8,128)(2,1)S(1)}, bf16[48,8192]{1,0:T(8,128)(2,1)}, u32[]{:S(2)}, u32[]{:S(2)}) collective-permute-start(bf16[48,8192]{1,0:T(8,128)(2,1)S(1)} %copy-done.2), channel_id=1, source_target_pairs={{0,7},{1,0},{2,1},{3,2},{4,3},{5,4},{6,5},{7,6},{8,15},{9,8},{10,9... | collective-permute-start | bytes 2359304 | tf_op jit(solution)/shard_map/ppermute | solution.py:62
  16.7 37.6 %collective-permute-start = (bf16[48,8192]{1,0:T(8,128)(2,1)S(1)}, bf16[48,8192]{1,0:T(8,128)(2,1)}, u32[]{:S(2)}, u32[]{:S(2)}) collective-permute-start(bf16[48,8192]{1,0:T(8,128)(2,1)S(1)} %copy-done.2), channel_id=1, source_target_pairs={{0,8},{1,9},{2,10},{3,11},{4,12},{5,13},{6,14},{7,15},{8,0},{9,1},... | collective-permute-start | bytes 2359304 | tf_op jit(solution)/shard_map/ppermute | solution.py:62
  19.6 34.7 %collective-permute-start.2 = (bf16[48,8192]{1,0:T(8,128)(2,1)S(1)}, bf16[48,8192]{1,0:T(8,128)(2,1)}, u32[]{:S(2)}, u32[]{:S(2)}) collective-permute-start(bf16[48,8192]{1,0:T(8,128)(2,1)S(1)} %copy-done.2), channel_id=1, source_target_pairs={{0,1},{1,2},{2,3},{3,4},{4,5},{5,6},{6,7},{7,0},{8,9},{9,10},{10,1... | collective-permute-start | bytes 2359304 | tf_op jit(solution)/shard_map/ppermute | solution.py:62
  39.3 35.4 %all-to-all-start = ((bf16[48,16,512]{2,0,1:T(8,128)(2,1)}), bf16[48,16,512]{2,0,1:T(8,128)(2,1)}, u32[]{:S(2)}, u32[]{:S(2)}) async-start(bf16[48,16,512]{2,0,1:T(8,128)(2,1)} %bitcast.133), calls=%async_computation | async-start | bytes 1572864 | tf_op jit(solution)/shard_map/all_to_all | solution.py:69
  54.3 50.3 %collective-permute-start.6 = (bf16[48,8192]{1,0:T(8,128)(2,1)}, bf16[48,8192]{1,0:T(8,128)(2,1)}, u32[]{:S(2)}, u32[]{:S(2)}) collective-permute-start(bf16[48,8192]{1,0:T(8,128)(2,1)} %collective-permute-done), channel_id=1, source_target_pairs={{0,1},{1,2},{2,3},{3,4},{4,5},{5,6},{6,7},{7,0},{8,9},{9,10},{10,1... | collective-permute-start | bytes 2359304 | tf_op jit(solution)/shard_map/ppermute | solution.py:62
  56.6 47.9 %collective-permute-start.5 = (bf16[48,8192]{1,0:T(8,128)(2,1)}, bf16[48,8192]{1,0:T(8,128)(2,1)}, u32[]{:S(2)}, u32[]{:S(2)}) collective-permute-start(bf16[48,8192]{1,0:T(8,128)(2,1)} %collective-permute-done), channel_id=1, source_target_pairs={{0,7},{1,0},{2,1},{3,2},{4,3},{5,4},{6,5},{7,6},{8,15},{9,8},{10,9... | collective-permute-start | bytes 2359304 | tf_op jit(solution)/shard_map/ppermute | solution.py:62
  61.5 41.9 %collective-permute-start.3 = (bf16[48,8192]{1,0:T(8,128)(2,1)}, bf16[48,8192]{1,0:T(8,128)(2,1)}, u32[]{:S(2)}, u32[]{:S(2)}) collective-permute-start(bf16[48,8192]{1,0:T(8,128)(2,1)} %collective-permute-done.1), channel_id=1, source_target_pairs={{0,7},{1,0},{2,1},{3,2},{4,3},{5,4},{6,5},{7,6},{8,15},{9,8},{10,9... | collective-permute-start | bytes 2359304 | tf_op jit(solution)/shard_map/ppermute | solution.py:62
  63.5 41.0 %collective-permute-start.4 = (bf16[48,8192]{1,0:T(8,128)(2,1)}, bf16[48,8192]{1,0:T(8,128)(2,1)}, u32[]{:S(2)}, u32[]{:S(2)}) collective-permute-start(bf16[48,8192]{1,0:T(8,128)(2,1)} %collective-permute-done.2), channel_id=1, source_target_pairs={{0,1},{1,2},{2,3},{3,4},{4,5},{5,6},{6,7},{7,0},{8,9},{9,10},{10,1... | collective-permute-start | bytes 2359304 | tf_op jit(solution)/shard_map/ppermute | solution.py:62
  106.5 14.5 %collective-permute-start.11 = (f32[768,64]{0,1:T(8,128)S(1)}, f32[768,64]{0,1:T(8,128)S(1)}, u32[]{:S(2)}, u32[]{:S(2)}) collective-permute-start(f32[768,64]{0,1:T(8,128)S(1)} %select_reduce_fusion), channel_id=1, source_target_pairs={{0,8},{1,9},{2,10},{3,11},{4,12},{5,13},{6,14},{7,15},{8,0},{9,1},... | collective-permute-start | bytes 589832 | tf_op jit(solution)/shard_map/ppermute | solution.py:62
  109.5 20.6 %collective-permute-start.7 = (bf16[48,8192]{1,0:T(8,128)(2,1)}, bf16[48,8192]{1,0:T(8,128)(2,1)S(1)}, u32[]{:S(2)}, u32[]{:S(2)}) collective-permute-start(bf16[48,8192]{1,0:T(8,128)(2,1)} %collective-permute-done.3), channel_id=1, source_target_pairs={{0,7},{1,0},{2,1},{3,2},{4,3},{5,4},{6,5},{7,6},{8,15},{9,8},{10,9... | collective-permute-start | bytes 2359304 | tf_op jit(solution)/shard_map/ppermute | solution.py:62
  111.0 21.8 %collective-permute-start.8 = (bf16[48,8192]{1,0:T(8,128)(2,1)}, bf16[48,8192]{1,0:T(8,128)(2,1)S(1)}, u32[]{:S(2)}, u32[]{:S(2)}) collective-permute-start(bf16[48,8192]{1,0:T(8,128)(2,1)} %collective-permute-done.4), channel_id=1, source_target_pairs={{0,1},{1,2},{2,3},{3,4},{4,5},{5,6},{6,7},{7,0},{8,9},{9,10},{10,1... | collective-permute-start | bytes 2359304 | tf_op jit(solution)/shard_map/ppermute | solution.py:62
  111.6 33.3 %collective-permute-start.9 = (bf16[48,8192]{1,0:T(8,128)(2,1)}, bf16[48,8192]{1,0:T(8,128)(2,1)S(1)}, u32[]{:S(2)}, u32[]{:S(2)}) collective-permute-start(bf16[48,8192]{1,0:T(8,128)(2,1)} %collective-permute-done.5), channel_id=1, source_target_pairs={{0,7},{1,0},{2,1},{3,2},{4,3},{5,4},{6,5},{7,6},{8,15},{9,8},{10,9... | collective-permute-start | bytes 2359304 | tf_op jit(solution)/shard_map/ppermute | solution.py:62
  114.2 33.0 %collective-permute-start.10 = (bf16[48,8192]{1,0:T(8,128)(2,1)}, bf16[48,8192]{1,0:T(8,128)(2,1)S(1)}, u32[]{:S(2)}, u32[]{:S(2)}) collective-permute-start(bf16[48,8192]{1,0:T(8,128)(2,1)} %collective-permute-done.6), channel_id=1, source_target_pairs={{0,1},{1,2},{2,3},{3,4},{4,5},{5,6},{6,7},{7,0},{8,9},{9,10},{10,1... | collective-permute-start | bytes 2359304 | tf_op jit(solution)/shard_map/ppermute | solution.py:62
  147.3 10.7 %collective-permute-start.16 = (f32[384,64]{0,1:T(8,128)S(1)}, f32[384,64]{0,1:T(8,128)S(1)}, u32[]{:S(2)}, u32[]{:S(2)}) collective-permute-start(f32[384,64]{0,1:T(8,128)S(1)} %get-tuple-element.63), channel_id=1, source_target_pairs={{0,4},{1,5},{2,6},{3,7},{4,0},{5,1},{6,2},{7,3},{8,12},{9,13},{10,... | collective-permute-start | bytes 294920 | tf_op jit(solution)/shard_map/ppermute | solution.py:62
  151.9 35.7 %collective-permute-start.14 = (bf16[48,8192]{1,0:T(8,128)(2,1)S(1)}, bf16[48,8192]{1,0:T(8,128)(2,1)S(1)}, u32[]{:S(2)}, u32[]{:S(2)}) collective-permute-start(bf16[48,8192]{1,0:T(8,128)(2,1)S(1)} %collective-permute-done.9), channel_id=1, source_target_pairs={{0,7},{1,0},{2,1},{3,2},{4,3},{5,4},{6,5},{7,6},{8,15},{9,8},{10,9... | collective-permute-start | bytes 2359304 | tf_op jit(solution)/shard_map/ppermute | solution.py:62
  152.2 35.5 %collective-permute-start.15 = (bf16[48,8192]{1,0:T(8,128)(2,1)S(1)}, bf16[48,8192]{1,0:T(8,128)(2,1)S(1)}, u32[]{:S(2)}, u32[]{:S(2)}) collective-permute-start(bf16[48,8192]{1,0:T(8,128)(2,1)S(1)} %collective-permute-done.10), channel_id=1, source_target_pairs={{0,1},{1,2},{2,3},{3,4},{4,5},{5,6},{6,7},{7,0},{8,9},{9,10},{10,1... | collective-permute-start | bytes 2359304 | tf_op jit(solution)/shard_map/ppermute | solution.py:62
  155.8 31.8 %collective-permute-start.13 = (bf16[24,8192]{1,0:T(8,128)(2,1)S(1)}, bf16[24,8192]{1,0:T(8,128)(2,1)S(1)}, u32[]{:S(2)}, u32[]{:S(2)}) collective-permute-start(bf16[24,8192]{1,0:T(8,128)(2,1)S(1)} %slice.71), channel_id=1, source_target_pairs={{0,1},{1,2},{2,3},{3,4},{4,5},{5,6},{6,7},{7,0},{8,9},{9,10},{10,1... | collective-permute-start | bytes 1179656 | tf_op jit(solution)/shard_map/ppermute | solution.py:62
  158.0 29.6 %collective-permute-start.12 = (bf16[24,8192]{1,0:T(8,128)(2,1)S(1)}, bf16[24,8192]{1,0:T(8,128)(2,1)S(1)}, u32[]{:S(2)}, u32[]{:S(2)}) collective-permute-start(bf16[24,8192]{1,0:T(8,128)(2,1)S(1)} %slice.70), channel_id=1, source_target_pairs={{0,7},{1,0},{2,1},{3,2},{4,3},{5,4},{6,5},{7,6},{8,15},{9,8},{10,9... | collective-permute-start | bytes 1179656 | tf_op jit(solution)/shard_map/ppermute | solution.py:62
  159.5 28.1 %collective-permute-start.18 = (f32[384,64]{0,1:T(8,128)S(1)}, f32[384,64]{0,1:T(8,128)S(1)}, u32[]{:S(2)}, u32[]{:S(2)}) collective-permute-start(f32[384,64]{0,1:T(8,128)S(1)} %collective-permute-done.17), channel_id=1, source_target_pairs={{0,6},{1,7},{2,0},{3,1},{4,2},{5,3},{6,4},{7,5},{8,14},{9,15},{10,... | collective-permute-start | bytes 294920 | tf_op jit(solution)/shard_map/ppermute | solution.py:62
  187.7 12.6 %collective-permute-start.21 = (f32[768,64]{0,1:T(8,128)S(1)}, f32[768,64]{0,1:T(8,128)S(1)}, u32[]{:S(2)}, u32[]{:S(2)}) collective-permute-start(f32[768,64]{0,1:T(8,128)S(1)} %maximum_add_fusion), channel_id=1, source_target_pairs={{0,2},{1,3},{2,0},{3,1},{4,6},{5,7},{6,4},{7,5},{8,10},{9,11},{10,... | collective-permute-start | bytes 589832 | tf_op jit(solution)/shard_map/ppermute | solution.py:62
  190.5 18.4 %collective-permute-start.20 = (bf16[24,8192]{1,0:T(8,128)(2,1)S(1)}, bf16[24,8192]{1,0:T(8,128)(2,1)S(1)}, u32[]{:S(2)}, u32[]{:S(2)}) collective-permute-start(bf16[24,8192]{1,0:T(8,128)(2,1)S(1)} %slice.83), channel_id=1, source_target_pairs={{0,1},{1,2},{2,3},{3,4},{4,5},{5,6},{6,7},{7,0},{8,9},{9,10},{10,1... | collective-permute-start | bytes 1179656 | tf_op jit(solution)/shard_map/ppermute | solution.py:62
  190.5 18.4 %collective-permute-start.19 = (bf16[24,8192]{1,0:T(8,128)(2,1)S(1)}, bf16[24,8192]{1,0:T(8,128)(2,1)S(1)}, u32[]{:S(2)}, u32[]{:S(2)}) collective-permute-start(bf16[24,8192]{1,0:T(8,128)(2,1)S(1)} %slice.82), channel_id=1, source_target_pairs={{0,7},{1,0},{2,1},{3,2},{4,3},{5,4},{6,5},{7,6},{8,15},{9,8},{10,9... | collective-permute-start | bytes 1179656 | tf_op jit(solution)/shard_map/ppermute | solution.py:62
  200.4 8.5 %collective-permute-start.22 = (f32[768,64]{0,1:T(8,128)S(1)}, f32[768,64]{0,1:T(8,128)S(1)}, u32[]{:S(2)}, u32[]{:S(2)}) collective-permute-start(f32[768,64]{0,1:T(8,128)S(1)} %add.91), channel_id=1, source_target_pairs={{0,1},{1,0},{2,3},{3,2},{4,5},{5,4},{6,7},{7,6},{8,9},{9,8},{10,11... | collective-permute-start | bytes 589832 | tf_op jit(solution)/shard_map/ppermute | solution.py:62
  (8 other events, 133.9 us)

commit v12 on v7

--- a/solution.py
+++ b/solution.py
@@ -74,8 +74,8 @@
         ).reshape(group_rows, tenants, rank_size)
         return jnp.sum(jnp.where(tenant_masks[:, :, None], wide, jnp.zeros((), jnp.float32)), axis=1)
 
-    sum_steps = [ring]
-    step = ring // 2
+    sum_steps = [ring // 2, ring]
+    step = ring // 4
     while step >= 1:
         sum_steps.append(step)
         step //= 2

time: 209 us -> 211 us (level)
  waiting for transfers between devices: 103 us -> 107 us
    ppermute x21, waiting for transfers between devices: 86.2 us -> 90.5 us  [hop(): return lax.ppermute(value, 'tensor', pairs)]
  transfers between devices with their start and end apart: 23 -> 23, of which waited for: 12 -> 11; matrix products, arithmetic and copies ran while one was open for 15% -> 15% of each run, Pallas kernels for 0% -> 0%
where the time goes in v12:
time: 211 us; the launch traced here: 210 us
  waiting for transfers between devices  107 us (51%)
  starting transfers between devices  58.3 us (28%)
  matrix products  25.3 us (12%)
  local copies, waits for them, and re-layouts  15.9 us (8%)
  other arithmetic  3.82 us (2%)
    ppermute x21, waiting for transfers between devices, hop(): return lax.ppermute(value, 'tensor', pairs)  90.5 us
    ppermute x21, starting transfers between devices, hop(): return lax.ppermute(value, 'tensor', pairs)  41.4 us
    dot_general x6, matrix products, on_device(): product = jnp.dot(stacked, q_weight, preferred_element_type=jnp.float32)  21.9 us
    all_to_all x1, waiting for transfers between devices, on_device(): recv = lax.all_to_all(send, 'dp', 0, 0, tiled=True)  12.7 us
    all_to_all x1, starting transfers between devices, on_device(): local_cols = lax.all_to_all(tokens, 'tensor', 1, 0, tiled=True)  11 us
    unnamed x36, local copies, waits for them, and re-layouts  9.97 us
    all_to_all x1, starting transfers between devices, on_device(): recv = lax.all_to_all(send, 'dp', 0, 0, tiled=True)  5.99 us
  transfers between devices with their start and end apart: 23, of which 11 were waited for; matrix products, arithmetic and copies ran while one was open for 15% of the time, Pallas kernels for 0%

profile of v12, /device:TPU:2, one launch (start us, length us, event | category | flops | bytes accessed | tf_op | source)
XLA Modules:
  0.0 210.5 jit_solution(17918281170294049781)
XLA Ops:
  4.8 6.0 %all-to-all-start.1 = ((bf16[16,128,512]{2,1,0:T(8,128)(2,1)}), bf16[16,128,512]{2,1,0:T(8,128)(2,1)S(1)}, u32[]{:S(2)}, u32[]{:S(2)}) async-start(bf16[16,128,512]{2,1,0:T(8,128)(2,1)} %broadcast_select_fusion), calls=%async_computation.1 | async-start | bytes 4194304 | tf_op jit(solution)/shard_map/all_to_all | solution.py:42
  10.8 5.9 %collective-permute-start.1 = (bf16[48,8192]{1,0:T(8,128)(2,1)S(1)}, bf16[48,8192]{1,0:T(8,128)(2,1)}, u32[]{:S(2)}, u32[]{:S(2)}) collective-permute-start(bf16[48,8192]{1,0:T(8,128)(2,1)S(1)} %copy-done.2), channel_id=1, source_target_pairs={{0,7},{1,0},{2,1},{3,2},{4,3},{5,4},{6,5},{7,6},{8,15},{9,8},{10,9... | collective-permute-start | bytes 2359304 | tf_op jit(solution)/shard_map/ppermute | solution.py:62
  16.7 2.9 %collective-permute-start = (bf16[48,8192]{1,0:T(8,128)(2,1)S(1)}, bf16[48,8192]{1,0:T(8,128)(2,1)}, u32[]{:S(2)}, u32[]{:S(2)}) collective-permute-start(bf16[48,8192]{1,0:T(8,128)(2,1)S(1)} %copy-done.2), channel_id=1, source_target_pairs={{0,8},{1,9},{2,10},{3,11},{4,12},{5,13},{6,14},{7,15},{8,0},{9,1},... | collective-permute-start | bytes 2359304 | tf_op jit(solution)/shard_map/ppermute | solution.py:62
  21.1 5.6 %constant_dynamic-update-slice_fusion.1 = (f32[16,48,512]{2,1,0:T(8,128)}, f32[1,48,512]{2,1,0:T(8,128)S(1)}) fusion(bf16[48,8192]{1,0:T(8,128)(2,1)S(1)} %copy-done.2, bf16[8192,512]{1,0:T(8,128)(2,1)} %param.8), kind=kOutput, calls=%fused_computation.99 | convolution fusion | flops 402653184 | bytes 9371648 | tf_op jit(solution)/shard_map/dot_general | solution.py:150
  26.6 12.7 %all-to-all-done.1 = bf16[16,128,512]{2,1,0:T(8,128)(2,1)S(1)} async-done(((bf16[16,128,512]{2,1,0:T(8,128)(2,1)}), bf16[16,128,512]{2,1,0:T(8,128)(2,1)S(1)}, u32[]{:S(2)}, u32[]{:S(2)}) %all-to-all-start.1) | async-done | bytes 2097184 | tf_op jit(solution)/shard_map/all_to_all | solution.py:42
  39.3 11.0 %all-to-all-start = ((bf16[48,16,512]{2,0,1:T(8,128)(2,1)}), bf16[48,16,512]{2,0,1:T(8,128)(2,1)}, u32[]{:S(2)}, u32[]{:S(2)}) async-start(bf16[48,16,512]{2,0,1:T(8,128)(2,1)} %bitcast.133), calls=%async_computation | async-start | bytes 1572864 | tf_op jit(solution)/shard_map/all_to_all | solution.py:69
  50.9 3.4 %collective-permute-done = bf16[48,8192]{1,0:T(8,128)(2,1)} collective-permute-done((bf16[48,8192]{1,0:T(8,128)(2,1)S(1)}, bf16[48,8192]{1,0:T(8,128)(2,1)}, u32[]{:S(2)}, u32[]{:S(2)}) %collective-permute-start) | collective-permute-done | bytes 786464 | tf_op jit(solution)/shard_map/ppermute | solution.py:62
  54.3 2.4 %collective-permute-start.6 = (bf16[48,8192]{1,0:T(8,128)(2,1)}, bf16[48,8192]{1,0:T(8,128)(2,1)}, u32[]{:S(2)}, u32[]{:S(2)}) collective-permute-start(bf16[48,8192]{1,0:T(8,128)(2,1)} %collective-permute-done), channel_id=1, source_target_pairs={{0,1},{1,2},{2,3},{3,4},{4,5},{5,6},{6,7},{7,0},{8,9},{9,10},{10,1... | collective-permute-start | bytes 2359304 | tf_op jit(solution)/shard_map/ppermute | solution.py:62
  56.6 4.9 %collective-permute-start.5 = (bf16[48,8192]{1,0:T(8,128)(2,1)}, bf16[48,8192]{1,0:T(8,128)(2,1)}, u32[]{:S(2)}, u32[]{:S(2)}) collective-permute-start(bf16[48,8192]{1,0:T(8,128)(2,1)} %collective-permute-done), channel_id=1, source_target_pairs={{0,7},{1,0},{2,1},{3,2},{4,3},{5,4},{6,5},{7,6},{8,15},{9,8},{10,9... | collective-permute-start | bytes 2359304 | tf_op jit(solution)/shard_map/ppermute | solution.py:62
  61.5 2.0 collective-permute-start.3
  63.5 5.5 %fusion.16 = f32[144,512]{1,0:T(8,128)S(1)} fusion(bf16[8192,512]{1,0:T(8,128)(2,1)} %param.8, bf16[48,8192]{1,0:T(8,128)(2,1)} %collective-permute-done, bf16[48,8192]{1,0:T(8,128)(2,1)} %collective-permute-done.2, bf16[48,8192]{1,0:T(8,128)(2,1)} %collective-permute-done.1), kind=kOutput, calls=%fused_computation.19 | convolution fusion | flops 1215037440 | bytes 11042816 | tf_op jit(solution)/shard_map/dot_general | solution.py:150
  71.1 3.6 %all-to-all-done = bf16[48,16,512]{2,0,1:T(8,128)(2,1)} async-done(((bf16[48,16,512]{2,0,1:T(8,128)(2,1)}), bf16[48,16,512]{2,0,1:T(8,128)(2,1)}, u32[]{:S(2)}, u32[]{:S(2)}) %all-to-all-start) | async-done | bytes 786464 | tf_op jit(solution)/shard_map/all_to_all | solution.py:69
  74.7 28.6 %collective-permute-done.3 = bf16[48,8192]{1,0:T(8,128)(2,1)} collective-permute-done((bf16[48,8192]{1,0:T(8,128)(2,1)}, bf16[48,8192]{1,0:T(8,128)(2,1)}, u32[]{:S(2)}, u32[]{:S(2)}) %collective-permute-start.3) | collective-permute-done | bytes 786464 | tf_op jit(solution)/shard_map/ppermute | solution.py:62
  106.5 3.4 %collective-permute-start.11 = (f32[768,64]{0,1:T(8,128)S(1)}, f32[768,64]{0,1:T(8,128)S(1)}, u32[]{:S(2)}, u32[]{:S(2)}) collective-permute-start(f32[768,64]{0,1:T(8,128)S(1)} %select_reduce_fusion), channel_id=1, source_target_pairs={{0,4},{1,5},{2,6},{3,7},{4,0},{5,1},{6,2},{7,3},{8,12},{9,13},{10,... | collective-permute-start | bytes 589832 | tf_op jit(solution)/shard_map/ppermute | solution.py:62
  109.9 2.7 %collective-permute-start.7 = (bf16[48,8192]{1,0:T(8,128)(2,1)}, bf16[48,8192]{1,0:T(8,128)(2,1)S(1)}, u32[]{:S(2)}, u32[]{:S(2)}) collective-permute-start(bf16[48,8192]{1,0:T(8,128)(2,1)} %collective-permute-done.3), channel_id=1, source_target_pairs={{0,7},{1,0},{2,1},{3,2},{4,3},{5,4},{6,5},{7,6},{8,15},{9,8},{10,9... | collective-permute-start | bytes 2359304 | tf_op jit(solution)/shard_map/ppermute | solution.py:62
  112.5 3.2 %collective-permute-start.9 = (bf16[48,8192]{1,0:T(8,128)(2,1)}, bf16[48,8192]{1,0:T(8,128)(2,1)S(1)}, u32[]{:S(2)}, u32[]{:S(2)}) collective-permute-start(bf16[48,8192]{1,0:T(8,128)(2,1)} %collective-permute-done.5), channel_id=1, source_target_pairs={{0,7},{1,0},{2,1},{3,2},{4,3},{5,4},{6,5},{7,6},{8,15},{9,8},{10,9... | collective-permute-start | bytes 2359304 | tf_op jit(solution)/shard_map/ppermute | solution.py:62
  115.8 6.1 %fusion = f32[192,512]{1,0:T(8,128)S(1)} fusion(bf16[8192,512]{1,0:T(8,128)(2,1)} %param.8, bf16[48,8192]{1,0:T(8,128)(2,1)} %collective-permute-done.6, bf16[48,8192]{1,0:T(8,128)(2,1)} %collective-permute-done.5, bf16[48,8192]{1,0:T(8,128)(2,1)} %collective-permute-done.4, bf16[48,8192]{1,0:T(8,128)(2,1)} %collective-permute-done.3), kind=kOutput, calls=%fused_computation.3 | convolution fusion | flops 1623195648 | bytes 11927552 | tf_op jit(solution)/shard_map/dot_general | solution.py:150
  122.6 14.5 %collective-permute-done.7 = bf16[48,8192]{1,0:T(8,128)(2,1)S(1)} collective-permute-done((bf16[48,8192]{1,0:T(8,128)(2,1)}, bf16[48,8192]{1,0:T(8,128)(2,1)S(1)}, u32[]{:S(2)}, u32[]{:S(2)}) %collective-permute-start.7) | collective-permute-done | bytes 786464 | tf_op jit(solution)/shard_map/ppermute | solution.py:62
  137.1 16.1 %collective-permute-done.9 = bf16[48,8192]{1,0:T(8,128)(2,1)S(1)} collective-permute-done((bf16[48,8192]{1,0:T(8,128)(2,1)}, bf16[48,8192]{1,0:T(8,128)(2,1)S(1)}, u32[]{:S(2)}, u32[]{:S(2)}) %collective-permute-start.9) | collective-permute-done | bytes 786464 | tf_op jit(solution)/shard_map/ppermute | solution.py:62
  160.4 3.1 %collective-permute-start.16 = (f32[768,64]{0,1:T(8,128)S(1)}, f32[768,64]{0,1:T(8,128)S(1)}, u32[]{:S(2)}, u32[]{:S(2)}) collective-permute-start(f32[768,64]{0,1:T(8,128)S(1)} %add.86), channel_id=1, source_target_pairs={{0,8},{1,9},{2,10},{3,11},{4,12},{5,13},{6,14},{7,15},{8,0},{9,1},... | collective-permute-start | bytes 589832 | tf_op jit(solution)/shard_map/ppermute | solution.py:62
  164.1 3.6 %collective-permute-done.16 = f32[768,64]{0,1:T(8,128)S(1)} collective-permute-done((f32[768,64]{0,1:T(8,128)S(1)}, f32[768,64]{0,1:T(8,128)S(1)}, u32[]{:S(2)}, u32[]{:S(2)}) %collective-permute-start.16) | collective-permute-done | bytes 196640 | tf_op jit(solution)/shard_map/ppermute | solution.py:62
  167.7 14.6 %collective-permute-done.14 = bf16[48,8192]{1,0:T(8,128)(2,1)S(1)} collective-permute-done((bf16[48,8192]{1,0:T(8,128)(2,1)S(1)}, bf16[48,8192]{1,0:T(8,128)(2,1)S(1)}, u32[]{:S(2)}, u32[]{:S(2)}) %collective-permute-start.14) | collective-permute-done | bytes 786464 | tf_op jit(solution)/shard_map/ppermute | solution.py:62
  183.7 2.9 %collective-permute-start.18 = (bf16[24,8192]{1,0:T(8,128)(2,1)S(1)}, bf16[24,8192]{1,0:T(8,128)(2,1)S(1)}, u32[]{:S(2)}, u32[]{:S(2)}) collective-permute-start(bf16[24,8192]{1,0:T(8,128)(2,1)S(1)} %slice.75), channel_id=1, source_target_pairs={{0,1},{1,2},{2,3},{3,4},{4,5},{5,6},{6,7},{7,0},{8,9},{9,10},{10,1... | collective-permute-start | bytes 1179656 | tf_op jit(solution)/shard_map/ppermute | solution.py:62
  195.3 7.7 %collective-permute-done.20 = f32[768,64]{0,1:T(8,128)S(1)} collective-permute-done((f32[768,64]{0,1:T(8,128)S(1)}, f32[768,64]{0,1:T(8,128)S(1)}, u32[]{:S(2)}, u32[]{:S(2)}) %collective-permute-start.20) | collective-permute-done | bytes 196640 | tf_op jit(solution)/shard_map/ppermute | solution.py:62
  (102 shorter events, 37.9 us)
Async XLA Ops:
  4.8 34.5 %all-to-all-start.1 = ((bf16[16,128,512]{2,1,0:T(8,128)(2,1)}), bf16[16,128,512]{2,1,0:T(8,128)(2,1)S(1)}, u32[]{:S(2)}, u32[]{:S(2)}) async-start(bf16[16,128,512]{2,1,0:T(8,128)(2,1)} %broadcast_select_fusion), calls=%async_computation.1 | async-start | bytes 4194304 | tf_op jit(solution)/shard_map/all_to_all | solution.py:42
  10.8 40.1 %collective-permute-start.1 = (bf16[48,8192]{1,0:T(8,128)(2,1)S(1)}, bf16[48,8192]{1,0:T(8,128)(2,1)}, u32[]{:S(2)}, u32[]{:S(2)}) collective-permute-start(bf16[48,8192]{1,0:T(8,128)(2,1)S(1)} %copy-done.2), channel_id=1, source_target_pairs={{0,7},{1,0},{2,1},{3,2},{4,3},{5,4},{6,5},{7,6},{8,15},{9,8},{10,9... | collective-permute-start | bytes 2359304 | tf_op jit(solution)/shard_map/ppermute | solution.py:62
  16.7 37.6 %collective-permute-start = (bf16[48,8192]{1,0:T(8,128)(2,1)S(1)}, bf16[48,8192]{1,0:T(8,128)(2,1)}, u32[]{:S(2)}, u32[]{:S(2)}) collective-permute-start(bf16[48,8192]{1,0:T(8,128)(2,1)S(1)} %copy-done.2), channel_id=1, source_target_pairs={{0,8},{1,9},{2,10},{3,11},{4,12},{5,13},{6,14},{7,15},{8,0},{9,1},... | collective-permute-start | bytes 2359304 | tf_op jit(solution)/shard_map/ppermute | solution.py:62
  19.6 34.7 %collective-permute-start.2 = (bf16[48,8192]{1,0:T(8,128)(2,1)S(1)}, bf16[48,8192]{1,0:T(8,128)(2,1)}, u32[]{:S(2)}, u32[]{:S(2)}) collective-permute-start(bf16[48,8192]{1,0:T(8,128)(2,1)S(1)} %copy-done.2), channel_id=1, source_target_pairs={{0,1},{1,2},{2,3},{3,4},{4,5},{5,6},{6,7},{7,0},{8,9},{9,10},{10,1... | collective-permute-start | bytes 2359304 | tf_op jit(solution)/shard_map/ppermute | solution.py:62
  39.3 35.4 %all-to-all-start = ((bf16[48,16,512]{2,0,1:T(8,128)(2,1)}), bf16[48,16,512]{2,0,1:T(8,128)(2,1)}, u32[]{:S(2)}, u32[]{:S(2)}) async-start(bf16[48,16,512]{2,0,1:T(8,128)(2,1)} %bitcast.133), calls=%async_computation | async-start | bytes 1572864 | tf_op jit(solution)/shard_map/all_to_all | solution.py:69
  54.3 50.3 %collective-permute-start.6 = (bf16[48,8192]{1,0:T(8,128)(2,1)}, bf16[48,8192]{1,0:T(8,128)(2,1)}, u32[]{:S(2)}, u32[]{:S(2)}) collective-permute-start(bf16[48,8192]{1,0:T(8,128)(2,1)} %collective-permute-done), channel_id=1, source_target_pairs={{0,1},{1,2},{2,3},{3,4},{4,5},{5,6},{6,7},{7,0},{8,9},{9,10},{10,1... | collective-permute-start | bytes 2359304 | tf_op jit(solution)/shard_map/ppermute | solution.py:62
  56.6 47.9 %collective-permute-start.5 = (bf16[48,8192]{1,0:T(8,128)(2,1)}, bf16[48,8192]{1,0:T(8,128)(2,1)}, u32[]{:S(2)}, u32[]{:S(2)}) collective-permute-start(bf16[48,8192]{1,0:T(8,128)(2,1)} %collective-permute-done), channel_id=1, source_target_pairs={{0,7},{1,0},{2,1},{3,2},{4,3},{5,4},{6,5},{7,6},{8,15},{9,8},{10,9... | collective-permute-start | bytes 2359304 | tf_op jit(solution)/shard_map/ppermute | solution.py:62
  61.5 41.9 %collective-permute-start.3 = (bf16[48,8192]{1,0:T(8,128)(2,1)}, bf16[48,8192]{1,0:T(8,128)(2,1)}, u32[]{:S(2)}, u32[]{:S(2)}) collective-permute-start(bf16[48,8192]{1,0:T(8,128)(2,1)} %collective-permute-done.1), channel_id=1, source_target_pairs={{0,7},{1,0},{2,1},{3,2},{4,3},{5,4},{6,5},{7,6},{8,15},{9,8},{10,9... | collective-permute-start | bytes 2359304 | tf_op jit(solution)/shard_map/ppermute | solution.py:62
  63.5 41.0 %collective-permute-start.4 = (bf16[48,8192]{1,0:T(8,128)(2,1)}, bf16[48,8192]{1,0:T(8,128)(2,1)}, u32[]{:S(2)}, u32[]{:S(2)}) collective-permute-start(bf16[48,8192]{1,0:T(8,128)(2,1)} %collective-permute-done.2), channel_id=1, source_target_pairs={{0,1},{1,2},{2,3},{3,4},{4,5},{5,6},{6,7},{7,0},{8,9},{9,10},{10,1... | collective-permute-start | bytes 2359304 | tf_op jit(solution)/shard_map/ppermute | solution.py:62
  104.6 54.0 %slice-start = ((s8[8388608]{0:T(1024)(128)(4,1)}), s8[4194304]{0:T(1024)(128)(4,1)S(1)}, s32[]{:S(2)}) async-start(s8[8388608]{0:T(1024)(128)(4,1)} %bitcast.130), calls=%async_computation.2 | async-start | bytes 8388608
  106.5 16.1 %collective-permute-start.11 = (f32[768,64]{0,1:T(8,128)S(1)}, f32[768,64]{0,1:T(8,128)S(1)}, u32[]{:S(2)}, u32[]{:S(2)}) collective-permute-start(f32[768,64]{0,1:T(8,128)S(1)} %select_reduce_fusion), channel_id=1, source_target_pairs={{0,4},{1,5},{2,6},{3,7},{4,0},{5,1},{6,2},{7,3},{8,12},{9,13},{10,... | collective-permute-start | bytes 589832 | tf_op jit(solution)/shard_map/ppermute | solution.py:62
  109.9 27.2 %collective-permute-start.7 = (bf16[48,8192]{1,0:T(8,128)(2,1)}, bf16[48,8192]{1,0:T(8,128)(2,1)S(1)}, u32[]{:S(2)}, u32[]{:S(2)}) collective-permute-start(bf16[48,8192]{1,0:T(8,128)(2,1)} %collective-permute-done.3), channel_id=1, source_target_pairs={{0,7},{1,0},{2,1},{3,2},{4,3},{5,4},{6,5},{7,6},{8,15},{9,8},{10,9... | collective-permute-start | bytes 2359304 | tf_op jit(solution)/shard_map/ppermute | solution.py:62
  112.5 24.5 %collective-permute-start.8 = (bf16[48,8192]{1,0:T(8,128)(2,1)}, bf16[48,8192]{1,0:T(8,128)(2,1)S(1)}, u32[]{:S(2)}, u32[]{:S(2)}) collective-permute-start(bf16[48,8192]{1,0:T(8,128)(2,1)} %collective-permute-done.4), channel_id=1, source_target_pairs={{0,1},{1,2},{2,3},{3,4},{4,5},{5,6},{6,7},{7,0},{8,9},{9,10},{10,1... | collective-permute-start | bytes 2359304 | tf_op jit(solution)/shard_map/ppermute | solution.py:62
  112.5 40.6 %collective-permute-start.9 = (bf16[48,8192]{1,0:T(8,128)(2,1)}, bf16[48,8192]{1,0:T(8,128)(2,1)S(1)}, u32[]{:S(2)}, u32[]{:S(2)}) collective-permute-start(bf16[48,8192]{1,0:T(8,128)(2,1)} %collective-permute-done.5), channel_id=1, source_target_pairs={{0,7},{1,0},{2,1},{3,2},{4,3},{5,4},{6,5},{7,6},{8,15},{9,8},{10,9... | collective-permute-start | bytes 2359304 | tf_op jit(solution)/shard_map/ppermute | solution.py:62
  115.8 37.4 %collective-permute-start.10 = (bf16[48,8192]{1,0:T(8,128)(2,1)}, bf16[48,8192]{1,0:T(8,128)(2,1)S(1)}, u32[]{:S(2)}, u32[]{:S(2)}) collective-permute-start(bf16[48,8192]{1,0:T(8,128)(2,1)} %collective-permute-done.6), channel_id=1, source_target_pairs={{0,1},{1,2},{2,3},{3,4},{4,5},{5,6},{6,7},{7,0},{8,9},{9,10},{10,1... | collective-permute-start | bytes 2359304 | tf_op jit(solution)/shard_map/ppermute | solution.py:62
  153.2 14.5 %collective-permute-start.13 = (bf16[24,8192]{1,0:T(8,128)(2,1)S(1)}, bf16[24,8192]{1,0:T(8,128)(2,1)S(1)}, u32[]{:S(2)}, u32[]{:S(2)}) collective-permute-start(bf16[24,8192]{1,0:T(8,128)(2,1)S(1)} %slice.65), channel_id=1, source_target_pairs={{0,1},{1,2},{2,3},{3,4},{4,5},{5,6},{6,7},{7,0},{8,9},{9,10},{10,1... | collective-permute-start | bytes 1179656 | tf_op jit(solution)/shard_map/ppermute | solution.py:62
  154.7 13.0 %collective-permute-start.12 = (bf16[24,8192]{1,0:T(8,128)(2,1)S(1)}, bf16[24,8192]{1,0:T(8,128)(2,1)S(1)}, u32[]{:S(2)}, u32[]{:S(2)}) collective-permute-start(bf16[24,8192]{1,0:T(8,128)(2,1)S(1)} %slice.64), channel_id=1, source_target_pairs={{0,7},{1,0},{2,1},{3,2},{4,3},{5,4},{6,5},{7,6},{8,15},{9,8},{10,9... | collective-permute-start | bytes 1179656 | tf_op jit(solution)/shard_map/ppermute | solution.py:62
  156.6 25.8 %collective-permute-start.14 = (bf16[48,8192]{1,0:T(8,128)(2,1)S(1)}, bf16[48,8192]{1,0:T(8,128)(2,1)S(1)}, u32[]{:S(2)}, u32[]{:S(2)}) collective-permute-start(bf16[48,8192]{1,0:T(8,128)(2,1)S(1)} %collective-permute-done.9), channel_id=1, source_target_pairs={{0,7},{1,0},{2,1},{3,2},{4,3},{5,4},{6,5},{7,6},{8,15},{9,8},{10,9... | collective-permute-start | bytes 2359304 | tf_op jit(solution)/shard_map/ppermute | solution.py:62
  158.0 24.4 %collective-permute-start.15 = (bf16[48,8192]{1,0:T(8,128)(2,1)S(1)}, bf16[48,8192]{1,0:T(8,128)(2,1)S(1)}, u32[]{:S(2)}, u32[]{:S(2)}) collective-permute-start(bf16[48,8192]{1,0:T(8,128)(2,1)S(1)} %collective-permute-done.10), channel_id=1, source_target_pairs={{0,1},{1,2},{2,3},{3,4},{4,5},{5,6},{6,7},{7,0},{8,9},{9,10},{10,1... | collective-permute-start | bytes 2359304 | tf_op jit(solution)/shard_map/ppermute | solution.py:62
  160.4 7.3 %collective-permute-start.16 = (f32[768,64]{0,1:T(8,128)S(1)}, f32[768,64]{0,1:T(8,128)S(1)}, u32[]{:S(2)}, u32[]{:S(2)}) collective-permute-start(f32[768,64]{0,1:T(8,128)S(1)} %add.86), channel_id=1, source_target_pairs={{0,8},{1,9},{2,10},{3,11},{4,12},{5,13},{6,14},{7,15},{8,0},{9,1},... | collective-permute-start | bytes 589832 | tf_op jit(solution)/shard_map/ppermute | solution.py:62
  182.4 11.9 %collective-permute-start.19 = (f32[768,64]{0,1:T(8,128)S(1)}, f32[768,64]{0,1:T(8,128)S(1)}, u32[]{:S(2)}, u32[]{:S(2)}) collective-permute-start(f32[768,64]{0,1:T(8,128)S(1)} %add.87), channel_id=1, source_target_pairs={{0,2},{1,3},{2,0},{3,1},{4,6},{5,7},{6,4},{7,5},{8,10},{9,11},{10,... | collective-permute-start | bytes 589832 | tf_op jit(solution)/shard_map/ppermute | solution.py:62
  183.7 19.4 %collective-permute-start.18 = (bf16[24,8192]{1,0:T(8,128)(2,1)S(1)}, bf16[24,8192]{1,0:T(8,128)(2,1)S(1)}, u32[]{:S(2)}, u32[]{:S(2)}) collective-permute-start(bf16[24,8192]{1,0:T(8,128)(2,1)S(1)} %slice.75), channel_id=1, source_target_pairs={{0,1},{1,2},{2,3},{3,4},{4,5},{5,6},{6,7},{7,0},{8,9},{9,10},{10,1... | collective-permute-start | bytes 1179656 | tf_op jit(solution)/shard_map/ppermute | solution.py:62
  186.6 16.5 %collective-permute-start.17 = (bf16[24,8192]{1,0:T(8,128)(2,1)S(1)}, bf16[24,8192]{1,0:T(8,128)(2,1)S(1)}, u32[]{:S(2)}, u32[]{:S(2)}) collective-permute-start(bf16[24,8192]{1,0:T(8,128)(2,1)S(1)} %slice.74), channel_id=1, source_target_pairs={{0,7},{1,0},{2,1},{3,2},{4,3},{5,4},{6,5},{7,6},{8,15},{9,8},{10,9... | collective-permute-start | bytes 1179656 | tf_op jit(solution)/shard_map/ppermute | solution.py:62
  194.3 8.8 %collective-permute-start.20 = (f32[768,64]{0,1:T(8,128)S(1)}, f32[768,64]{0,1:T(8,128)S(1)}, u32[]{:S(2)}, u32[]{:S(2)}) collective-permute-start(f32[768,64]{0,1:T(8,128)S(1)} %add.91), channel_id=1, source_target_pairs={{0,1},{1,0},{2,3},{3,2},{4,5},{5,4},{6,7},{7,6},{8,9},{9,8},{10,11... | collective-permute-start | bytes 589832 | tf_op jit(solution)/shard_map/ppermute | solution.py:62
  (6 other events, 81.6 us)

commit v13 on v7

--- a/solution.py
+++ b/solution.py
@@ -162,17 +162,24 @@
         )
         return ordered.reshape((group_rows,) + own_list[0].shape[1:])
 
-    base_projection = to_group_order(base_of["own"], base_of["partner"])
-    low_rank = low_sum.astype(jnp.bfloat16)
-    low_wide = jnp.where(
-        tenant_masks[:, :, None], low_rank[:, None, :], jnp.zeros((), jnp.bfloat16)
-    )
+    base_rel = jnp.stack([jnp.stack(base_of["own"]), jnp.stack(base_of["partner"])])
+    base_rel = base_rel.reshape(group_rows, columns)
+    sides = jnp.arange(2, dtype=jnp.int32)[:, None, None]
+    steps = jnp.arange(ring, dtype=jnp.int32)[None, :, None]
+    rows = jnp.arange(shard_rows, dtype=jnp.int32)[None, None, :]
+    row_half = jnp.where(sides == 0, half, 1 - half)
+    row_of = ((row_half * ring + (ring_at + steps) % ring) * shard_rows + rows).reshape(group_rows)
+    low_rank = jnp.take(low_sum.astype(jnp.bfloat16), row_of, axis=0)
+    masks_rel = jnp.take(tenant_masks, row_of, axis=0)
+    low_wide = jnp.where(masks_rel[:, :, None], low_rank[:, None, :], jnp.zeros((), jnp.bfloat16))
     adapter_contribution = jnp.dot(
         low_wide.reshape(group_rows, tenants * rank_size),
         up_flat,
         preferred_element_type=jnp.float32,
     )
-    return (base_projection + adapter_scale * adapter_contribution).astype(jnp.bfloat16)
+    out_rel = (base_rel + adapter_scale * adapter_contribution).astype(jnp.bfloat16)
+    out_rel = out_rel.reshape(2, ring, shard_rows, columns)
+    return to_group_order([out_rel[0, k] for k in range(ring)], [out_rel[1, k] for k in range(ring)])
 
 
 def solution(mesh):

time: 209 us -> 234 us (1.12)
  waiting for transfers between devices: 103 us -> 128 us
  starting transfers between devices: 60.4 us -> 55.8 us
  matrix products: 25.3 us -> 28.4 us
    ppermute x21, waiting for transfers between devices: 86.2 us -> 114 us  [hop(): return lax.ppermute(value, 'tensor', pairs)]
    unnamed x36 -> x46, local copies, waits for them, and re-layouts: 9.97 us -> 4.96 us
    ppermute x21, starting transfers between devices: 43.4 us -> 38.8 us  [hop(): return lax.ppermute(value, 'tensor', pairs)]
    dot_general x6, matrix products: 21.9 us -> 26 us  [on_device(): product = jnp.dot(stacked, q_weight, preferred_element_type=jnp.float32)]
    gather x0 -> x2, local copies, waits for them, and re-layouts: none -> 3.59 us  [the longest x1 1.87 us: on_device(): low_rank = jnp.take(low_sum.astype(jnp.bfloat16), row_of, axis=0)]
  transfers between devices with their start and end apart: 23 -> 23, of which waited for: 12 -> 13; matrix products, arithmetic and copies ran while one was open for 15% -> 15% of each run, Pallas kernels for 0% -> 0%
where the time goes in v13:
time: 234 us; the launch traced here: 233 us
  waiting for transfers between devices  128 us (55%)
  starting transfers between devices  55.8 us (24%)
  matrix products  28.4 us (12%)
  local copies, waits for them, and re-layouts  15.2 us (6%)
  other arithmetic  5.59 us (2%)
    ppermute x21, waiting for transfers between devices, hop(): return lax.ppermute(value, 'tensor', pairs)  114 us
    ppermute x21, starting transfers between devices, hop(): return lax.ppermute(value, 'tensor', pairs)  38.8 us
    dot_general x6, matrix products, on_device(): product = jnp.dot(stacked, q_weight, preferred_element_type=jnp.float32)  26 us
    all_to_all x1, starting transfers between devices, on_device(): local_cols = lax.all_to_all(tokens, 'tensor', 1, 0, tiled=True)  11 us
    all_to_all x1, waiting for transfers between devices, on_device(): recv = lax.all_to_all(send, 'dp', 0, 0, tiled=True)  10.5 us
    all_to_all x1, starting transfers between devices, on_device(): recv = lax.all_to_all(send, 'dp', 0, 0, tiled=True)  5.99 us
    unnamed x46, local copies, waits for them, and re-layouts  4.96 us
  transfers between devices with their start and end apart: 23, of which 13 were waited for; matrix products, arithmetic and copies ran while one was open for 15% of the time, Pallas kernels for 0%

profile of v13, /device:TPU:2, one launch (start us, length us, event | category | flops | bytes accessed | tf_op | source)
XLA Modules:
  0.0 233.5 jit_solution(11972267729928121579)
XLA Ops:
  5.1 6.0 %all-to-all-start.1 = ((bf16[16,128,512]{2,1,0:T(8,128)(2,1)}), bf16[16,128,512]{2,1,0:T(8,128)(2,1)S(1)}, u32[]{:S(2)}, u32[]{:S(2)}) async-start(bf16[16,128,512]{2,1,0:T(8,128)(2,1)} %broadcast_select_fusion), calls=%async_computation.1 | async-start | bytes 4194304 | tf_op jit(solution)/shard_map/all_to_all | solution.py:42
  11.1 3.0 %collective-permute-start = (bf16[48,8192]{1,0:T(8,128)(2,1)S(1)}, bf16[48,8192]{1,0:T(8,128)(2,1)}, u32[]{:S(2)}, u32[]{:S(2)}) collective-permute-start(bf16[48,8192]{1,0:T(8,128)(2,1)S(1)} %copy-done.2), channel_id=1, source_target_pairs={{0,8},{1,9},{2,10},{3,11},{4,12},{5,13},{6,14},{7,15},{8,0},{9,1},... | collective-permute-start | bytes 2359304 | tf_op jit(solution)/shard_map/ppermute | solution.py:62
  14.1 5.9 %collective-permute-start.1 = (bf16[48,8192]{1,0:T(8,128)(2,1)S(1)}, bf16[48,8192]{1,0:T(8,128)(2,1)}, u32[]{:S(2)}, u32[]{:S(2)}) collective-permute-start(bf16[48,8192]{1,0:T(8,128)(2,1)S(1)} %copy-done.2), channel_id=1, source_target_pairs={{0,7},{1,0},{2,1},{3,2},{4,3},{5,4},{6,5},{7,6},{8,15},{9,8},{10,9... | collective-permute-start | bytes 2359304 | tf_op jit(solution)/shard_map/ppermute | solution.py:62
  23.6 5.6 %fusion.33 = f32[8,48,512]{2,1,0:T(8,128)} fusion(bf16[48,8192]{1,0:T(8,128)(2,1)S(1)} %copy-done.2, bf16[8192,512]{1,0:T(8,128)(2,1)} %param.8), kind=kOutput, calls=%fused_computation.44 | convolution fusion | flops 402653184 | bytes 9273344 | tf_op jit(solution)/shard_map/dot_general | solution.py:150
  29.1 10.5 %all-to-all-done.1 = bf16[16,128,512]{2,1,0:T(8,128)(2,1)S(1)} async-done(((bf16[16,128,512]{2,1,0:T(8,128)(2,1)}), bf16[16,128,512]{2,1,0:T(8,128)(2,1)S(1)}, u32[]{:S(2)}, u32[]{:S(2)}) %all-to-all-start.1) | async-done | bytes 2097184 | tf_op jit(solution)/shard_map/all_to_all | solution.py:42
  39.7 11.0 %all-to-all-start = ((bf16[48,16,512]{2,0,1:T(8,128)(2,1)}), bf16[48,16,512]{2,0,1:T(8,128)(2,1)}, u32[]{:S(2)}, u32[]{:S(2)}) async-start(bf16[48,16,512]{2,0,1:T(8,128)(2,1)} %bitcast.209), calls=%async_computation | async-start | bytes 1572864 | tf_op jit(solution)/shard_map/all_to_all | solution.py:69
  51.0 3.6 %collective-permute-done = bf16[48,8192]{1,0:T(8,128)(2,1)} collective-permute-done((bf16[48,8192]{1,0:T(8,128)(2,1)S(1)}, bf16[48,8192]{1,0:T(8,128)(2,1)}, u32[]{:S(2)}, u32[]{:S(2)}) %collective-permute-start) | collective-permute-done | bytes 786464 | tf_op jit(solution)/shard_map/ppermute | solution.py:62
  54.6 7.2 %collective-permute-start.5 = (bf16[48,8192]{1,0:T(8,128)(2,1)}, bf16[48,8192]{1,0:T(8,128)(2,1)}, u32[]{:S(2)}, u32[]{:S(2)}) collective-permute-start(bf16[48,8192]{1,0:T(8,128)(2,1)} %collective-permute-done), channel_id=1, source_target_pairs={{0,7},{1,0},{2,1},{3,2},{4,3},{5,4},{6,5},{7,6},{8,15},{9,8},{10,9... | collective-permute-start | bytes 2359304 | tf_op jit(solution)/shard_map/ppermute | solution.py:62
  61.8 3.2 %collective-permute-start.3 = (bf16[48,8192]{1,0:T(8,128)(2,1)}, bf16[48,8192]{1,0:T(8,128)(2,1)}, u32[]{:S(2)}, u32[]{:S(2)}) collective-permute-start(bf16[48,8192]{1,0:T(8,128)(2,1)} %collective-permute-done.1), channel_id=1, source_target_pairs={{0,7},{1,0},{2,1},{3,2},{4,3},{5,4},{6,5},{7,6},{8,15},{9,8},{10,9... | collective-permute-start | bytes 2359304 | tf_op jit(solution)/shard_map/ppermute | solution.py:62
  65.1 5.5 %fusion.16 = f32[144,512]{1,0:T(8,128)S(1)} fusion(bf16[8192,512]{1,0:T(8,128)(2,1)} %param.8, bf16[48,8192]{1,0:T(8,128)(2,1)} %collective-permute-done, bf16[48,8192]{1,0:T(8,128)(2,1)} %collective-permute-done.2, bf16[48,8192]{1,0:T(8,128)(2,1)} %collective-permute-done.1), kind=kOutput, calls=%fused_computation.21 | convolution fusion | flops 1215037440 | bytes 11042816 | tf_op jit(solution)/shard_map/dot_general | solution.py:150
  72.0 3.0 %all-to-all-done = bf16[48,16,512]{2,0,1:T(8,128)(2,1)} async-done(((bf16[48,16,512]{2,0,1:T(8,128)(2,1)}), bf16[48,16,512]{2,0,1:T(8,128)(2,1)}, u32[]{:S(2)}, u32[]{:S(2)}) %all-to-all-start) | async-done | bytes 786464 | tf_op jit(solution)/shard_map/all_to_all | solution.py:69
  75.0 28.6 %collective-permute-done.3 = bf16[48,8192]{1,0:T(8,128)(2,1)} collective-permute-done((bf16[48,8192]{1,0:T(8,128)(2,1)}, bf16[48,8192]{1,0:T(8,128)(2,1)}, u32[]{:S(2)}, u32[]{:S(2)}) %collective-permute-start.3) | collective-permute-done | bytes 786464 | tf_op jit(solution)/shard_map/ppermute | solution.py:62
  106.9 2.7 %collective-permute-start.9 = (bf16[48,8192]{1,0:T(8,128)(2,1)}, bf16[48,8192]{1,0:T(8,128)(2,1)}, u32[]{:S(2)}, u32[]{:S(2)}) collective-permute-start(bf16[48,8192]{1,0:T(8,128)(2,1)} %collective-permute-done.5), channel_id=1, source_target_pairs={{0,7},{1,0},{2,1},{3,2},{4,3},{5,4},{6,5},{7,6},{8,15},{9,8},{10,9... | collective-permute-start | bytes 2359304 | tf_op jit(solution)/shard_map/ppermute | solution.py:62
  111.5 3.1 %collective-permute-start.11 = (f32[768,64]{1,0:T(8,128)S(1)}, f32[768,64]{1,0:T(8,128)S(1)}, u32[]{:S(2)}, u32[]{:S(2)}) collective-permute-start(f32[768,64]{1,0:T(8,128)S(1)} %copy.45), channel_id=1, source_target_pairs={{0,8},{1,9},{2,10},{3,11},{4,12},{5,13},{6,14},{7,15},{8,0},{9,1},... | collective-permute-start | bytes 589832 | tf_op jit(solution)/shard_map/ppermute | solution.py:62
  114.6 6.1 %fusion = f32[192,512]{1,0:T(8,128)S(1)} fusion(bf16[8192,512]{1,0:T(8,128)(2,1)} %param.8, bf16[48,8192]{1,0:T(8,128)(2,1)} %collective-permute-done.6, bf16[48,8192]{1,0:T(8,128)(2,1)} %collective-permute-done.5, bf16[48,8192]{1,0:T(8,128)(2,1)} %collective-permute-done.4, bf16[48,8192]{1,0:T(8,128)(2,1)} %collective-permute-done.3), kind=kOutput, calls=%fused_computation.5 | convolution fusion | flops 1623195648 | bytes 11927552 | tf_op jit(solution)/shard_map/dot_general | solution.py:150
  122.5 3.1 %collective-permute-done.7 = bf16[48,8192]{1,0:T(8,128)(2,1)S(1)} collective-permute-done((bf16[48,8192]{1,0:T(8,128)(2,1)}, bf16[48,8192]{1,0:T(8,128)(2,1)S(1)}, u32[]{:S(2)}, u32[]{:S(2)}) %collective-permute-start.7) | collective-permute-done | bytes 786464 | tf_op jit(solution)/shard_map/ppermute | solution.py:62
  125.5 2.8 %collective-permute-done.8 = bf16[48,8192]{1,0:T(8,128)(2,1)} collective-permute-done((bf16[48,8192]{1,0:T(8,128)(2,1)}, bf16[48,8192]{1,0:T(8,128)(2,1)}, u32[]{:S(2)}, u32[]{:S(2)}) %collective-permute-start.8) | collective-permute-done | bytes 786464 | tf_op jit(solution)/shard_map/ppermute | solution.py:62
  128.3 12.3 %collective-permute-done.9 = bf16[48,8192]{1,0:T(8,128)(2,1)} collective-permute-done((bf16[48,8192]{1,0:T(8,128)(2,1)}, bf16[48,8192]{1,0:T(8,128)(2,1)}, u32[]{:S(2)}, u32[]{:S(2)}) %collective-permute-start.9) | collective-permute-done | bytes 786464 | tf_op jit(solution)/shard_map/ppermute | solution.py:62
  140.6 2.4 %collective-permute-done.10 = bf16[48,8192]{1,0:T(8,128)(2,1)} collective-permute-done((bf16[48,8192]{1,0:T(8,128)(2,1)}, bf16[48,8192]{1,0:T(8,128)(2,1)}, u32[]{:S(2)}, u32[]{:S(2)}) %collective-permute-start.10) | collective-permute-done | bytes 786464 | tf_op jit(solution)/shard_map/ppermute | solution.py:62
  148.3 5.9 %fusion.8 = f32[192,512]{1,0:T(8,128)S(1)} fusion(bf16[8192,512]{1,0:T(8,128)(2,1)} %param.8, bf16[48,8192]{1,0:T(8,128)(2,1)} %collective-permute-done.10, bf16[48,8192]{1,0:T(8,128)(2,1)} %collective-permute-done.9, bf16[48,8192]{1,0:T(8,128)(2,1)} %collective-permute-done.8, bf16[48,8192]{1,0:T(8,128)(2,1)S(1)} %collective-permute-done.7), kind=kOutput, calls=%fused_computation.13 | convolution fusion | flops 1623195648 | bytes 11927552 | tf_op jit(solution)/shard_map/dot_general | solution.py:150
  154.2 4.7 %collective-permute-start.16 = (f32[768,64]{1,0:T(8,128)S(1)}, f32[768,64]{1,0:T(8,128)S(1)}, u32[]{:S(2)}, u32[]{:S(2)}) collective-permute-start(f32[768,64]{1,0:T(8,128)S(1)} %add.180), channel_id=1, source_target_pairs={{0,4},{1,5},{2,6},{3,7},{4,0},{5,1},{6,2},{7,3},{8,12},{9,13},{10,... | collective-permute-start | bytes 589832 | tf_op jit(solution)/shard_map/ppermute | solution.py:62
  159.6 31.8 %collective-permute-done.16 = f32[768,64]{1,0:T(8,128)S(1)} collective-permute-done((f32[768,64]{1,0:T(8,128)S(1)}, f32[768,64]{1,0:T(8,128)S(1)}, u32[]{:S(2)}, u32[]{:S(2)}) %collective-permute-start.16) | collective-permute-done | bytes 196640 | tf_op jit(solution)/shard_map/ppermute | solution.py:62
  195.1 20.2 %collective-permute-done.19 = f32[768,64]{1,0:T(8,128)S(1)} collective-permute-done((f32[768,64]{1,0:T(8,128)S(1)}, f32[768,64]{1,0:T(8,128)S(1)}, u32[]{:S(2)}, u32[]{:S(2)}) %collective-permute-start.19) | collective-permute-done | bytes 196640 | tf_op jit(solution)/shard_map/ppermute | solution.py:62
  216.3 7.3 %collective-permute-done.20 = f32[768,64]{1,0:T(8,128)S(1)} collective-permute-done((f32[768,64]{1,0:T(8,128)S(1)}, f32[768,64]{1,0:T(8,128)S(1)}, u32[]{:S(2)}, u32[]{:S(2)}) %collective-permute-start.20) | collective-permute-done | bytes 196640 | tf_op jit(solution)/shard_map/ppermute | solution.py:62
  (131 shorter events, 37.5 us)
Async XLA Ops:
  5.1 34.5 %all-to-all-start.1 = ((bf16[16,128,512]{2,1,0:T(8,128)(2,1)}), bf16[16,128,512]{2,1,0:T(8,128)(2,1)S(1)}, u32[]{:S(2)}, u32[]{:S(2)}) async-start(bf16[16,128,512]{2,1,0:T(8,128)(2,1)} %broadcast_select_fusion), calls=%async_computation.1 | async-start | bytes 4194304 | tf_op jit(solution)/shard_map/all_to_all | solution.py:42
  11.1 43.5 %collective-permute-start = (bf16[48,8192]{1,0:T(8,128)(2,1)S(1)}, bf16[48,8192]{1,0:T(8,128)(2,1)}, u32[]{:S(2)}, u32[]{:S(2)}) collective-permute-start(bf16[48,8192]{1,0:T(8,128)(2,1)S(1)} %copy-done.2), channel_id=1, source_target_pairs={{0,8},{1,9},{2,10},{3,11},{4,12},{5,13},{6,14},{7,15},{8,0},{9,1},... | collective-permute-start | bytes 2359304 | tf_op jit(solution)/shard_map/ppermute | solution.py:62
  14.1 40.5 %collective-permute-start.1 = (bf16[48,8192]{1,0:T(8,128)(2,1)S(1)}, bf16[48,8192]{1,0:T(8,128)(2,1)}, u32[]{:S(2)}, u32[]{:S(2)}) collective-permute-start(bf16[48,8192]{1,0:T(8,128)(2,1)S(1)} %copy-done.2), channel_id=1, source_target_pairs={{0,7},{1,0},{2,1},{3,2},{4,3},{5,4},{6,5},{7,6},{8,15},{9,8},{10,9... | collective-permute-start | bytes 2359304 | tf_op jit(solution)/shard_map/ppermute | solution.py:62
  20.0 34.7 %collective-permute-start.2 = (bf16[48,8192]{1,0:T(8,128)(2,1)S(1)}, bf16[48,8192]{1,0:T(8,128)(2,1)}, u32[]{:S(2)}, u32[]{:S(2)}) collective-permute-start(bf16[48,8192]{1,0:T(8,128)(2,1)S(1)} %copy-done.2), channel_id=1, source_target_pairs={{0,1},{1,2},{2,3},{3,4},{4,5},{5,6},{6,7},{7,0},{8,9},{9,10},{10,1... | collective-permute-start | bytes 2359304 | tf_op jit(solution)/shard_map/ppermute | solution.py:62
  39.7 35.4 %all-to-all-start = ((bf16[48,16,512]{2,0,1:T(8,128)(2,1)}), bf16[48,16,512]{2,0,1:T(8,128)(2,1)}, u32[]{:S(2)}, u32[]{:S(2)}) async-start(bf16[48,16,512]{2,0,1:T(8,128)(2,1)} %bitcast.209), calls=%async_computation | async-start | bytes 1572864 | tf_op jit(solution)/shard_map/all_to_all | solution.py:69
  54.6 50.3 %collective-permute-start.5 = (bf16[48,8192]{1,0:T(8,128)(2,1)}, bf16[48,8192]{1,0:T(8,128)(2,1)}, u32[]{:S(2)}, u32[]{:S(2)}) collective-permute-start(bf16[48,8192]{1,0:T(8,128)(2,1)} %collective-permute-done), channel_id=1, source_target_pairs={{0,7},{1,0},{2,1},{3,2},{4,3},{5,4},{6,5},{7,6},{8,15},{9,8},{10,9... | collective-permute-start | bytes 2359304 | tf_op jit(solution)/shard_map/ppermute | solution.py:62
  61.8 43.1 %collective-permute-start.6 = (bf16[48,8192]{1,0:T(8,128)(2,1)}, bf16[48,8192]{1,0:T(8,128)(2,1)}, u32[]{:S(2)}, u32[]{:S(2)}) collective-permute-start(bf16[48,8192]{1,0:T(8,128)(2,1)} %collective-permute-done), channel_id=1, source_target_pairs={{0,1},{1,2},{2,3},{3,4},{4,5},{5,6},{6,7},{7,0},{8,9},{9,10},{10,1... | collective-permute-start | bytes 2359304 | tf_op jit(solution)/shard_map/ppermute | solution.py:62
  61.8 41.9 %collective-permute-start.3 = (bf16[48,8192]{1,0:T(8,128)(2,1)}, bf16[48,8192]{1,0:T(8,128)(2,1)}, u32[]{:S(2)}, u32[]{:S(2)}) collective-permute-start(bf16[48,8192]{1,0:T(8,128)(2,1)} %collective-permute-done.1), channel_id=1, source_target_pairs={{0,7},{1,0},{2,1},{3,2},{4,3},{5,4},{6,5},{7,6},{8,15},{9,8},{10,9... | collective-permute-start | bytes 2359304 | tf_op jit(solution)/shard_map/ppermute | solution.py:62
  65.1 39.8 %collective-permute-start.4 = (bf16[48,8192]{1,0:T(8,128)(2,1)}, bf16[48,8192]{1,0:T(8,128)(2,1)}, u32[]{:S(2)}, u32[]{:S(2)}) collective-permute-start(bf16[48,8192]{1,0:T(8,128)(2,1)} %collective-permute-done.2), channel_id=1, source_target_pairs={{0,1},{1,2},{2,3},{3,4},{4,5},{5,6},{6,7},{7,0},{8,9},{9,10},{10,1... | collective-permute-start | bytes 2359304 | tf_op jit(solution)/shard_map/ppermute | solution.py:62
  104.9 20.6 %collective-permute-start.7 = (bf16[48,8192]{1,0:T(8,128)(2,1)}, bf16[48,8192]{1,0:T(8,128)(2,1)S(1)}, u32[]{:S(2)}, u32[]{:S(2)}) collective-permute-start(bf16[48,8192]{1,0:T(8,128)(2,1)} %collective-permute-done.3), channel_id=1, source_target_pairs={{0,7},{1,0},{2,1},{3,2},{4,3},{5,4},{6,5},{7,6},{8,15},{9,8},{10,9... | collective-permute-start | bytes 2359304 | tf_op jit(solution)/shard_map/ppermute | solution.py:62
  106.4 21.9 %collective-permute-start.8 = (bf16[48,8192]{1,0:T(8,128)(2,1)}, bf16[48,8192]{1,0:T(8,128)(2,1)}, u32[]{:S(2)}, u32[]{:S(2)}) collective-permute-start(bf16[48,8192]{1,0:T(8,128)(2,1)} %collective-permute-done.4), channel_id=1, source_target_pairs={{0,1},{1,2},{2,3},{3,4},{4,5},{5,6},{6,7},{7,0},{8,9},{9,10},{10,1... | collective-permute-start | bytes 2359304 | tf_op jit(solution)/shard_map/ppermute | solution.py:62
  106.9 33.7 %collective-permute-start.9 = (bf16[48,8192]{1,0:T(8,128)(2,1)}, bf16[48,8192]{1,0:T(8,128)(2,1)}, u32[]{:S(2)}, u32[]{:S(2)}) collective-permute-start(bf16[48,8192]{1,0:T(8,128)(2,1)} %collective-permute-done.5), channel_id=1, source_target_pairs={{0,7},{1,0},{2,1},{3,2},{4,3},{5,4},{6,5},{7,6},{8,15},{9,8},{10,9... | collective-permute-start | bytes 2359304 | tf_op jit(solution)/shard_map/ppermute | solution.py:62
  109.6 33.4 %collective-permute-start.10 = (bf16[48,8192]{1,0:T(8,128)(2,1)}, bf16[48,8192]{1,0:T(8,128)(2,1)}, u32[]{:S(2)}, u32[]{:S(2)}) collective-permute-start(bf16[48,8192]{1,0:T(8,128)(2,1)} %collective-permute-done.6), channel_id=1, source_target_pairs={{0,1},{1,2},{2,3},{3,4},{4,5},{5,6},{6,7},{7,0},{8,9},{9,10},{10,1... | collective-permute-start | bytes 2359304 | tf_op jit(solution)/shard_map/ppermute | solution.py:62
  111.5 10.9 %collective-permute-start.11 = (f32[768,64]{1,0:T(8,128)S(1)}, f32[768,64]{1,0:T(8,128)S(1)}, u32[]{:S(2)}, u32[]{:S(2)}) collective-permute-start(f32[768,64]{1,0:T(8,128)S(1)} %copy.45), channel_id=1, source_target_pairs={{0,8},{1,9},{2,10},{3,11},{4,12},{5,13},{6,14},{7,15},{8,0},{9,1},... | collective-permute-start | bytes 589832 | tf_op jit(solution)/shard_map/ppermute | solution.py:62
  143.0 50.7 %slice-start = ((s8[8388608]{0:T(1024)(128)(4,1)}), s8[4194304]{0:T(1024)(128)(4,1)S(1)}, s32[]{:S(2)}) async-start(s8[8388608]{0:T(1024)(128)(4,1)} %bitcast.206), calls=%async_computation.2 | async-start | bytes 8388608
  143.1 48.3 %collective-permute-start.12 = (bf16[24,8192]{1,0:T(8,128)(2,1)S(1)}, bf16[24,8192]{1,0:T(8,128)(2,1)S(1)}, u32[]{:S(2)}, u32[]{:S(2)}) collective-permute-start(bf16[24,8192]{1,0:T(8,128)(2,1)S(1)} %slice.112), channel_id=1, source_target_pairs={{0,7},{1,0},{2,1},{3,2},{4,3},{5,4},{6,5},{7,6},{8,15},{9,8},{10,9... | collective-permute-start | bytes 1179656 | tf_op jit(solution)/shard_map/ppermute | solution.py:62
  144.8 46.6 %collective-permute-start.13 = (bf16[24,8192]{1,0:T(8,128)(2,1)S(1)}, bf16[24,8192]{1,0:T(8,128)(2,1)S(1)}, u32[]{:S(2)}, u32[]{:S(2)}) collective-permute-start(bf16[24,8192]{1,0:T(8,128)(2,1)S(1)} %slice.113), channel_id=1, source_target_pairs={{0,1},{1,2},{2,3},{3,4},{4,5},{5,6},{6,7},{7,0},{8,9},{9,10},{10,1... | collective-permute-start | bytes 1179656 | tf_op jit(solution)/shard_map/ppermute | solution.py:62
  146.3 45.1 %collective-permute-start.14 = (bf16[48,8192]{1,0:T(8,128)(2,1)}, bf16[48,8192]{1,0:T(8,128)(2,1)S(1)}, u32[]{:S(2)}, u32[]{:S(2)}) collective-permute-start(bf16[48,8192]{1,0:T(8,128)(2,1)} %collective-permute-done.9), channel_id=1, source_target_pairs={{0,7},{1,0},{2,1},{3,2},{4,3},{5,4},{6,5},{7,6},{8,15},{9,8},{10,9... | collective-permute-start | bytes 2359304 | tf_op jit(solution)/shard_map/ppermute | solution.py:62
  148.1 43.3 %collective-permute-start.15 = (bf16[48,8192]{1,0:T(8,128)(2,1)}, bf16[48,8192]{1,0:T(8,128)(2,1)S(1)}, u32[]{:S(2)}, u32[]{:S(2)}) collective-permute-start(bf16[48,8192]{1,0:T(8,128)(2,1)} %collective-permute-done.10), channel_id=1, source_target_pairs={{0,1},{1,2},{2,3},{3,4},{4,5},{5,6},{6,7},{7,0},{8,9},{9,10},{10,1... | collective-permute-start | bytes 2359304 | tf_op jit(solution)/shard_map/ppermute | solution.py:62
  154.2 37.1 %collective-permute-start.16 = (f32[768,64]{1,0:T(8,128)S(1)}, f32[768,64]{1,0:T(8,128)S(1)}, u32[]{:S(2)}, u32[]{:S(2)}) collective-permute-start(f32[768,64]{1,0:T(8,128)S(1)} %add.180), channel_id=1, source_target_pairs={{0,4},{1,5},{2,6},{3,7},{4,0},{5,1},{6,2},{7,3},{8,12},{9,13},{10,... | collective-permute-start | bytes 589832 | tf_op jit(solution)/shard_map/ppermute | solution.py:62
  191.5 32.2 %collective-permute-start.17 = (bf16[24,8192]{1,0:T(8,128)(2,1)S(1)}, bf16[24,8192]{1,0:T(8,128)(2,1)S(1)}, u32[]{:S(2)}, u32[]{:S(2)}) collective-permute-start(bf16[24,8192]{1,0:T(8,128)(2,1)S(1)} %slice.122), channel_id=1, source_target_pairs={{0,7},{1,0},{2,1},{3,2},{4,3},{5,4},{6,5},{7,6},{8,15},{9,8},{10,9... | collective-permute-start | bytes 1179656 | tf_op jit(solution)/shard_map/ppermute | solution.py:62
  191.6 32.1 %collective-permute-start.18 = (bf16[24,8192]{1,0:T(8,128)(2,1)S(1)}, bf16[24,8192]{1,0:T(8,128)(2,1)S(1)}, u32[]{:S(2)}, u32[]{:S(2)}) collective-permute-start(bf16[24,8192]{1,0:T(8,128)(2,1)S(1)} %slice.123), channel_id=1, source_target_pairs={{0,1},{1,2},{2,3},{3,4},{4,5},{5,6},{6,7},{7,0},{8,9},{9,10},{10,1... | collective-permute-start | bytes 1179656 | tf_op jit(solution)/shard_map/ppermute | solution.py:62
  193.7 21.6 %collective-permute-start.19 = (f32[768,64]{1,0:T(8,128)S(1)}, f32[768,64]{1,0:T(8,128)S(1)}, u32[]{:S(2)}, u32[]{:S(2)}) collective-permute-start(f32[768,64]{1,0:T(8,128)S(1)} %add.181), channel_id=1, source_target_pairs={{0,2},{1,3},{2,0},{3,1},{4,6},{5,7},{6,4},{7,5},{8,10},{9,11},{10,... | collective-permute-start | bytes 589832 | tf_op jit(solution)/shard_map/ppermute | solution.py:62
  215.3 8.3 %collective-permute-start.20 = (f32[768,64]{1,0:T(8,128)S(1)}, f32[768,64]{1,0:T(8,128)S(1)}, u32[]{:S(2)}, u32[]{:S(2)}) collective-permute-start(f32[768,64]{1,0:T(8,128)S(1)} %add.182), channel_id=1, source_target_pairs={{0,1},{1,0},{2,3},{3,2},{4,5},{5,4},{6,7},{7,6},{8,9},{9,8},{10,11... | collective-permute-start | bytes 589832 | tf_op jit(solution)/shard_map/ppermute | solution.py:62
  (7 other events, 89.7 us)
